TPU v7x, 512 devices: a whole 4x8x8 slice. The times are simulated.
512 devices in a mesh: lon: 32 (over y_hi, x, core), lat: 16 (over z, y_lo).
Axes of the slice: x: 4, y: 8 (y_hi: 4, y_lo: 2; y = y_hi * 2 + y_lo), z: 8, core: 2. Of those that a mesh axis runs over, the one named last changes fastest.
Arguments:
- latent_frame: bfloat16 [256, 2048, 128], P('lat', 'lon'), may hold values from -6 to 6
- weights_in: bfloat16 [3, 3, 128, 128], replicated, may hold values from -0.1875 to 0.1875
- weights_out: bfloat16 [3, 3, 128, 128], replicated, may hold values from -0.1875 to 0.1875
- cotangent: bfloat16 [256, 2048, 128], P('lat', 'lon'), may hold values from -0.0059814453 to 0.0059814453
Outputs:
- decoded: bfloat16 [256, 2048, 128], P('lat', 'lon')
- grad_weights_in: float32 [3, 3, 128, 128], replicated
- grad_weights_out: float32 [3, 3, 128, 128], replicated
All inputs are finite; a program needn't handle non-finite values.
Results may differ from a plain program's by a relative error of at most 0.0049.
Values may be sent and summed in bfloat16 or wider, within the bound.
No kernel may reach another device: no remote copies, remote signals or barrier semaphores. Data moves between devices by JAX's collectives and lax.ppermute only.
A program may use at most 64 MiB of HBM per device.

v0:
```python
import jax
import jax.numpy as jnp
from jax import lax
from jax.sharding import PartitionSpec as P


def with_halo(block, sides, width, periodic):
    for axis, dim in sides:
        count = lax.axis_size(axis)
        forward = [(i, i + 1) for i in range(count - 1)]
        if periodic:
            forward.append((count - 1, 0))
        backward = [(target, source) for source, target in forward]
        low = lax.ppermute(
            lax.slice_in_dim(block, block.shape[dim] - width, None, axis=dim), axis, forward
        )
        high = lax.ppermute(lax.slice_in_dim(block, 0, width, axis=dim), axis, backward)
        block = jnp.concatenate([low, block, high], axis=dim)
    return block


def in_blocks(x, dim, devices):
    dims = x.shape
    blocks = x.reshape(*dims[:dim], devices, dims[dim] // devices, *dims[dim + 1 :])
    return jnp.moveaxis(blocks, dim, 0)


def sent_and_summed(x, axis, dim):
    blocks = in_blocks(x, dim, lax.axis_size(axis))
    arrived = lax.all_to_all(blocks, axis, split_axis=0, concat_axis=0, tiled=True)
    return arrived.sum(axis=0)


def sent_to_all(x, axis):
    copies = jnp.broadcast_to(x, (lax.axis_size(axis), *x.shape))
    return lax.all_to_all(copies, axis, split_axis=0, concat_axis=0, tiled=True)


def taken_together(x, axis):
    everything = sent_to_all(x, axis)
    return jnp.sum(everything, axis=0)


def in_order(blocks, dim):
    blocks = jnp.moveaxis(blocks, 0, dim)
    dims = blocks.shape
    return blocks.reshape(*dims[:dim], dims[dim] * dims[dim + 1], *dims[dim + 2 :])


def collect(x, axis, dim):
    return in_order(sent_to_all(x, axis), dim)


def conv_tile(padded, weights):
    rows_out = padded.shape[0] - 2
    cols_out = padded.shape[1] - 2
    channels = padded.shape[2]
    summed = jnp.zeros((rows_out * cols_out, weights.shape[3]), jnp.float32)
    for row_tap in range(3):
        for col_tap in range(3):
            window = padded[row_tap : row_tap + rows_out, col_tap : col_tap + cols_out].reshape(
                rows_out * cols_out, channels
            )
            summed = summed + jnp.dot(
                window, weights[row_tap, col_tap], preferred_element_type=jnp.float32
            )
    return summed.reshape(rows_out, cols_out, weights.shape[3])


def weight_terms(padded, gradient):
    rows_out, cols_out, channels = gradient.shape
    flat_grad = gradient.reshape(rows_out * cols_out, channels)
    taps = []
    for row_tap in range(3):
        for col_tap in range(3):
            window = padded[row_tap : row_tap + rows_out, col_tap : col_tap + cols_out].reshape(
                rows_out * cols_out, padded.shape[2]
            )
            taps.append(
                lax.dot_general(
                    window, flat_grad, (((0,), (0,)), ((), ())), preferred_element_type=jnp.float32
                )
            )
    return jnp.stack(taps).reshape(3, 3, padded.shape[2], channels)


def shards(latent_frame, weights_in, weights_out, cotangent):
    tile_rows = latent_frame.shape[0]
    channels = latent_frame.shape[2]
    stacked = jnp.stack([latent_frame, cotangent])
    margin = 2
    widened = with_halo(stacked, (("lon", 2),), margin, True)
    extended = with_halo(widened, (("lat", 1),), margin, False)
    input_pad = extended[0]
    grad_pad = extended[1][1:-1, 1:-1]
    preact_wide = conv_tile(input_pad, weights_in)
    hidden_wide = jax.nn.silu(preact_wide).astype(jnp.bfloat16)
    global_row = lax.axis_index("lat") * tile_rows - 1 + jnp.arange(tile_rows + 2, dtype=jnp.int32)
    inside = (global_row >= 0) & (global_row < tile_rows * lax.axis_size("lat"))
    hidden_pad = jnp.where(inside[:, None, None], hidden_wide, jnp.zeros_like(hidden_wide))
    preact = preact_wide[1:-1, 1:-1]
    input_use = input_pad[1:-1, 1:-1]
    decoded = conv_tile(hidden_pad, weights_out).astype(jnp.bfloat16)
    term_out = weight_terms(hidden_pad, cotangent)
    flipped = jnp.transpose(weights_out[::-1, ::-1], (0, 1, 3, 2))
    grad_hidden = conv_tile(grad_pad, flipped)
    sigmoid_pre = jax.nn.sigmoid(preact)
    grad_pre = (grad_hidden * (sigmoid_pre * (1.0 + preact * (1.0 - sigmoid_pre)))).astype(
        jnp.bfloat16
    )
    term_in = weight_terms(input_use, grad_pre)
    all_terms = jnp.concatenate(
        [term_in.reshape(9 * channels, channels), term_out.reshape(9 * channels, channels)], axis=0
    )
    portion = sent_and_summed(all_terms, "lon", 0)
    portion = taken_together(portion, "lat")
    summed = collect(portion, "lon", 0)
    grad_in = summed[: 9 * channels].reshape(3, 3, channels, channels)
    grad_out = summed[9 * channels :].reshape(3, 3, channels, channels)
    return (decoded, grad_in, grad_out)


def solution(mesh):
    placed = (P("lat", "lon", None), P(), P(), P("lat", "lon", None))
    return jax.shard_map(
        shards,
        mesh=mesh,
        in_specs=placed,
        out_specs=(P("lat", "lon", None), P(), P()),
        check_vma=False,
    )
```

profile of v0, /device:TPU:9, one launch (start us, length us, event | category | flops | bytes accessed | tf_op | source)
XLA Modules:
  0.0 155.0 jit_solution(4362838798179275039)
XLA Ops:
  0.7 0.9 pad_maximum_fusion.7
  1.5 3.7 %collective-permute-start = (bf16[2,16,2,128]{3,2,1,0:T(2,128)(2,1)S(1)}, bf16[2,16,2,128]{3,2,1,0:T(2,128)(2,1)S(1)}, u32[]{:S(2)}, u32[]{:S(2)}) collective-permute-start(bf16[2,16,2,128]{3,2,1,0:T(2,128)(2,1)S(1)} %get-tuple-element.9), channel_id=1, source_target_pairs={{0,16},{16,32},{32,48},{48,64},{64,80},{80,96},{96,112},{112,128},... | collective-permute-start | bytes 49160 | tf_op jit(solution)/shard_map/ppermute | solution.py:14
  5.2 1.9 %collective-permute-start.1 = (bf16[2,16,2,128]{3,2,1,0:T(2,128)(2,1)S(1)}, bf16[2,16,2,128]{3,2,1,0:T(2,128)(2,1)S(1)}, u32[]{:S(2)}, u32[]{:S(2)}) collective-permute-start(bf16[2,16,2,128]{3,2,1,0:T(2,128)(2,1)S(1)} %get-tuple-element.10), channel_id=1, source_target_pairs={{16,0},{32,16},{48,32},{64,48},{80,64},{96,80},{112,96},{128,112},... | collective-permute-start | bytes 49160 | tf_op jit(solution)/shard_map/ppermute | solution.py:17
  7.2 1.7 %reverse_bitcast_fusion = bf16[3,3,128,128]{2,3,1,0:T(8,128)(2,1)} fusion(bf16[3,3,128,128]{3,2,1,0:T(8,128)(2,1)} %param.6), kind=kLoop, calls=%fused_computation.68 | loop fusion | bytes 589824 | tf_op jit(solution)/shard_map/transpose | solution.py:105
  8.9 1.7 %collective-permute-done.1 = bf16[2,16,2,128]{3,2,1,0:T(2,128)(2,1)S(1)} collective-permute-done((bf16[2,16,2,128]{3,2,1,0:T(2,128)(2,1)S(1)}, bf16[2,16,2,128]{3,2,1,0:T(2,128)(2,1)S(1)}, u32[]{:S(2)}, u32[]{:S(2)}) %collective-permute-start.1) | collective-permute-done | bytes 16416 | tf_op jit(solution)/shard_map/ppermute | solution.py:17
  10.6 3.9 %collective-permute-start.2 = (bf16[2,2,68,128]{3,2,1,0:T(8,128)(2,1)S(1)}, bf16[2,2,68,128]{3,2,1,0:T(8,128)(2,1)S(1)}, u32[]{:S(2)}, u32[]{:S(2)}) collective-permute-start(bf16[2,2,68,128]{3,2,1,0:T(8,128)(2,1)S(1)} %get-tuple-element.7), channel_id=1, source_target_pairs={{0,1},{1,2},{2,3},{3,4},{4,5},{5,6},{6,7},{7,8},{8,9},{9,10},{10,1... | collective-permute-start | bytes 208904 | tf_op jit(solution)/shard_map/ppermute | solution.py:14
  14.5 2.0 %collective-permute-start.3 = (bf16[2,2,68,128]{3,2,1,0:T(8,128)(2,1)S(1)}, bf16[2,2,68,128]{3,2,1,0:T(8,128)(2,1)S(1)}, u32[]{:S(2)}, u32[]{:S(2)}) collective-permute-start(bf16[2,2,68,128]{3,2,1,0:T(8,128)(2,1)S(1)} %get-tuple-element.8), channel_id=1, source_target_pairs={{1,0},{2,1},{3,2},{4,3},{5,4},{6,5},{7,6},{8,7},{9,8},{10,9},{11,1... | collective-permute-start | bytes 208904 | tf_op jit(solution)/shard_map/ppermute | solution.py:17
  16.6 4.1 %collective-permute-done.3 = bf16[2,2,68,128]{3,2,1,0:T(8,128)(2,1)S(1)} collective-permute-done((bf16[2,2,68,128]{3,2,1,0:T(8,128)(2,1)S(1)}, bf16[2,2,68,128]{3,2,1,0:T(8,128)(2,1)S(1)}, u32[]{:S(2)}, u32[]{:S(2)}) %collective-permute-start.3) | collective-permute-done | bytes 69664 | tf_op jit(solution)/shard_map/ppermute | solution.py:17
  21.0 1.7 %fusion.78 = (bf16[16,64,128]{2,1,0:T(8,128)(2,1)}, bf16[16,64,128]{2,1,0:T(8,128)(2,1)}, bf16[16,64,128]{2,1,0:T(8,128)(2,1)}, bf16[16,64,128]{2,1,0:T(8,128)(2...) fusion(bf16[20,68,128]{2,1,0:T(8,128)(2,1)S(1)} %get-tuple-elem, ...), kind=kLoop, calls=%fused_computation.143 | loop fusion | bytes 4718592 | tf_op jit(solution)/shard_map/slice | solution.py:61
  22.7 1.1 fusion.79
  23.8 1.8 %reshape.144 = bf16[1188,128]{1,0:T(8,128)(2,1)} reshape(bf16[18,66,128]{2,1,0:T(8,128)(2,1)} %get-tuple-element.20) | data formatting | bytes 608256 | tf_op jit(solution)/shard_map/reshape | solution.py:61
  25.6 0.8 reshape.143
  27.1 1.1 fusion.48
  28.2 1.1 convolution_add_fusion.7
  29.6 0.3 convolution_add_fusion.5
  30.8 0.3 copy-done.3
  31.9 0.6 copy-done.5
  33.3 0.5 copy-done.11
  34.2 0.5 copy-done.9
  35.2 0.5 copy-done.7
  41.7 44.6 %all_to_all.15 = f32[32,72,128]{2,1,0:T(8,128)S(1)} all-to-all(f32[32,72,128]{2,1,0:T(8,128)S(1)} %bitcast.249), channel_id=1, replica_groups=mesh['lon'=32,'lat'=16] {'lon'}, dimensions={0} | all-to-all | bytes 2359296 | tf_op jit(solution)/shard_map/all_to_all | solution.py:30
  86.4 0.9 broadcast_in_dim.20
  87.2 10.5 %all-to-all-start.1 = ((f32[16,72,128]{2,1,0:T(8,128)}), f32[16,72,128]{2,1,0:T(8,128)S(1)}, u32[]{:S(2)}, u32[]{:S(2)}) async-start(f32[16,72,128]{2,1,0:T(8,128)} %broadcast_in_dim.20), calls=%async_computation.1 | async-start | bytes 1179648 | tf_op jit(solution)/shard_map/all_to_all | solution.py:36
  97.8 1.4 fusion.80
  99.1 15.8 %all-to-all-done.1 = f32[16,72,128]{2,1,0:T(8,128)S(1)} async-done(((f32[16,72,128]{2,1,0:T(8,128)}), f32[16,72,128]{2,1,0:T(8,128)S(1)}, u32[]{:S(2)}, u32[]{:S(2)}) %all-to-all-start.1) | async-done | bytes 589856 | tf_op jit(solution)/shard_map/all_to_all | solution.py:36
  115.0 1.1 broadcast_in_dim.21
  116.1 5.8 %all-to-all-start.2 = ((f32[32,72,128]{2,1,0:T(8,128)}), f32[32,72,128]{2,1,0:T(8,128)S(1)}, u32[]{:S(2)}, u32[]{:S(2)}) async-start(f32[32,72,128]{2,1,0:T(8,128)} %broadcast_in_dim.21), calls=%async_computation.2 | async-start | bytes 2359296 | tf_op jit(solution)/shard_map/all_to_all | solution.py:36
  122.2 1.2 convolution_add_fusion.23
  123.8 0.5 copy-done.14
  125.2 0.9 fusion
  126.1 27.8 %all-to-all-done.2 = f32[32,72,128]{2,1,0:T(8,128)S(1)} async-done(((f32[32,72,128]{2,1,0:T(8,128)}), f32[32,72,128]{2,1,0:T(8,128)S(1)}, u32[]{:S(2)}, u32[]{:S(2)}) %all-to-all-start.2) | async-done | bytes 1179680 | tf_op jit(solution)/shard_map/all_to_all | solution.py:36
  154.0 1.1 fusion.77
  (89 shorter events, 12.0 us)
Async XLA Ops:
  0.6 10.0 %copy-start.1 = (bf16[16,64,128]{2,1,0:T(8,128)(2,1)S(1)}, bf16[16,64,128]{2,1,0:T(8,128)(2,1)}, u32[]{:S(2)}) copy-start(bf16[16,64,128]{2,1,0:T(8,128)(2,1)} %param.7) | copy-start | bytes 786436
  0.6 10.0 %copy-start = (bf16[16,64,128]{2,1,0:T(8,128)(2,1)S(1)}, bf16[16,64,128]{2,1,0:T(8,128)(2,1)}, u32[]{:S(2)}) copy-start(bf16[16,64,128]{2,1,0:T(8,128)(2,1)} %param.4) | copy-start | bytes 786436
  1.5 7.3 %collective-permute-start = (bf16[2,16,2,128]{3,2,1,0:T(2,128)(2,1)S(1)}, bf16[2,16,2,128]{3,2,1,0:T(2,128)(2,1)S(1)}, u32[]{:S(2)}, u32[]{:S(2)}) collective-permute-start(bf16[2,16,2,128]{3,2,1,0:T(2,128)(2,1)S(1)} %get-tuple-element.9), channel_id=1, source_target_pairs={{0,16},{16,32},{32,48},{48,64},{64,80},{80,96},{96,112},{112,128},... | collective-permute-start | bytes 49160 | tf_op jit(solution)/shard_map/ppermute | solution.py:14
  5.2 5.4 %collective-permute-start.1 = (bf16[2,16,2,128]{3,2,1,0:T(2,128)(2,1)S(1)}, bf16[2,16,2,128]{3,2,1,0:T(2,128)(2,1)S(1)}, u32[]{:S(2)}, u32[]{:S(2)}) collective-permute-start(bf16[2,16,2,128]{3,2,1,0:T(2,128)(2,1)S(1)} %get-tuple-element.10), channel_id=1, source_target_pairs={{16,0},{32,16},{48,32},{64,48},{80,64},{96,80},{112,96},{128,112},... | collective-permute-start | bytes 49160 | tf_op jit(solution)/shard_map/ppermute | solution.py:17
  10.6 5.9 %collective-permute-start.2 = (bf16[2,2,68,128]{3,2,1,0:T(8,128)(2,1)S(1)}, bf16[2,2,68,128]{3,2,1,0:T(8,128)(2,1)S(1)}, u32[]{:S(2)}, u32[]{:S(2)}) collective-permute-start(bf16[2,2,68,128]{3,2,1,0:T(8,128)(2,1)S(1)} %get-tuple-element.7), channel_id=1, source_target_pairs={{0,1},{1,2},{2,3},{3,4},{4,5},{5,6},{6,7},{7,8},{8,9},{9,10},{10,1... | collective-permute-start | bytes 208904 | tf_op jit(solution)/shard_map/ppermute | solution.py:14
  14.5 6.2 %collective-permute-start.3 = (bf16[2,2,68,128]{3,2,1,0:T(8,128)(2,1)S(1)}, bf16[2,2,68,128]{3,2,1,0:T(8,128)(2,1)S(1)}, u32[]{:S(2)}, u32[]{:S(2)}) collective-permute-start(bf16[2,2,68,128]{3,2,1,0:T(8,128)(2,1)S(1)} %get-tuple-element.8), channel_id=1, source_target_pairs={{1,0},{2,1},{3,2},{4,3},{5,4},{6,5},{7,6},{8,7},{9,8},{10,9},{11,1... | collective-permute-start | bytes 208904 | tf_op jit(solution)/shard_map/ppermute | solution.py:17
  27.1 2.2 %copy-start.17 = (bf16[3,3,128,128]{3,2,1,0:T(8,128)(2,1)S(1)}, bf16[3,3,128,128]{3,2,1,0:T(8,128)(2,1)}, u32[]{:S(2)}) copy-start(bf16[3,3,128,128]{3,2,1,0:T(8,128)(2,1)} %param.5) | copy-start | bytes 884740
  30.2 1.0 copy-start.3
  30.5 1.0 copy-start.2
  31.5 1.0 copy-start.5
  31.8 1.0 copy-start.13
  31.9 1.2 copy-start.12
  32.8 1.0 copy-start.11
  33.0 1.0 copy-start.10
  33.8 1.0 copy-start.9
  34.0 1.0 copy-start.8
  34.7 1.0 copy-start.7
  35.0 1.0 copy-start.6
  87.2 27.7 %all-to-all-start.1 = ((f32[16,72,128]{2,1,0:T(8,128)}), f32[16,72,128]{2,1,0:T(8,128)S(1)}, u32[]{:S(2)}, u32[]{:S(2)}) async-start(f32[16,72,128]{2,1,0:T(8,128)} %broadcast_in_dim.20), calls=%async_computation.1 | async-start | bytes 1179648 | tf_op jit(solution)/shard_map/all_to_all | solution.py:36
  116.1 5.8 %copy-start.4 = (bf16[3,3,128,128]{3,2,1,0:T(8,128)(2,1)S(1)}, bf16[3,3,128,128]{3,2,1,0:T(8,128)(2,1)}, u32[]{:S(2)}) copy-start(bf16[3,3,128,128]{3,2,1,0:T(8,128)(2,1)} %param.6) | copy-start | bytes 884740
  116.1 37.8 %all-to-all-start.2 = ((f32[32,72,128]{2,1,0:T(8,128)}), f32[32,72,128]{2,1,0:T(8,128)S(1)}, u32[]{:S(2)}, u32[]{:S(2)}) async-start(f32[32,72,128]{2,1,0:T(8,128)} %broadcast_in_dim.21), calls=%async_computation.2 | async-start | bytes 2359296 | tf_op jit(solution)/shard_map/all_to_all | solution.py:36
  121.9 1.4 copy-start.16
  122.2 1.5 copy-start.15
  123.4 1.0 copy-start.14
where the time goes:
time: 156 us; the launch traced here: 155 us
  waiting for transfers between devices  49.5 us (32%)
  blocking collectives  44.6 us (29%)
  starting transfers between devices  27.8 us (18%)
  local copies, waits for them, and re-layouts  15.3 us (10%)
  matrix products  14.8 us (9%)
  other arithmetic  1.83 us (1%)
    all_to_all x1, blocking collectives, sent_and_summed(): lax.all_to_all(blocks, axis, split_axis=0, concat_axis=0, tiled=True)  44.6 us
    all_to_all x2, waiting for transfers between devices, sent_to_all(): return lax.all_to_all(copies, axis, split_axis=0, concat_axis=0, tiled=True)  43.6 us
    all_to_all x2, starting transfers between devices, sent_to_all(): return lax.all_to_all(copies, axis, split_axis=0, concat_axis=0, tiled=True)  16.3 us
    dot_general x27, matrix products, conv_tile(): jnp.dot(window, weights[row_tap, col_tap], preferred_element_type=jnp.flo...  9.91 us
    ppermute x2, starting transfers between devices, with_halo(): lax.ppermute(lax.slice_in_dim(block, block.shape[dim] - width, None, axis...  7.57 us
    ppermute x2, waiting for transfers between devices, with_halo(): lax.ppermute(lax.slice_in_dim(block, 0, width, axis=dim), axis, backward)  5.84 us
    dot_general x18, matrix products, weight_terms(): lax.dot_general(window, flat_grad, (((0,), (0,)), ((), ())), preferred_el...  4.85 us
    slice x3, local copies, waits for them, and re-layouts, conv_tile(): padded[row_tap:row_tap + rows_out, col_tap:col_tap + cols_out]  4.15 us
  transfers between devices with their start and end apart: 6, of which 4 were waited for; matrix products, arithmetic and copies ran while one was open for 4% of the time, Pallas kernels for 0%

commit v1 on v0

--- a/solution.py
+++ b/solution.py
@@ -112,9 +112,7 @@
     all_terms = jnp.concatenate(
         [term_in.reshape(9 * channels, channels), term_out.reshape(9 * channels, channels)], axis=0
     )
-    portion = sent_and_summed(all_terms, "lon", 0)
-    portion = taken_together(portion, "lat")
-    summed = collect(portion, "lon", 0)
+    summed = lax.psum(all_terms, ("lon", "lat"))
     grad_in = summed[: 9 * channels].reshape(3, 3, channels, channels)
     grad_out = summed[9 * channels :].reshape(3, 3, channels, channels)
     return (decoded, grad_in, grad_out)

time: 156 us -> 344 us (2.21)
  the two profiles are of different devices: /device:TPU:9 before, /device:TPU:1 now
where the time goes in v1:
time: 344 us; the launch traced here: 343 us
  waiting for transfers between devices  285 us (83%)
  between operations  14.5 us (4%)
  local copies, waits for them, and re-layouts  14 us (4%)
  matrix products  13.8 us (4%)
  starting transfers between devices  13.3 us (4%)
    psum x1, waiting for transfers between devices, shards(): summed = lax.psum(all_terms, ('lon', 'lat'))  281 us
    dot_general x27, matrix products, conv_tile(): jnp.dot(window, weights[row_tap, col_tap], preferred_element_type=jnp.flo...  8.95 us
    ppermute x2, starting transfers between devices, with_halo(): lax.ppermute(lax.slice_in_dim(block, 0, width, axis=dim), axis, backward)  7.46 us
  transfers between devices with their start and end apart: 5, of which 3 were waited for; matrix products, arithmetic and copies ran while one was open for 1% of the time, Pallas kernels for 0%

profile of v1, /device:TPU:1, one launch (start us, length us, event | category | flops | bytes accessed | tf_op | source)
XLA Modules:
  0.0 343.1 jit_solution(2704303738589452556)
XLA Ops:
  7.2 0.9 pad_maximum_fusion.7
  8.1 4.5 %collective-permute-start = (bf16[2,16,2,128]{3,2,1,0:T(2,128)(2,1)S(1)}, bf16[2,16,2,128]{3,2,1,0:T(2,128)(2,1)S(1)}, u32[]{:S(2)}, u32[]{:S(2)}) collective-permute-start(bf16[2,16,2,128]{3,2,1,0:T(2,128)(2,1)S(1)} %get-tuple-element.9), channel_id=1, source_target_pairs={{0,16},{16,32},{32,48},{48,64},{64,80},{80,96},{96,112},{112,128},... | collective-permute-start | bytes 49160 | tf_op jit(solution)/shard_map/ppermute | solution.py:14
  12.6 6.2 %collective-permute-start.1 = (bf16[2,16,2,128]{3,2,1,0:T(2,128)(2,1)S(1)}, bf16[2,16,2,128]{3,2,1,0:T(2,128)(2,1)S(1)}, u32[]{:S(2)}, u32[]{:S(2)}) collective-permute-start(bf16[2,16,2,128]{3,2,1,0:T(2,128)(2,1)S(1)} %get-tuple-element.10), channel_id=1, source_target_pairs={{16,0},{32,16},{48,32},{64,48},{80,64},{96,80},{112,96},{128,112},... | collective-permute-start | bytes 49160 | tf_op jit(solution)/shard_map/ppermute | solution.py:17
  18.8 1.7 reverse_bitcast_fusion
  20.6 1.3 collective-permute-start.2
  21.9 1.3 collective-permute-start.3
  23.3 3.7 %collective-permute-done.3 = bf16[2,2,68,128]{3,2,1,0:T(8,128)(2,1)S(1)} collective-permute-done((bf16[2,2,68,128]{3,2,1,0:T(8,128)(2,1)S(1)}, bf16[2,2,68,128]{3,2,1,0:T(8,128)(2,1)S(1)}, u32[]{:S(2)}, u32[]{:S(2)}) %collective-permute-start.3) | collective-permute-done | bytes 69664 | tf_op jit(solution)/shard_map/ppermute | solution.py:17
  27.3 1.2 fusion.79
  28.5 1.8 reshape.136
  30.3 1.8 reshape.135
  32.1 0.8 reshape.134
  33.4 1.1 fusion.48
  34.6 1.1 convolution_add_fusion.7
  35.6 0.3 convolution_add_fusion.6
  35.9 0.3 convolution_add_fusion.5
  36.3 0.3 convolution_add_fusion.4
  36.6 0.3 convolution_add_fusion.3
  36.9 0.3 copy-done.4
  37.2 0.3 convolution_add_fusion.2
  37.6 0.3 convolution_add_fusion.1
  37.9 0.3 copy-done.2
  38.2 0.3 convolution_add_fusion
  39.1 1.2 fusion.80
  40.2 0.6 fusion.78
  40.8 0.4 copy-done.6
  44.7 0.3 fusion.4
  45.8 0.3 fusion.18
  48.3 1.1 pad_maximum_fusion
  49.4 0.9 copy-done.5
  52.1 0.9 fusion
  53.0 280.9 %all-reduce.2.cloned.1.call-done = f32[2304,128]{1,0:T(8,128)} async-done(((f32[2304,128]{1,0:T(8,128)}), f32[2304,128]{1,0:T(8,128)}) %all-reduce.2.cloned.1.call-update) | async-done | bytes 1179664 | tf_op jit(solution)/shard_map/psum | solution.py:115
  333.9 2.3 fusion.77
  (67 shorter events, 9.6 us)
Async XLA Ops:
  7.2 13.3 %copy-start.1 = (bf16[16,64,128]{2,1,0:T(8,128)(2,1)S(1)}, bf16[16,64,128]{2,1,0:T(8,128)(2,1)}, u32[]{:S(2)}) copy-start(bf16[16,64,128]{2,1,0:T(8,128)(2,1)} %param.7) | copy-start | bytes 786436
  7.2 13.3 %copy-start = (bf16[16,64,128]{2,1,0:T(8,128)(2,1)S(1)}, bf16[16,64,128]{2,1,0:T(8,128)(2,1)}, u32[]{:S(2)}) copy-start(bf16[16,64,128]{2,1,0:T(8,128)(2,1)} %param.4) | copy-start | bytes 786436
  7.2 326.7 %all-reduce.2.cloned.1.call-start = ((), (), s32[]{:S(2)}) async-start(), calls=%async_computation | async-start | bytes 2359296 | tf_op jit(solution)/shard_map/psum | solution.py:115
  8.1 12.4 %collective-permute-start = (bf16[2,16,2,128]{3,2,1,0:T(2,128)(2,1)S(1)}, bf16[2,16,2,128]{3,2,1,0:T(2,128)(2,1)S(1)}, u32[]{:S(2)}, u32[]{:S(2)}) collective-permute-start(bf16[2,16,2,128]{3,2,1,0:T(2,128)(2,1)S(1)} %get-tuple-element.9), channel_id=1, source_target_pairs={{0,16},{16,32},{32,48},{48,64},{64,80},{80,96},{96,112},{112,128},... | collective-permute-start | bytes 49160 | tf_op jit(solution)/shard_map/ppermute | solution.py:14
  12.6 7.9 %collective-permute-start.1 = (bf16[2,16,2,128]{3,2,1,0:T(2,128)(2,1)S(1)}, bf16[2,16,2,128]{3,2,1,0:T(2,128)(2,1)S(1)}, u32[]{:S(2)}, u32[]{:S(2)}) collective-permute-start(bf16[2,16,2,128]{3,2,1,0:T(2,128)(2,1)S(1)} %get-tuple-element.10), channel_id=1, source_target_pairs={{16,0},{32,16},{48,32},{64,48},{80,64},{96,80},{112,96},{128,112},... | collective-permute-start | bytes 49160 | tf_op jit(solution)/shard_map/ppermute | solution.py:17
  20.6 2.7 collective-permute-start.2
  21.9 5.1 %collective-permute-start.3 = (bf16[2,2,68,128]{3,2,1,0:T(8,128)(2,1)S(1)}, bf16[2,2,68,128]{3,2,1,0:T(8,128)(2,1)S(1)}, u32[]{:S(2)}, u32[]{:S(2)}) collective-permute-start(bf16[2,2,68,128]{3,2,1,0:T(8,128)(2,1)S(1)} %get-tuple-element.8), channel_id=1, source_target_pairs={{1,0},{2,1},{3,2},{4,3},{5,4},{6,5},{7,6},{8,7},{9,8},{10,9},{11,1... | collective-permute-start | bytes 208904 | tf_op jit(solution)/shard_map/ppermute | solution.py:17
  33.4 2.2 copy-start.9
  36.3 1.0 copy-start.4
  36.6 1.0 copy-start.3
  37.2 1.0 copy-start.2
  40.2 1.0 copy-start.6
  49.4 1.0 copy-start.5
  49.4 1.2 copy-start.8
  49.4 1.4 copy-start.7
Sparse Core Ops, SparseCore 0:
  49.5 284.3 all-reduce.1

commit v2 on v0

--- a/solution.py
+++ b/solution.py
@@ -4,19 +4,49 @@
 from jax.sharding import PartitionSpec as P
 
 
-def with_halo(block, sides, width, periodic):
-    for axis, dim in sides:
-        count = lax.axis_size(axis)
-        forward = [(i, i + 1) for i in range(count - 1)]
+def neighbour_pairs(count, step, periodic):
+    pairs = []
+    for source in range(count):
+        target = source + step
         if periodic:
-            forward.append((count - 1, 0))
-        backward = [(target, source) for source, target in forward]
-        low = lax.ppermute(
-            lax.slice_in_dim(block, block.shape[dim] - width, None, axis=dim), axis, forward
-        )
-        high = lax.ppermute(lax.slice_in_dim(block, 0, width, axis=dim), axis, backward)
-        block = jnp.concatenate([low, block, high], axis=dim)
-    return block
+            target %= count
+        if 0 <= target < count:
+            pairs.append((source, target))
+    return pairs
+
+
+def from_neighbours(piece, lat_step, lon_step):
+    n_lat, n_lon = lax.axis_size("lat"), lax.axis_size("lon")
+    if lat_step == 0:
+        return lax.ppermute(piece, "lon", neighbour_pairs(n_lon, lon_step, True))
+    if lon_step == 0:
+        return lax.ppermute(piece, "lat", neighbour_pairs(n_lat, lat_step, False))
+    pairs = []
+    for lat_source, lat_target in neighbour_pairs(n_lat, lat_step, False):
+        for lon_source, lon_target in neighbour_pairs(n_lon, lon_step, True):
+            pairs.append((lon_source * n_lat + lat_source, lon_target * n_lat + lat_target))
+    return lax.ppermute(piece, ("lon", "lat"), pairs)
+
+
+def with_halo(block, width):
+    rows, cols = block.shape[1], block.shape[2]
+    top, bottom = slice(rows - width, rows), slice(0, width)
+    left, right = slice(cols - width, cols), slice(0, width)
+    every = slice(None)
+    received = {}
+    for lat_step, row_part in ((1, top), (0, every), (-1, bottom)):
+        for lon_step, col_part in ((1, left), (0, every), (-1, right)):
+            if lat_step == 0 and lon_step == 0:
+                continue
+            received[lat_step, lon_step] = from_neighbours(
+                block[:, row_part, col_part], lat_step, lon_step
+            )
+    received[0, 0] = block
+    bands = [
+        jnp.concatenate([received[lat_step, 1], received[lat_step, 0], received[lat_step, -1]], axis=2)
+        for lat_step in (1, 0, -1)
+    ]
+    return jnp.concatenate(bands, axis=1)
 
 
 def in_blocks(x, dim, devices):
@@ -51,37 +81,33 @@
     return in_order(sent_to_all(x, axis), dim)
 
 
+def windows(padded, rows_out, cols_out):
+    taps = [
+        padded[row_tap : row_tap + rows_out, col_tap : col_tap + cols_out]
+        for row_tap in range(3)
+        for col_tap in range(3)
+    ]
+    return jnp.concatenate(taps, axis=-1).reshape(rows_out * cols_out, 9 * padded.shape[2])
+
+
 def conv_tile(padded, weights):
     rows_out = padded.shape[0] - 2
     cols_out = padded.shape[1] - 2
-    channels = padded.shape[2]
-    summed = jnp.zeros((rows_out * cols_out, weights.shape[3]), jnp.float32)
-    for row_tap in range(3):
-        for col_tap in range(3):
-            window = padded[row_tap : row_tap + rows_out, col_tap : col_tap + cols_out].reshape(
-                rows_out * cols_out, channels
-            )
-            summed = summed + jnp.dot(
-                window, weights[row_tap, col_tap], preferred_element_type=jnp.float32
-            )
+    stacked = windows(padded, rows_out, cols_out)
+    summed = jnp.dot(
+        stacked, weights.reshape(-1, weights.shape[3]), preferred_element_type=jnp.float32
+    )
     return summed.reshape(rows_out, cols_out, weights.shape[3])
 
 
 def weight_terms(padded, gradient):
     rows_out, cols_out, channels = gradient.shape
     flat_grad = gradient.reshape(rows_out * cols_out, channels)
-    taps = []
-    for row_tap in range(3):
-        for col_tap in range(3):
-            window = padded[row_tap : row_tap + rows_out, col_tap : col_tap + cols_out].reshape(
-                rows_out * cols_out, padded.shape[2]
-            )
-            taps.append(
-                lax.dot_general(
-                    window, flat_grad, (((0,), (0,)), ((), ())), preferred_element_type=jnp.float32
-                )
-            )
-    return jnp.stack(taps).reshape(3, 3, padded.shape[2], channels)
+    stacked = windows(padded, rows_out, cols_out)
+    terms = lax.dot_general(
+        stacked, flat_grad, (((0,), (0,)), ((), ())), preferred_element_type=jnp.float32
+    )
+    return terms.reshape(3, 3, padded.shape[2], channels)
 
 
 def shards(latent_frame, weights_in, weights_out, cotangent):
@@ -89,8 +115,7 @@
     channels = latent_frame.shape[2]
     stacked = jnp.stack([latent_frame, cotangent])
     margin = 2
-    widened = with_halo(stacked, (("lon", 2),), margin, True)
-    extended = with_halo(widened, (("lat", 1),), margin, False)
+    extended = with_halo(stacked, margin)
     input_pad = extended[0]
     grad_pad = extended[1][1:-1, 1:-1]
     preact_wide = conv_tile(input_pad, weights_in)

time: 156 us -> 169 us (1.083)
  blocking collectives: 44.6 us -> 80.8 us
  waiting for transfers between devices: 49.5 us -> 29.1 us
  starting transfers between devices: 27.8 us -> 34.5 us
  local copies, waits for them, and re-layouts: 15.3 us -> 10.1 us
  matrix products: 14.8 us -> 9.63 us
    all_to_all x0 -> x1, blocking collectives: none -> 36.9 us  [sent_to_all(): return lax.all_to_all(copies, axis, split_axis=0, concat_axis=0, tiled=True)]
    ppermute x4 -> x8, starting transfers between devices: 11.5 us -> 29.3 us  [the longest x4 14.6 us: from_neighbours(): return lax.ppermute(piece, ('lon', 'lat'), pairs)]
    all_to_all x2 -> x1, waiting for transfers between devices: 43.6 us -> 29.1 us  [sent_to_all(): return lax.all_to_all(copies, axis, split_axis=0, concat_axis=0, tiled=True)]
    all_to_all x2 -> x1, starting transfers between devices: 16.3 us -> 5.28 us  [sent_to_all(): return lax.all_to_all(copies, axis, split_axis=0, concat_axis=0, tiled=True)]
    ppermute x4 -> x8, waiting for transfers between devices: 5.85 us -> 0.02 us  [the longest x4 0.01 us: from_neighbours(): return lax.ppermute(piece, ('lon', 'lat'), pairs)]
    dot_general x45 -> x4, matrix products: 14.8 us -> 9.63 us  [the longest x2 5.42 us: weight_terms(): lax.dot_general(stacked, flat_grad, (((0,), (0,)), ((), ())), preferred_e...]
    unnamed x36 -> x47, local copies, waits for them, and re-layouts: 3.1 us -> 7.32 us
    slice x3 -> x0, local copies, waits for them, and re-layouts: 4.15 us -> none  [conv_tile(): padded[row_tap:row_tap + rows_out, col_tap:col_tap + cols_out]]
  transfers between devices with their start and end apart: 6 -> 9, of which waited for: 4 -> 1; matrix products, arithmetic and copies ran while one was open for 4% -> 4% of each run, Pallas kernels for 0% -> 0%
where the time goes in v2:
time: 169 us; the launch traced here: 168 us
  blocking collectives  80.8 us (48%)
  starting transfers between devices  34.5 us (20%)
  waiting for transfers between devices  29.1 us (17%)
  local copies, waits for them, and re-layouts  10.1 us (6%)
  matrix products  9.63 us (6%)
  other arithmetic  3.03 us (2%)
    all_to_all x1, blocking collectives, sent_and_summed(): lax.all_to_all(blocks, axis, split_axis=0, concat_axis=0, tiled=True)  43.8 us
    all_to_all x1, blocking collectives, sent_to_all(): return lax.all_to_all(copies, axis, split_axis=0, concat_axis=0, tiled=True)  36.9 us
    all_to_all x1, waiting for transfers between devices, sent_to_all(): return lax.all_to_all(copies, axis, split_axis=0, concat_axis=0, tiled=True)  29.1 us
    ppermute x4, starting transfers between devices, from_neighbours(): return lax.ppermute(piece, ('lon', 'lat'), pairs)  14.6 us
    ppermute x2, starting transfers between devices, from_neighbours(): return lax.ppermute(piece, 'lat', neighbour_pairs(n_lat, lat_step, False))  8.45 us
    unnamed x47, local copies, waits for them, and re-layouts  7.32 us
    ppermute x2, starting transfers between devices, from_neighbours(): return lax.ppermute(piece, 'lon', neighbour_pairs(n_lon, lon_step, True))  6.18 us
    dot_general x2, matrix products, weight_terms(): lax.dot_general(stacked, flat_grad, (((0,), (0,)), ((), ())), preferred_e...  5.42 us
  transfers between devices with their start and end apart: 9, of which 1 were waited for; matrix products, arithmetic and copies ran while one was open for 4% of the time, Pallas kernels for 0%

profile of v2, /device:TPU:9, one launch (start us, length us, event | category | flops | bytes accessed | tf_op | source)
XLA Modules:
  0.0 168.4 jit_solution(4170531995281547602)
XLA Ops:
  0.7 0.9 pad_maximum_fusion.8
  1.5 5.4 %collective-permute-start = (bf16[2,2,2,128]{3,2,1,0:T(2,128)(2,1)S(1)}, bf16[2,2,2,128]{3,2,1,0:T(2,128)(2,1)S(1)}, u32[]{:S(2)}, u32[]{:S(2)}) collective-permute-start(bf16[2,2,2,128]{3,2,1,0:T(2,128)(2,1)S(1)} %get-tuple-element.7), channel_id=1, source_target_pairs={{0,17},{16,33},{32,49},{48,65},{64,81},{80,97},{96,113},{112,129},... | collective-permute-start | bytes 6152 | tf_op jit(solution)/shard_map/ppermute | solution.py:28
  6.9 2.0 %collective-permute-start.2 = (bf16[2,2,2,128]{3,2,1,0:T(2,128)(2,1)S(1)}, bf16[2,2,2,128]{3,2,1,0:T(2,128)(2,1)S(1)}, u32[]{:S(2)}, u32[]{:S(2)}) collective-permute-start(bf16[2,2,2,128]{3,2,1,0:T(2,128)(2,1)S(1)} %get-tuple-element.9), channel_id=1, source_target_pairs={{0,497},{16,1},{32,17},{48,33},{64,49},{80,65},{96,81},{112,97},{1... | collective-permute-start | bytes 6152 | tf_op jit(solution)/shard_map/ppermute | solution.py:28
  8.9 4.5 %collective-permute-start.5 = (bf16[2,2,2,128]{3,2,1,0:T(2,128)(2,1)S(1)}, bf16[2,2,2,128]{3,2,1,0:T(2,128)(2,1)S(1)}, u32[]{:S(2)}, u32[]{:S(2)}) collective-permute-start(bf16[2,2,2,128]{3,2,1,0:T(2,128)(2,1)S(1)} %get-tuple-element.8), channel_id=1, source_target_pairs={{1,16},{17,32},{33,48},{49,64},{65,80},{81,96},{97,112},{113,128},... | collective-permute-start | bytes 6152 | tf_op jit(solution)/shard_map/ppermute | solution.py:28
  13.4 2.8 %collective-permute-start.7 = (bf16[2,2,2,128]{3,2,1,0:T(2,128)(2,1)S(1)}, bf16[2,2,2,128]{3,2,1,0:T(2,128)(2,1)S(1)}, u32[]{:S(2)}, u32[]{:S(2)}) collective-permute-start(bf16[2,2,2,128]{3,2,1,0:T(2,128)(2,1)S(1)} %get-tuple-element.10), channel_id=1, source_target_pairs={{1,496},{17,0},{33,16},{49,32},{65,48},{81,64},{97,80},{113,96},{1... | collective-permute-start | bytes 6152 | tf_op jit(solution)/shard_map/ppermute | solution.py:28
  16.2 0.8 pad_maximum_fusion.2
  17.0 6.5 %collective-permute-start.1 = (bf16[2,2,64,128]{3,2,1,0:T(8,128)(2,1)S(1)}, bf16[2,2,64,128]{3,2,1,0:T(8,128)(2,1)S(1)}, u32[]{:S(2)}, u32[]{:S(2)}) collective-permute-start(bf16[2,2,64,128]{3,2,1,0:T(8,128)(2,1)S(1)} %get-tuple-element.11), channel_id=1, source_target_pairs={{0,1},{1,2},{2,3},{3,4},{4,5},{5,6},{6,7},{7,8},{8,9},{9,10},{10,1... | collective-permute-start | bytes 196616 | tf_op jit(solution)/shard_map/ppermute | solution.py:23
  23.6 0.8 pad_maximum_fusion.4
  24.4 1.9 %collective-permute-start.6 = (bf16[2,2,64,128]{3,2,1,0:T(8,128)(2,1)S(1)}, bf16[2,2,64,128]{3,2,1,0:T(8,128)(2,1)S(1)}, u32[]{:S(2)}, u32[]{:S(2)}) collective-permute-start(bf16[2,2,64,128]{3,2,1,0:T(8,128)(2,1)S(1)} %get-tuple-element.12), channel_id=1, source_target_pairs={{1,0},{2,1},{3,2},{4,3},{5,4},{6,5},{7,6},{8,7},{9,8},{10,9},{11,1... | collective-permute-start | bytes 196616 | tf_op jit(solution)/shard_map/ppermute | solution.py:23
  26.4 1.9 %collective-permute-start.3 = (bf16[2,16,2,128]{3,2,1,0:T(2,128)(2,1)S(1)}, bf16[2,16,2,128]{3,2,1,0:T(2,128)(2,1)S(1)}, u32[]{:S(2)}, u32[]{:S(2)}) collective-permute-start(bf16[2,16,2,128]{3,2,1,0:T(2,128)(2,1)S(1)} %get-tuple-element.13), channel_id=1, source_target_pairs={{0,16},{16,32},{32,48},{48,64},{64,80},{80,96},{96,112},{112,128},... | collective-permute-start | bytes 49160 | tf_op jit(solution)/shard_map/ppermute | solution.py:21
  28.3 4.3 %collective-permute-start.4 = (bf16[2,16,2,128]{3,2,1,0:T(2,128)(2,1)S(1)}, bf16[2,16,2,128]{3,2,1,0:T(2,128)(2,1)S(1)}, u32[]{:S(2)}, u32[]{:S(2)}) collective-permute-start(bf16[2,16,2,128]{3,2,1,0:T(2,128)(2,1)S(1)} %get-tuple-element.14), channel_id=1, source_target_pairs={{0,496},{16,0},{32,16},{48,32},{64,48},{80,64},{96,80},{112,96},{1... | collective-permute-start | bytes 49160 | tf_op jit(solution)/shard_map/ppermute | solution.py:21
  32.6 1.2 copy.8
  33.9 0.3 maximum_maximum_fusion
  34.9 0.1 slice_dynamic-update-slice_fusion.12
  35.3 0.1 slice_dynamic-update-slice_fusion.25
  36.1 0.1 slice_dynamic-update-slice_fusion.7
  36.3 0.1 slice_dynamic-update-slice_fusion.6
  37.1 1.1 fusion.10
  38.2 0.1 slice_dynamic-update-slice_fusion.34
  39.1 0.8 convolution_bitcast_fusion
  40.0 0.6 copy-done.3
  40.6 0.2 slice_dynamic-update-slice_fusion.9
  40.8 1.4 copy-done.5
  42.2 0.8 copy-done.6
  43.0 4.6 %convolution_bitcast_fusion.1 = f32[1152,128]{1,0:T(8,128)S(1)} fusion(bf16[16,64,1152]{2,1,0:T(8,128)(2,1)} %copy-done.5, bf16[16,64,1152]{2,1,0:T(8,128)(2,1)} %copy-done.6, bf16[1152,128,1]{1,0,2:T(8,128)(2,1)S(1)} %bitcast.46, f32[18,66,128]{2,1,0:T(8,128)S(1)} %get-tuple-element.16), kind=kOutput, calls=%fused_computation.1 | convolution fusion | flops 605159424 | bytes 6127616 | tf_op jit(solution)/shard_map/dot_general | solution.py:107
  47.7 43.8 %all_to_all.15 = f32[32,72,128]{2,1,0:T(8,128)S(1)} all-to-all(f32[32,72,128]{2,1,0:T(8,128)S(1)} %bitcast.34), channel_id=1, replica_groups=mesh['lon'=32,'lat'=16] {'lon'}, dimensions={0} | all-to-all | bytes 2359296 | tf_op jit(solution)/shard_map/all_to_all | solution.py:60
  91.6 36.9 %all_to_all.16 = f32[16,72,128]{2,1,0:T(8,128)S(1)} all-to-all(f32[16,72,128]{2,1,0:T(8,128)S(1)} %broadcast_in_dim.20), channel_id=1, replica_groups=mesh['lon'=32,'lat'=16] {'lat'}, dimensions={0} | all-to-all | bytes 1179648 | tf_op jit(solution)/shard_map/all_to_all | solution.py:66
  128.6 1.1 broadcast_in_dim.21
  129.8 5.3 %all-to-all-start.2 = ((f32[32,72,128]{2,1,0:T(8,128)}), f32[32,72,128]{2,1,0:T(8,128)S(1)}, u32[]{:S(2)}, u32[]{:S(2)}) async-start(f32[32,72,128]{2,1,0:T(8,128)} %broadcast_in_dim.21), calls=%async_computation.2 | async-start | bytes 2359296 | tf_op jit(solution)/shard_map/all_to_all | solution.py:66
  135.1 3.1 %convolution_convert_fusion = bf16[16,64,128]{2,1,0:T(8,128)(2,1)} fusion(bf16[16,64,1152]{2,1,0:T(8,128)(2,1)} %copy-done.3, bf16[1152,128,1]{1,0,2:T(8,128)(2,1)S(1)} %bitcast.43), kind=kOutput, calls=%fused_computation.3 | convolution fusion | flops 302120960 | bytes 2916352 | tf_op jit(solution)/shard_map/dot_general | solution.py:97
  138.2 29.1 %all-to-all-done.2 = f32[32,72,128]{2,1,0:T(8,128)S(1)} async-done(((f32[32,72,128]{2,1,0:T(8,128)}), f32[32,72,128]{2,1,0:T(8,128)S(1)}, u32[]{:S(2)}, u32[]{:S(2)}) %all-to-all-start.2) | async-done | bytes 1179680 | tf_op jit(solution)/shard_map/all_to_all | solution.py:66
  167.3 1.1 fusion.13
  (55 shorter events, 3.3 us)
Async XLA Ops:
  0.6 36.5 %copy-start = (bf16[3,3,128,128]{3,2,1,0:T(8,128)(2,1)S(1)}, bf16[3,3,128,128]{3,2,1,0:T(8,128)(2,1)}, u32[]{:S(2)}) copy-start(bf16[3,3,128,128]{3,2,1,0:T(8,128)(2,1)} %param.5) | copy-start | bytes 884740
  0.6 33.2 %copy-start.1 = (bf16[16,64,128]{2,1,0:T(8,128)(2,1)S(1)}, bf16[16,64,128]{2,1,0:T(8,128)(2,1)}, u32[]{:S(2)}) copy-start(bf16[16,64,128]{2,1,0:T(8,128)(2,1)} %param.4) | copy-start | bytes 786436
  0.7 33.2 %copy-start.2 = (bf16[16,64,128]{2,1,0:T(8,128)(2,1)S(1)}, bf16[16,64,128]{2,1,0:T(8,128)(2,1)}, u32[]{:S(2)}) copy-start(bf16[16,64,128]{2,1,0:T(8,128)(2,1)} %param.7) | copy-start | bytes 786436
  1.5 22.9 %collective-permute-start = (bf16[2,2,2,128]{3,2,1,0:T(2,128)(2,1)S(1)}, bf16[2,2,2,128]{3,2,1,0:T(2,128)(2,1)S(1)}, u32[]{:S(2)}, u32[]{:S(2)}) collective-permute-start(bf16[2,2,2,128]{3,2,1,0:T(2,128)(2,1)S(1)} %get-tuple-element.7), channel_id=1, source_target_pairs={{0,17},{16,33},{32,49},{48,65},{64,81},{80,97},{96,113},{112,129},... | collective-permute-start | bytes 6152 | tf_op jit(solution)/shard_map/ppermute | solution.py:28
  6.9 19.4 %collective-permute-start.2 = (bf16[2,2,2,128]{3,2,1,0:T(2,128)(2,1)S(1)}, bf16[2,2,2,128]{3,2,1,0:T(2,128)(2,1)S(1)}, u32[]{:S(2)}, u32[]{:S(2)}) collective-permute-start(bf16[2,2,2,128]{3,2,1,0:T(2,128)(2,1)S(1)} %get-tuple-element.9), channel_id=1, source_target_pairs={{0,497},{16,1},{32,17},{48,33},{64,49},{80,65},{96,81},{112,97},{1... | collective-permute-start | bytes 6152 | tf_op jit(solution)/shard_map/ppermute | solution.py:28
  8.9 19.4 %collective-permute-start.5 = (bf16[2,2,2,128]{3,2,1,0:T(2,128)(2,1)S(1)}, bf16[2,2,2,128]{3,2,1,0:T(2,128)(2,1)S(1)}, u32[]{:S(2)}, u32[]{:S(2)}) collective-permute-start(bf16[2,2,2,128]{3,2,1,0:T(2,128)(2,1)S(1)} %get-tuple-element.8), channel_id=1, source_target_pairs={{1,16},{17,32},{33,48},{49,64},{65,80},{81,96},{97,112},{113,128},... | collective-permute-start | bytes 6152 | tf_op jit(solution)/shard_map/ppermute | solution.py:28
  13.4 20.4 %collective-permute-start.7 = (bf16[2,2,2,128]{3,2,1,0:T(2,128)(2,1)S(1)}, bf16[2,2,2,128]{3,2,1,0:T(2,128)(2,1)S(1)}, u32[]{:S(2)}, u32[]{:S(2)}) collective-permute-start(bf16[2,2,2,128]{3,2,1,0:T(2,128)(2,1)S(1)} %get-tuple-element.10), channel_id=1, source_target_pairs={{1,496},{17,0},{33,16},{49,32},{65,48},{81,64},{97,80},{113,96},{1... | collective-permute-start | bytes 6152 | tf_op jit(solution)/shard_map/ppermute | solution.py:28
  17.0 16.8 %collective-permute-start.1 = (bf16[2,2,64,128]{3,2,1,0:T(8,128)(2,1)S(1)}, bf16[2,2,64,128]{3,2,1,0:T(8,128)(2,1)S(1)}, u32[]{:S(2)}, u32[]{:S(2)}) collective-permute-start(bf16[2,2,64,128]{3,2,1,0:T(8,128)(2,1)S(1)} %get-tuple-element.11), channel_id=1, source_target_pairs={{0,1},{1,2},{2,3},{3,4},{4,5},{5,6},{6,7},{7,8},{8,9},{9,10},{10,1... | collective-permute-start | bytes 196616 | tf_op jit(solution)/shard_map/ppermute | solution.py:23
  24.4 9.4 %collective-permute-start.6 = (bf16[2,2,64,128]{3,2,1,0:T(8,128)(2,1)S(1)}, bf16[2,2,64,128]{3,2,1,0:T(8,128)(2,1)S(1)}, u32[]{:S(2)}, u32[]{:S(2)}) collective-permute-start(bf16[2,2,64,128]{3,2,1,0:T(8,128)(2,1)S(1)} %get-tuple-element.12), channel_id=1, source_target_pairs={{1,0},{2,1},{3,2},{4,3},{5,4},{6,5},{7,6},{8,7},{9,8},{10,9},{11,1... | collective-permute-start | bytes 196616 | tf_op jit(solution)/shard_map/ppermute | solution.py:23
  26.4 7.4 %collective-permute-start.3 = (bf16[2,16,2,128]{3,2,1,0:T(2,128)(2,1)S(1)}, bf16[2,16,2,128]{3,2,1,0:T(2,128)(2,1)S(1)}, u32[]{:S(2)}, u32[]{:S(2)}) collective-permute-start(bf16[2,16,2,128]{3,2,1,0:T(2,128)(2,1)S(1)} %get-tuple-element.13), channel_id=1, source_target_pairs={{0,16},{16,32},{32,48},{48,64},{64,80},{80,96},{96,112},{112,128},... | collective-permute-start | bytes 49160 | tf_op jit(solution)/shard_map/ppermute | solution.py:21
  28.3 5.5 %collective-permute-start.4 = (bf16[2,16,2,128]{3,2,1,0:T(2,128)(2,1)S(1)}, bf16[2,16,2,128]{3,2,1,0:T(2,128)(2,1)S(1)}, u32[]{:S(2)}, u32[]{:S(2)}) collective-permute-start(bf16[2,16,2,128]{3,2,1,0:T(2,128)(2,1)S(1)} %get-tuple-element.14), channel_id=1, source_target_pairs={{0,496},{16,0},{32,16},{48,32},{64,48},{80,64},{96,80},{112,96},{1... | collective-permute-start | bytes 49160 | tf_op jit(solution)/shard_map/ppermute | solution.py:21
  39.1 1.4 copy-start.3
  40.8 1.4 copy-start.5
  40.8 2.2 %copy-start.6 = (bf16[16,64,1152]{2,1,0:T(8,128)(2,1)}, bf16[16,64,1152]{2,1,0:T(8,128)(2,1)S(1)}, u32[]{:S(2)}) copy-start(bf16[16,64,1152]{2,1,0:T(8,128)(2,1)S(1)} %get-tuple-element.17) | copy-start | bytes 7077892
  128.6 6.5 %copy-start.4 = (bf16[3,3,128,128]{3,2,1,0:T(8,128)(2,1)S(1)}, bf16[3,3,128,128]{3,2,1,0:T(8,128)(2,1)}, u32[]{:S(2)}) copy-start(bf16[3,3,128,128]{3,2,1,0:T(8,128)(2,1)} %param.6) | copy-start | bytes 884740
  129.8 37.5 %all-to-all-start.2 = ((f32[32,72,128]{2,1,0:T(8,128)}), f32[32,72,128]{2,1,0:T(8,128)S(1)}, u32[]{:S(2)}, u32[]{:S(2)}) async-start(f32[32,72,128]{2,1,0:T(8,128)} %broadcast_in_dim.21), calls=%async_computation.2 | async-start | bytes 2359296 | tf_op jit(solution)/shard_map/all_to_all | solution.py:66

commit v3 on v0

--- a/solution.py
+++ b/solution.py
@@ -51,37 +51,33 @@
     return in_order(sent_to_all(x, axis), dim)
 
 
+def windows(padded, rows_out, cols_out):
+    taps = [
+        padded[row_tap : row_tap + rows_out, col_tap : col_tap + cols_out]
+        for row_tap in range(3)
+        for col_tap in range(3)
+    ]
+    return jnp.concatenate(taps, axis=-1).reshape(rows_out * cols_out, 9 * padded.shape[2])
+
+
 def conv_tile(padded, weights):
     rows_out = padded.shape[0] - 2
     cols_out = padded.shape[1] - 2
-    channels = padded.shape[2]
-    summed = jnp.zeros((rows_out * cols_out, weights.shape[3]), jnp.float32)
-    for row_tap in range(3):
-        for col_tap in range(3):
-            window = padded[row_tap : row_tap + rows_out, col_tap : col_tap + cols_out].reshape(
-                rows_out * cols_out, channels
-            )
-            summed = summed + jnp.dot(
-                window, weights[row_tap, col_tap], preferred_element_type=jnp.float32
-            )
+    stacked = windows(padded, rows_out, cols_out)
+    summed = jnp.dot(
+        stacked, weights.reshape(-1, weights.shape[3]), preferred_element_type=jnp.float32
+    )
     return summed.reshape(rows_out, cols_out, weights.shape[3])
 
 
 def weight_terms(padded, gradient):
     rows_out, cols_out, channels = gradient.shape
     flat_grad = gradient.reshape(rows_out * cols_out, channels)
-    taps = []
-    for row_tap in range(3):
-        for col_tap in range(3):
-            window = padded[row_tap : row_tap + rows_out, col_tap : col_tap + cols_out].reshape(
-                rows_out * cols_out, padded.shape[2]
-            )
-            taps.append(
-                lax.dot_general(
-                    window, flat_grad, (((0,), (0,)), ((), ())), preferred_element_type=jnp.float32
-                )
-            )
-    return jnp.stack(taps).reshape(3, 3, padded.shape[2], channels)
+    stacked = windows(padded, rows_out, cols_out)
+    terms = lax.dot_general(
+        stacked, flat_grad, (((0,), (0,)), ((), ())), preferred_element_type=jnp.float32
+    )
+    return terms.reshape(3, 3, padded.shape[2], channels)
 
 
 def shards(latent_frame, weights_in, weights_out, cotangent):

time: 156 us -> 149 us (0.955)
  blocking collectives: 44.6 us -> 72.9 us
  waiting for transfers between devices: 49.5 us -> 35.8 us
  starting transfers between devices: 27.8 us -> 16.5 us
  local copies, waits for them, and re-layouts: 15.3 us -> 10.1 us
  matrix products: 14.8 us -> 9.63 us
    all_to_all x0 -> x1, blocking collectives: none -> 28.5 us  [sent_to_all(): return lax.all_to_all(copies, axis, split_axis=0, concat_axis=0, tiled=True)]
    all_to_all x2 -> x1, waiting for transfers between devices: 43.6 us -> 29.1 us  [sent_to_all(): return lax.all_to_all(copies, axis, split_axis=0, concat_axis=0, tiled=True)]
    all_to_all x2 -> x1, starting transfers between devices: 16.3 us -> 5.05 us  [sent_to_all(): return lax.all_to_all(copies, axis, split_axis=0, concat_axis=0, tiled=True)]
    dot_general x45 -> x4, matrix products: 14.8 us -> 9.63 us  [the longest x2 5.42 us: weight_terms(): lax.dot_general(stacked, flat_grad, (((0,), (0,)), ((), ())), preferred_e...]
    unnamed x36 -> x47, local copies, waits for them, and re-layouts: 3.1 us -> 7.33 us
    slice x3 -> x0, local copies, waits for them, and re-layouts: 4.15 us -> none  [conv_tile(): padded[row_tap:row_tap + rows_out, col_tap:col_tap + cols_out]]
    reshape x10 -> x0, local copies, waits for them, and re-layouts: 3.22 us -> none  [the longest x9 3.17 us: conv_tile(): padded[row_tap:row_tap + rows_out, col_tap:col_tap + cols_out]]
    transpose x1 -> x0, local copies, waits for them, and re-layouts: 1.69 us -> none  [shards(): flipped = jnp.transpose(weights_out[::-1, ::-1], (0, 1, 3, 2))]
  transfers between devices with their start and end apart: 6 -> 5, of which waited for: 4 -> 3; matrix products, arithmetic and copies ran while one was open for 4% -> 3% of each run, Pallas kernels for 0% -> 0%
where the time goes in v3:
time: 149 us; the launch traced here: 148 us
  blocking collectives  72.9 us (49%)
  waiting for transfers between devices  35.8 us (24%)
  starting transfers between devices  16.5 us (11%)
  local copies, waits for them, and re-layouts  10.1 us (7%)
  matrix products  9.63 us (6%)
  other arithmetic  2.22 us (1%)
    all_to_all x1, blocking collectives, sent_and_summed(): lax.all_to_all(blocks, axis, split_axis=0, concat_axis=0, tiled=True)  44.3 us
    all_to_all x1, waiting for transfers between devices, sent_to_all(): return lax.all_to_all(copies, axis, split_axis=0, concat_axis=0, tiled=True)  29.1 us
    all_to_all x1, blocking collectives, sent_to_all(): return lax.all_to_all(copies, axis, split_axis=0, concat_axis=0, tiled=True)  28.5 us
    ppermute x2, starting transfers between devices, with_halo(): lax.ppermute(lax.slice_in_dim(block, block.shape[dim] - width, None, axis...  7.57 us
    unnamed x47, local copies, waits for them, and re-layouts  7.33 us
    ppermute x2, waiting for transfers between devices, with_halo(): lax.ppermute(lax.slice_in_dim(block, 0, width, axis=dim), axis, backward)  6.7 us
    dot_general x2, matrix products, weight_terms(): lax.dot_general(stacked, flat_grad, (((0,), (0,)), ((), ())), preferred_e...  5.42 us
    all_to_all x1, starting transfers between devices, sent_to_all(): return lax.all_to_all(copies, axis, split_axis=0, concat_axis=0, tiled=True)  5.05 us
  transfers between devices with their start and end apart: 5, of which 3 were waited for; matrix products, arithmetic and copies ran while one was open for 3% of the time, Pallas kernels for 0%

profile of v3, /device:TPU:9, one launch (start us, length us, event | category | flops | bytes accessed | tf_op | source)
XLA Modules:
  0.0 148.2 jit_solution(12403951223350027215)
XLA Ops:
  0.7 0.9 pad_maximum_fusion.7
  1.6 3.7 %collective-permute-start = (bf16[2,16,2,128]{3,2,1,0:T(2,128)(2,1)S(1)}, bf16[2,16,2,128]{3,2,1,0:T(2,128)(2,1)S(1)}, u32[]{:S(2)}, u32[]{:S(2)}) collective-permute-start(bf16[2,16,2,128]{3,2,1,0:T(2,128)(2,1)S(1)} %get-tuple-element.9), channel_id=1, source_target_pairs={{0,16},{16,32},{32,48},{48,64},{64,80},{80,96},{96,112},{112,128},... | collective-permute-start | bytes 49160 | tf_op jit(solution)/shard_map/ppermute | solution.py:14
  5.3 1.9 %collective-permute-start.1 = (bf16[2,16,2,128]{3,2,1,0:T(2,128)(2,1)S(1)}, bf16[2,16,2,128]{3,2,1,0:T(2,128)(2,1)S(1)}, u32[]{:S(2)}, u32[]{:S(2)}) collective-permute-start(bf16[2,16,2,128]{3,2,1,0:T(2,128)(2,1)S(1)} %get-tuple-element.10), channel_id=1, source_target_pairs={{16,0},{32,16},{48,32},{64,48},{80,64},{96,80},{112,96},{128,112},... | collective-permute-start | bytes 49160 | tf_op jit(solution)/shard_map/ppermute | solution.py:17
  7.2 1.2 copy.8
  8.4 2.2 %collective-permute-done.1 = bf16[2,16,2,128]{3,2,1,0:T(2,128)(2,1)S(1)} collective-permute-done((bf16[2,16,2,128]{3,2,1,0:T(2,128)(2,1)S(1)}, bf16[2,16,2,128]{3,2,1,0:T(2,128)(2,1)S(1)}, u32[]{:S(2)}, u32[]{:S(2)}) %collective-permute-start.1) | collective-permute-done | bytes 16416 | tf_op jit(solution)/shard_map/ppermute | solution.py:17
  10.6 0.9 pad_maximum_fusion.5
  11.5 3.9 %collective-permute-start.2 = (bf16[2,2,68,128]{3,2,1,0:T(8,128)(2,1)S(1)}, bf16[2,2,68,128]{3,2,1,0:T(8,128)(2,1)S(1)}, u32[]{:S(2)}, u32[]{:S(2)}) collective-permute-start(bf16[2,2,68,128]{3,2,1,0:T(8,128)(2,1)S(1)} %get-tuple-element.7), channel_id=1, source_target_pairs={{0,1},{1,2},{2,3},{3,4},{4,5},{5,6},{6,7},{7,8},{8,9},{9,10},{10,1... | collective-permute-start | bytes 208904 | tf_op jit(solution)/shard_map/ppermute | solution.py:14
  15.4 1.9 %collective-permute-start.3 = (bf16[2,2,68,128]{3,2,1,0:T(8,128)(2,1)S(1)}, bf16[2,2,68,128]{3,2,1,0:T(8,128)(2,1)S(1)}, u32[]{:S(2)}, u32[]{:S(2)}) collective-permute-start(bf16[2,2,68,128]{3,2,1,0:T(8,128)(2,1)S(1)} %get-tuple-element.8), channel_id=1, source_target_pairs={{1,0},{2,1},{3,2},{4,3},{5,4},{6,5},{7,6},{8,7},{9,8},{10,9},{11,1... | collective-permute-start | bytes 208904 | tf_op jit(solution)/shard_map/ppermute | solution.py:17
  17.3 4.5 %collective-permute-done.3 = bf16[2,2,68,128]{3,2,1,0:T(8,128)(2,1)S(1)} collective-permute-done((bf16[2,2,68,128]{3,2,1,0:T(8,128)(2,1)S(1)}, bf16[2,2,68,128]{3,2,1,0:T(8,128)(2,1)S(1)}, u32[]{:S(2)}, u32[]{:S(2)}) %collective-permute-start.3) | collective-permute-done | bytes 69664 | tf_op jit(solution)/shard_map/ppermute | solution.py:17
  21.8 0.3 pad_maximum_fusion.1
  22.7 0.1 slice_dynamic-update-slice_fusion.13
  22.9 0.1 slice_dynamic-update-slice_fusion.12
  23.3 0.1 slice_dynamic-update-slice_fusion.25
  24.1 0.1 slice_dynamic-update-slice_fusion.7
  24.2 0.1 slice_dynamic-update-slice_fusion.6
  24.8 0.1 slice_dynamic-update-slice_fusion.1
  24.9 0.1 slice_dynamic-update-slice_fusion
  25.0 1.1 fusion.10
  26.2 0.1 slice_dynamic-update-slice_fusion.34
  27.1 0.8 convolution_bitcast_fusion
  27.9 0.6 copy-done.1
  28.5 0.2 slice_dynamic-update-slice_fusion.9
  28.7 1.4 copy-done.5
  30.1 0.8 copy-done.6
  30.9 4.6 %convolution_bitcast_fusion.1 = f32[1152,128]{1,0:T(8,128)S(1)} fusion(bf16[16,64,1152]{2,1,0:T(8,128)(2,1)} %copy-done.5, bf16[16,64,1152]{2,1,0:T(8,128)(2,1)} %copy-done.6, bf16[1152,128,1]{1,0,2:T(8,128)(2,1)S(1)} %bitcast.44, f32[18,66,128]{2,1,0:T(8,128)S(1)} %get-tuple-element.12), kind=kOutput, calls=%fused_computation.1 | convolution fusion | flops 605159424 | bytes 6127616 | tf_op jit(solution)/shard_map/dot_general | solution.py:77
  35.6 44.3 %all_to_all.15 = f32[32,72,128]{2,1,0:T(8,128)S(1)} all-to-all(f32[32,72,128]{2,1,0:T(8,128)S(1)} %bitcast.34), channel_id=1, replica_groups=mesh['lon'=32,'lat'=16] {'lon'}, dimensions={0} | all-to-all | bytes 2359296 | tf_op jit(solution)/shard_map/all_to_all | solution.py:30
  80.1 28.5 %all_to_all.16 = f32[16,72,128]{2,1,0:T(8,128)S(1)} all-to-all(f32[16,72,128]{2,1,0:T(8,128)S(1)} %broadcast_in_dim.20), channel_id=1, replica_groups=mesh['lon'=32,'lat'=16] {'lat'}, dimensions={0} | all-to-all | bytes 1179648 | tf_op jit(solution)/shard_map/all_to_all | solution.py:36
  108.6 1.1 broadcast_in_dim.21
  109.8 5.0 %all-to-all-start.2 = ((f32[32,72,128]{2,1,0:T(8,128)}), f32[32,72,128]{2,1,0:T(8,128)S(1)}, u32[]{:S(2)}, u32[]{:S(2)}) async-start(f32[32,72,128]{2,1,0:T(8,128)} %broadcast_in_dim.21), calls=%async_computation.2 | async-start | bytes 2359296 | tf_op jit(solution)/shard_map/all_to_all | solution.py:36
  114.8 3.1 %convolution_convert_fusion = bf16[16,64,128]{2,1,0:T(8,128)(2,1)} fusion(bf16[16,64,1152]{2,1,0:T(8,128)(2,1)} %copy-done.1, bf16[1152,128,1]{1,0,2:T(8,128)(2,1)S(1)} %bitcast.41), kind=kOutput, calls=%fused_computation.3 | convolution fusion | flops 302120960 | bytes 2916352 | tf_op jit(solution)/shard_map/dot_general | solution.py:67
  118.0 29.1 %all-to-all-done.2 = f32[32,72,128]{2,1,0:T(8,128)S(1)} async-done(((f32[32,72,128]{2,1,0:T(8,128)}), f32[32,72,128]{2,1,0:T(8,128)S(1)}, u32[]{:S(2)}, u32[]{:S(2)}) %all-to-all-start.2) | async-done | bytes 1179680 | tf_op jit(solution)/shard_map/all_to_all | solution.py:36
  147.1 1.1 fusion.13
  (46 shorter events, 2.9 us)
Async XLA Ops:
  0.6 24.4 %copy-start = (bf16[3,3,128,128]{3,2,1,0:T(8,128)(2,1)S(1)}, bf16[3,3,128,128]{3,2,1,0:T(8,128)(2,1)}, u32[]{:S(2)}) copy-start(bf16[3,3,128,128]{3,2,1,0:T(8,128)(2,1)} %param.5) | copy-start | bytes 884740
  0.6 21.2 %copy-start.2 = (bf16[16,64,128]{2,1,0:T(8,128)(2,1)S(1)}, bf16[16,64,128]{2,1,0:T(8,128)(2,1)}, u32[]{:S(2)}) copy-start(bf16[16,64,128]{2,1,0:T(8,128)(2,1)} %param.4) | copy-start | bytes 786436
  0.7 21.2 %copy-start.3 = (bf16[16,64,128]{2,1,0:T(8,128)(2,1)S(1)}, bf16[16,64,128]{2,1,0:T(8,128)(2,1)}, u32[]{:S(2)}) copy-start(bf16[16,64,128]{2,1,0:T(8,128)(2,1)} %param.7) | copy-start | bytes 786436
  1.6 6.8 %collective-permute-start = (bf16[2,16,2,128]{3,2,1,0:T(2,128)(2,1)S(1)}, bf16[2,16,2,128]{3,2,1,0:T(2,128)(2,1)S(1)}, u32[]{:S(2)}, u32[]{:S(2)}) collective-permute-start(bf16[2,16,2,128]{3,2,1,0:T(2,128)(2,1)S(1)} %get-tuple-element.9), channel_id=1, source_target_pairs={{0,16},{16,32},{32,48},{48,64},{64,80},{80,96},{96,112},{112,128},... | collective-permute-start | bytes 49160 | tf_op jit(solution)/shard_map/ppermute | solution.py:14
  5.3 5.4 %collective-permute-start.1 = (bf16[2,16,2,128]{3,2,1,0:T(2,128)(2,1)S(1)}, bf16[2,16,2,128]{3,2,1,0:T(2,128)(2,1)S(1)}, u32[]{:S(2)}, u32[]{:S(2)}) collective-permute-start(bf16[2,16,2,128]{3,2,1,0:T(2,128)(2,1)S(1)} %get-tuple-element.10), channel_id=1, source_target_pairs={{16,0},{32,16},{48,32},{64,48},{80,64},{96,80},{112,96},{128,112},... | collective-permute-start | bytes 49160 | tf_op jit(solution)/shard_map/ppermute | solution.py:17
  11.5 5.8 %collective-permute-start.2 = (bf16[2,2,68,128]{3,2,1,0:T(8,128)(2,1)S(1)}, bf16[2,2,68,128]{3,2,1,0:T(8,128)(2,1)S(1)}, u32[]{:S(2)}, u32[]{:S(2)}) collective-permute-start(bf16[2,2,68,128]{3,2,1,0:T(8,128)(2,1)S(1)} %get-tuple-element.7), channel_id=1, source_target_pairs={{0,1},{1,2},{2,3},{3,4},{4,5},{5,6},{6,7},{7,8},{8,9},{9,10},{10,1... | collective-permute-start | bytes 208904 | tf_op jit(solution)/shard_map/ppermute | solution.py:14
  15.4 6.5 %collective-permute-start.3 = (bf16[2,2,68,128]{3,2,1,0:T(8,128)(2,1)S(1)}, bf16[2,2,68,128]{3,2,1,0:T(8,128)(2,1)S(1)}, u32[]{:S(2)}, u32[]{:S(2)}) collective-permute-start(bf16[2,2,68,128]{3,2,1,0:T(8,128)(2,1)S(1)} %get-tuple-element.8), channel_id=1, source_target_pairs={{1,0},{2,1},{3,2},{4,3},{5,4},{6,5},{7,6},{8,7},{9,8},{10,9},{11,1... | collective-permute-start | bytes 208904 | tf_op jit(solution)/shard_map/ppermute | solution.py:17
  27.1 1.4 copy-start.1
  28.7 1.4 copy-start.5
  28.7 2.2 %copy-start.6 = (bf16[16,64,1152]{2,1,0:T(8,128)(2,1)}, bf16[16,64,1152]{2,1,0:T(8,128)(2,1)S(1)}, u32[]{:S(2)}) copy-start(bf16[16,64,1152]{2,1,0:T(8,128)(2,1)S(1)} %get-tuple-element.13) | copy-start | bytes 7077892
  108.6 6.2 %copy-start.4 = (bf16[3,3,128,128]{3,2,1,0:T(8,128)(2,1)S(1)}, bf16[3,3,128,128]{3,2,1,0:T(8,128)(2,1)}, u32[]{:S(2)}) copy-start(bf16[3,3,128,128]{3,2,1,0:T(8,128)(2,1)} %param.6) | copy-start | bytes 884740
  109.8 37.3 %all-to-all-start.2 = ((f32[32,72,128]{2,1,0:T(8,128)}), f32[32,72,128]{2,1,0:T(8,128)S(1)}, u32[]{:S(2)}, u32[]{:S(2)}) async-start(f32[32,72,128]{2,1,0:T(8,128)} %broadcast_in_dim.21), calls=%async_computation.2 | async-start | bytes 2359296 | tf_op jit(solution)/shard_map/all_to_all | solution.py:36

commit v4 on v3

--- a/solution.py
+++ b/solution.py
@@ -1,7 +1,9 @@
 import jax
 import jax.numpy as jnp
 from jax import lax
-from jax.sharding import PartitionSpec as P
+from jax.sharding import Mesh, PartitionSpec as P
+
+LON = ("lon_chip", "core")
 
 
 def with_halo(block, sides, width, periodic):
@@ -80,12 +82,33 @@
     return terms.reshape(3, 3, padded.shape[2], channels)
 
 
+def with_partner(x):
+    return lax.ppermute(x, "core", [(0, 1), (1, 0)])
+
+
+def reduced_everywhere(terms):
+    core = lax.axis_index("core")
+    half = terms.shape[0] // 2
+    mine = lax.dynamic_slice_in_dim(terms, core * half, half, 0)
+    other = lax.dynamic_slice_in_dim(terms, (1 - core) * half, half, 0)
+    chip_sum = mine + with_partner(other)
+    portion = sent_and_summed(chip_sum, "lon_chip", 0)
+    portion = taken_together(portion, "lat")
+    gathered = collect(portion, "lon_chip", 0)
+    partner = with_partner(gathered)
+    return jnp.where(
+        core == 0,
+        jnp.concatenate([gathered, partner], axis=0),
+        jnp.concatenate([partner, gathered], axis=0),
+    )
+
+
 def shards(latent_frame, weights_in, weights_out, cotangent):
     tile_rows = latent_frame.shape[0]
     channels = latent_frame.shape[2]
     stacked = jnp.stack([latent_frame, cotangent])
     margin = 2
-    widened = with_halo(stacked, (("lon", 2),), margin, True)
+    widened = with_halo(stacked, ((LON, 2),), margin, True)
     extended = with_halo(widened, (("lat", 1),), margin, False)
     input_pad = extended[0]
     grad_pad = extended[1][1:-1, 1:-1]
@@ -108,20 +131,20 @@
     all_terms = jnp.concatenate(
         [term_in.reshape(9 * channels, channels), term_out.reshape(9 * channels, channels)], axis=0
     )
-    portion = sent_and_summed(all_terms, "lon", 0)
-    portion = taken_together(portion, "lat")
-    summed = collect(portion, "lon", 0)
+    summed = reduced_everywhere(all_terms)
     grad_in = summed[: 9 * channels].reshape(3, 3, channels, channels)
     grad_out = summed[9 * channels :].reshape(3, 3, channels, channels)
     return (decoded, grad_in, grad_out)
 
 
 def solution(mesh):
-    placed = (P("lat", "lon", None), P(), P(), P("lat", "lon", None))
+    n_lon, n_lat = mesh.shape["lon"], mesh.shape["lat"]
+    split = Mesh(mesh.devices.reshape(n_lon // 2, 2, n_lat), (*LON, "lat"))
+    tiled = P("lat", LON, None)
     return jax.shard_map(
         shards,
-        mesh=mesh,
-        in_specs=placed,
-        out_specs=(P("lat", "lon", None), P(), P()),
+        mesh=split,
+        in_specs=(tiled, P(), P(), tiled),
+        out_specs=(tiled, P(), P()),
         check_vma=False,
     )

time: 149 us -> 139 us (0.933)
  the two profiles are of different devices: /device:TPU:9 before, /device:TPU:1 now
where the time goes in v4:
time: 139 us; the launch traced here: 138 us
  blocking collectives  74.6 us (54%)
  starting transfers between devices  27.4 us (20%)
  local copies, waits for them, and re-layouts  11.4 us (8%)
  matrix products  9.86 us (7%)
  other arithmetic  8.12 us (6%)
  waiting for transfers between devices  5.97 us (4%)
    all_to_all x2, blocking collectives, sent_to_all(): return lax.all_to_all(copies, axis, split_axis=0, concat_axis=0, tiled=True)  51.6 us
    all_to_all x1, blocking collectives, sent_and_summed(): lax.all_to_all(blocks, axis, split_axis=0, concat_axis=0, tiled=True)  23.1 us
    ppermute x2, starting transfers between devices, with_partner(): return lax.ppermute(x, 'core', [(0, 1), (1, 0)])  14.1 us
    ppermute x2, starting transfers between devices, with_halo(): lax.ppermute(lax.slice_in_dim(block, 0, width, axis=dim), axis, backward)  7.46 us
    unnamed x45, local copies, waits for them, and re-layouts  7.37 us
    dot_general x2, matrix products, weight_terms(): lax.dot_general(stacked, flat_grad, (((0,), (0,)), ((), ())), preferred_e...  6.45 us
    ppermute x2, starting transfers between devices, with_halo(): lax.ppermute(lax.slice_in_dim(block, block.shape[dim] - width, None, axis...  5.79 us
    ppermute x2, waiting for transfers between devices, with_halo(): lax.ppermute(lax.slice_in_dim(block, 0, width, axis=dim), axis, backward)  3.71 us
  transfers between devices with their start and end apart: 6, of which 4 were waited for; matrix products, arithmetic and copies ran while one was open for 2% of the time, Pallas kernels for 0%

profile of v4, /device:TPU:1, one launch (start us, length us, event | category | flops | bytes accessed | tf_op | source)
XLA Modules:
  0.0 138.3 jit_solution(18066270482488742650)
XLA Ops:
  0.7 0.9 pad_maximum_fusion.6
  1.6 4.5 %collective-permute-start = (bf16[2,16,2,128]{3,2,1,0:T(2,128)(2,1)S(1)}, bf16[2,16,2,128]{3,2,1,0:T(2,128)(2,1)S(1)}, u32[]{:S(2)}, u32[]{:S(2)}) collective-permute-start(bf16[2,16,2,128]{3,2,1,0:T(2,128)(2,1)S(1)} %get-tuple-element.9), channel_id=1, source_target_pairs={{0,16},{16,32},{32,48},{48,64},{64,80},{80,96},{96,112},{112,128},... | collective-permute-start | bytes 49160 | tf_op jit(solution)/shard_map/ppermute | solution.py:16
  6.1 6.2 %collective-permute-start.1 = (bf16[2,16,2,128]{3,2,1,0:T(2,128)(2,1)S(1)}, bf16[2,16,2,128]{3,2,1,0:T(2,128)(2,1)S(1)}, u32[]{:S(2)}, u32[]{:S(2)}) collective-permute-start(bf16[2,16,2,128]{3,2,1,0:T(2,128)(2,1)S(1)} %get-tuple-element.10), channel_id=1, source_target_pairs={{16,0},{32,16},{48,32},{64,48},{80,64},{96,80},{112,96},{128,112},... | collective-permute-start | bytes 49160 | tf_op jit(solution)/shard_map/ppermute | solution.py:19
  12.3 1.2 copy.8
  13.4 0.7 rev.3
  14.2 0.9 pad_maximum_fusion.4
  15.1 1.3 collective-permute-start.2
  16.4 1.3 collective-permute-start.3
  17.7 3.7 %collective-permute-done.3 = bf16[2,2,68,128]{3,2,1,0:T(8,128)(2,1)S(1)} collective-permute-done((bf16[2,2,68,128]{3,2,1,0:T(8,128)(2,1)S(1)}, bf16[2,2,68,128]{3,2,1,0:T(8,128)(2,1)S(1)}, u32[]{:S(2)}, u32[]{:S(2)}) %collective-permute-start.3) | collective-permute-done | bytes 69664 | tf_op jit(solution)/shard_map/ppermute | solution.py:19
  21.5 0.3 pad_maximum_fusion
  24.7 1.9 %fusion.13 = (bf16[18,66,128]{2,1,0:T(8,128)(2,1)S(1)}, f32[18,66,128]{2,1,0:T(8,128)}) fusion(pred[18]{0:T(512)(128)(4,1)S(1)} %compare_and_fusion, bf16[18,66,1152]{2,1,0:T(8,128)(2,1)S(1)} %slice_dynamic-update-slice_fusion, bf16[1152,128,1]{1,0,2:T(8,128)(2,1)S(1)} %bitcast.34), kind=kOutput, calls=%fused_computation.35 | convolution fusion | flops 351267840 | bytes 3944466 | tf_op jit(solution)/shard_map/dot_general | solution.py:69
  27.6 0.8 convolution_bitcast_fusion
  28.4 0.2 slice_dynamic-update-slice_fusion.9
  28.6 1.4 %copy-done.4 = bf16[16,64,1152]{2,1,0:T(8,128)(2,1)} copy-done((bf16[16,64,1152]{2,1,0:T(8,128)(2,1)}, bf16[16,64,1152]{2,1,0:T(8,128)(2,1)S(1)}, u32[]{:S(2)}) %copy-start.4) | copy-done | bytes 2359320
  30.0 1.4 %copy-done.5 = bf16[16,64,1152]{2,1,0:T(8,128)(2,1)} copy-done((bf16[16,64,1152]{2,1,0:T(8,128)(2,1)}, bf16[16,64,1152]{2,1,0:T(8,128)(2,1)S(1)}, u32[]{:S(2)}) %copy-start.5) | copy-done | bytes 2359320
  31.4 5.6 %convolution_bitcast_fusion.1 = f32[1152,128]{1,0:T(8,128)} fusion(bf16[16,64,1152]{2,1,0:T(8,128)(2,1)} %copy-done.4, bf16[16,64,1152]{2,1,0:T(8,128)(2,1)} %copy-done.5, bf16[1152,128,1]{1,0,2:T(8,128)(2,1)} %bitcast.47, f32[18,66,128]{2,1,0:T(8,128)} %get-tuple-element.12), kind=kOutput, calls=%fused_computation.1 | convolution fusion | flops 605159424 | bytes 6127616 | tf_op jit(solution)/shard_map/dot_general | solution.py:79
  37.1 2.1 %fusion.1 = f32[1152,128]{1,0:T(8,128)} fusion(s32[]{:T(128)S(6)} %select_n.21, f32[1152,128]{1,0:T(8,128)} %convolution_bitcast_fusion.1, f32[1152,128]{1,0:T(8,128)S(1)} %convolution_bitcast_fusion), kind=kLoop, calls=%fused_computation.12 | loop fusion | flops 147456 | bytes 1769476 | tf_op jit(solution)/shard_map/concatenate | solution.py:131
  39.2 7.9 %collective-permute-start.4 = (f32[1152,128]{1,0:T(8,128)}, f32[1152,128]{1,0:T(8,128)}, u32[]{:S(2)}, u32[]{:S(2)}) collective-permute-start(f32[1152,128]{1,0:T(8,128)} %fusion.1), channel_id=1, source_target_pairs={{0,16},{16,0},{1,17},{17,1},{2,18},{18,2},{3,19},{19,3},{4,20},{20... | collective-permute-start | bytes 1769480 | tf_op jit(solution)/shard_map/ppermute | solution.py:86
  47.1 1.9 %collective-permute-done.4 = f32[1152,128]{1,0:T(8,128)} collective-permute-done((f32[1152,128]{1,0:T(8,128)}, f32[1152,128]{1,0:T(8,128)}, u32[]{:S(2)}, u32[]{:S(2)}) %collective-permute-start.4) | collective-permute-done | bytes 589856 | tf_op jit(solution)/shard_map/ppermute | solution.py:86
  49.1 1.3 fusion.3
  50.4 23.1 %all_to_all.15 = f32[16,72,128]{2,1,0:T(8,128)S(1)} all-to-all(f32[16,72,128]{2,1,0:T(8,128)S(1)} %bitcast.37), channel_id=1, replica_groups=mesh['lon_chip'=16,'core'=2,'lat'=16] {'lon_chip'}, dimensions={0} | all-to-all | bytes 1179648 | tf_op jit(solution)/shard_map/all_to_all | solution.py:32
  73.4 0.7 reduce_sum.18
  74.1 0.8 broadcast_in_dim.20
  74.9 31.7 %all_to_all.16 = f32[16,72,128]{2,1,0:T(8,128)S(1)} all-to-all(f32[16,72,128]{2,1,0:T(8,128)S(1)} %broadcast_in_dim.20), channel_id=1, replica_groups=mesh['lon_chip'=16,'core'=2,'lat'=16] {'lat'}, dimensions={0} | all-to-all | bytes 1179648 | tf_op jit(solution)/shard_map/all_to_all | solution.py:38
  106.6 0.7 reduce_sum.19
  107.2 0.8 broadcast_in_dim.21
  108.0 19.9 %all_to_all.17 = f32[16,72,128]{2,1,0:T(8,128)S(1)} all-to-all(f32[16,72,128]{2,1,0:T(8,128)S(1)} %broadcast_in_dim.21), channel_id=1, replica_groups=mesh['lon_chip'=16,'core'=2,'lat'=16] {'lon_chip'}, dimensions={0} | all-to-all | bytes 1179648 | tf_op jit(solution)/shard_map/all_to_all | solution.py:38
  127.9 6.2 %collective-permute-start.5 = (f32[1152,128]{1,0:T(8,128)S(1)}, f32[1152,128]{1,0:T(8,128)}, u32[]{:S(2)}, u32[]{:S(2)}) collective-permute-start(f32[1152,128]{1,0:T(8,128)S(1)} %bitcast.35), channel_id=1, source_target_pairs={{0,16},{16,0},{1,17},{17,1},{2,18},{18,2},{3,19},{19,3},{4,20},{20... | collective-permute-start | bytes 1769480 | tf_op jit(solution)/shard_map/ppermute | solution.py:86
  134.2 1.5 %convolution_convert_fusion = bf16[16,64,128]{2,1,0:T(8,128)(2,1)} fusion(bf16[16,64,1152]{2,1,0:T(8,128)(2,1)S(1)} %slice_dynamic-update-slice_fusion.27, bf16[1152,128,1]{1,0,2:T(8,128)(2,1)S(1)} %bitcast.44), kind=kOutput, calls=%fused_computation.7 | convolution fusion | flops 302120960 | bytes 2916352 | tf_op jit(solution)/shard_map/dot_general | solution.py:69
  135.6 0.2 collective-permute-done.5
  135.9 1.4 maximum_select_fusion
  137.2 1.1 fusion.16
  (49 shorter events, 3.8 us)
Async XLA Ops:
  0.6 24.0 %copy-start = (bf16[3,3,128,128]{3,2,1,0:T(8,128)(2,1)S(1)}, bf16[3,3,128,128]{3,2,1,0:T(8,128)(2,1)}, u32[]{:S(2)}) copy-start(bf16[3,3,128,128]{3,2,1,0:T(8,128)(2,1)} %param.5) | copy-start | bytes 884740
  0.6 20.8 %copy-start.1 = (bf16[16,64,128]{2,1,0:T(8,128)(2,1)S(1)}, bf16[16,64,128]{2,1,0:T(8,128)(2,1)}, u32[]{:S(2)}) copy-start(bf16[16,64,128]{2,1,0:T(8,128)(2,1)} %param.4) | copy-start | bytes 786436
  0.7 20.8 %copy-start.2 = (bf16[16,64,128]{2,1,0:T(8,128)(2,1)S(1)}, bf16[16,64,128]{2,1,0:T(8,128)(2,1)}, u32[]{:S(2)}) copy-start(bf16[16,64,128]{2,1,0:T(8,128)(2,1)} %param.7) | copy-start | bytes 786436
  1.6 12.6 %collective-permute-start = (bf16[2,16,2,128]{3,2,1,0:T(2,128)(2,1)S(1)}, bf16[2,16,2,128]{3,2,1,0:T(2,128)(2,1)S(1)}, u32[]{:S(2)}, u32[]{:S(2)}) collective-permute-start(bf16[2,16,2,128]{3,2,1,0:T(2,128)(2,1)S(1)} %get-tuple-element.9), channel_id=1, source_target_pairs={{0,16},{16,32},{32,48},{48,64},{64,80},{80,96},{96,112},{112,128},... | collective-permute-start | bytes 49160 | tf_op jit(solution)/shard_map/ppermute | solution.py:16
  6.1 8.1 %collective-permute-start.1 = (bf16[2,16,2,128]{3,2,1,0:T(2,128)(2,1)S(1)}, bf16[2,16,2,128]{3,2,1,0:T(2,128)(2,1)S(1)}, u32[]{:S(2)}, u32[]{:S(2)}) collective-permute-start(bf16[2,16,2,128]{3,2,1,0:T(2,128)(2,1)S(1)} %get-tuple-element.10), channel_id=1, source_target_pairs={{16,0},{32,16},{48,32},{64,48},{80,64},{96,80},{112,96},{128,112},... | collective-permute-start | bytes 49160 | tf_op jit(solution)/shard_map/ppermute | solution.py:19
  15.1 2.7 %collective-permute-start.2 = (bf16[2,2,68,128]{3,2,1,0:T(8,128)(2,1)S(1)}, bf16[2,2,68,128]{3,2,1,0:T(8,128)(2,1)S(1)}, u32[]{:S(2)}, u32[]{:S(2)}) collective-permute-start(bf16[2,2,68,128]{3,2,1,0:T(8,128)(2,1)S(1)} %get-tuple-element.7), channel_id=1, source_target_pairs={{0,1},{1,2},{2,3},{3,4},{4,5},{5,6},{6,7},{7,8},{8,9},{9,10},{10,1... | collective-permute-start | bytes 208904 | tf_op jit(solution)/shard_map/ppermute | solution.py:16
  16.4 5.1 %collective-permute-start.3 = (bf16[2,2,68,128]{3,2,1,0:T(8,128)(2,1)S(1)}, bf16[2,2,68,128]{3,2,1,0:T(8,128)(2,1)S(1)}, u32[]{:S(2)}, u32[]{:S(2)}) collective-permute-start(bf16[2,2,68,128]{3,2,1,0:T(8,128)(2,1)S(1)} %get-tuple-element.8), channel_id=1, source_target_pairs={{1,0},{2,1},{3,2},{4,3},{5,4},{6,5},{7,6},{8,7},{9,8},{10,9},{11,1... | collective-permute-start | bytes 208904 | tf_op jit(solution)/shard_map/ppermute | solution.py:19
  28.6 1.4 %copy-start.4 = (bf16[16,64,1152]{2,1,0:T(8,128)(2,1)}, bf16[16,64,1152]{2,1,0:T(8,128)(2,1)S(1)}, u32[]{:S(2)}) copy-start(bf16[16,64,1152]{2,1,0:T(8,128)(2,1)S(1)} %get-tuple-element.14) | copy-start | bytes 7077892
  30.0 1.4 %copy-start.5 = (bf16[16,64,1152]{2,1,0:T(8,128)(2,1)}, bf16[16,64,1152]{2,1,0:T(8,128)(2,1)S(1)}, u32[]{:S(2)}) copy-start(bf16[16,64,1152]{2,1,0:T(8,128)(2,1)S(1)} %get-tuple-element.13) | copy-start | bytes 7077892
  39.2 9.9 %collective-permute-start.4 = (f32[1152,128]{1,0:T(8,128)}, f32[1152,128]{1,0:T(8,128)}, u32[]{:S(2)}, u32[]{:S(2)}) collective-permute-start(f32[1152,128]{1,0:T(8,128)} %fusion.1), channel_id=1, source_target_pairs={{0,16},{16,0},{1,17},{17,1},{2,18},{18,2},{3,19},{19,3},{4,20},{20... | collective-permute-start | bytes 1769480 | tf_op jit(solution)/shard_map/ppermute | solution.py:86
  73.4 60.7 %copy-start.3 = (bf16[3,3,128,128]{3,2,1,0:T(8,128)(2,1)S(1)}, bf16[3,3,128,128]{3,2,1,0:T(8,128)(2,1)}, u32[]{:S(2)}) copy-start(bf16[3,3,128,128]{3,2,1,0:T(8,128)(2,1)} %param.6) | copy-start | bytes 884740
  127.9 8.0 %collective-permute-start.5 = (f32[1152,128]{1,0:T(8,128)S(1)}, f32[1152,128]{1,0:T(8,128)}, u32[]{:S(2)}, u32[]{:S(2)}) collective-permute-start(f32[1152,128]{1,0:T(8,128)S(1)} %bitcast.35), channel_id=1, source_target_pairs={{0,16},{16,0},{1,17},{17,1},{2,18},{18,2},{3,19},{19,3},{4,20},{20... | collective-permute-start | bytes 1769480 | tf_op jit(solution)/shard_map/ppermute | solution.py:86

commit v5 on v4

--- a/solution.py
+++ b/solution.py
@@ -96,11 +96,7 @@
     portion = taken_together(portion, "lat")
     gathered = collect(portion, "lon_chip", 0)
     partner = with_partner(gathered)
-    return jnp.where(
-        core == 0,
-        jnp.concatenate([gathered, partner], axis=0),
-        jnp.concatenate([partner, gathered], axis=0),
-    )
+    return jnp.where(core == 0, gathered, partner), jnp.where(core == 0, partner, gathered)
 
 
 def shards(latent_frame, weights_in, weights_out, cotangent):
@@ -127,13 +123,14 @@
     grad_pre = (grad_hidden * (sigmoid_pre * (1.0 + preact * (1.0 - sigmoid_pre)))).astype(
         jnp.bfloat16
     )
+    grad_pre = lax.optimization_barrier(grad_pre)
     term_in = weight_terms(input_use, grad_pre)
     all_terms = jnp.concatenate(
         [term_in.reshape(9 * channels, channels), term_out.reshape(9 * channels, channels)], axis=0
     )
-    summed = reduced_everywhere(all_terms)
-    grad_in = summed[: 9 * channels].reshape(3, 3, channels, channels)
-    grad_out = summed[9 * channels :].reshape(3, 3, channels, channels)
+    grad_in, grad_out = reduced_everywhere(all_terms)
+    grad_in = grad_in.reshape(3, 3, channels, channels)
+    grad_out = grad_out.reshape(3, 3, channels, channels)
     return (decoded, grad_in, grad_out)
 
 

time: 139 us -> 131 us (0.942)
  matrix products: 9.86 us -> 5.05 us
  local copies, waits for them, and re-layouts: 11.4 us -> 7.54 us
    dot_general x2, matrix products: 6.45 us -> 1.64 us  [weight_terms(): lax.dot_general(stacked, flat_grad, (((0,), (0,)), ((), ())), preferred_e...]
    unnamed x45 -> x43, local copies, waits for them, and re-layouts: 7.37 us -> 5.36 us
    dot_general x2 -> x3, matrix products: 3.41 us -> 3.41 us  [conv_tile(): jnp.dot(stacked, weights.reshape(-1, weights.shape[3]), preferred_element...]
where the time goes in v5:
time: 131 us; the launch traced here: 130 us
  blocking collectives  74.1 us (57%)
  starting transfers between devices  28.3 us (22%)
  other arithmetic  7.96 us (6%)
  local copies, waits for them, and re-layouts  7.54 us (6%)
  waiting for transfers between devices  6.33 us (5%)
  matrix products  5.05 us (4%)
    all_to_all x2, blocking collectives, sent_to_all(): return lax.all_to_all(copies, axis, split_axis=0, concat_axis=0, tiled=True)  51.6 us
    all_to_all x1, blocking collectives, sent_and_summed(): lax.all_to_all(blocks, axis, split_axis=0, concat_axis=0, tiled=True)  22.5 us
    ppermute x2, starting transfers between devices, with_partner(): return lax.ppermute(x, 'core', [(0, 1), (1, 0)])  15 us
    ppermute x2, starting transfers between devices, with_halo(): lax.ppermute(lax.slice_in_dim(block, 0, width, axis=dim), axis, backward)  7.46 us
    ppermute x2, starting transfers between devices, with_halo(): lax.ppermute(lax.slice_in_dim(block, block.shape[dim] - width, None, axis...  5.79 us
    unnamed x43, local copies, waits for them, and re-layouts  5.36 us
    ppermute x2, waiting for transfers between devices, with_halo(): lax.ppermute(lax.slice_in_dim(block, 0, width, axis=dim), axis, backward)  4.07 us
    dot_general x3, matrix products, conv_tile(): jnp.dot(stacked, weights.reshape(-1, weights.shape[3]), preferred_element...  3.41 us
  transfers between devices with their start and end apart: 6, of which 4 were waited for; matrix products, arithmetic and copies ran while one was open for 2% of the time, Pallas kernels for 0%

profile of v5, /device:TPU:1, one launch (start us, length us, event | category | flops | bytes accessed | tf_op | source)
XLA Modules:
  0.0 130.3 jit_solution(3212787162672694776)
XLA Ops:
  0.7 0.9 pad_maximum_fusion.6
  1.6 4.5 %collective-permute-start = (bf16[2,16,2,128]{3,2,1,0:T(2,128)(2,1)S(1)}, bf16[2,16,2,128]{3,2,1,0:T(2,128)(2,1)S(1)}, u32[]{:S(2)}, u32[]{:S(2)}) collective-permute-start(bf16[2,16,2,128]{3,2,1,0:T(2,128)(2,1)S(1)} %get-tuple-element.9), channel_id=1, source_target_pairs={{0,16},{16,32},{32,48},{48,64},{64,80},{80,96},{96,112},{112,128},... | collective-permute-start | bytes 49160 | tf_op jit(solution)/shard_map/ppermute | solution.py:16
  6.1 6.2 %collective-permute-start.1 = (bf16[2,16,2,128]{3,2,1,0:T(2,128)(2,1)S(1)}, bf16[2,16,2,128]{3,2,1,0:T(2,128)(2,1)S(1)}, u32[]{:S(2)}, u32[]{:S(2)}) collective-permute-start(bf16[2,16,2,128]{3,2,1,0:T(2,128)(2,1)S(1)} %get-tuple-element.10), channel_id=1, source_target_pairs={{16,0},{32,16},{48,32},{64,48},{80,64},{96,80},{112,96},{128,112},... | collective-permute-start | bytes 49160 | tf_op jit(solution)/shard_map/ppermute | solution.py:19
  12.3 1.2 copy.8
  13.5 0.9 pad_maximum_fusion.4
  14.4 1.3 collective-permute-start.2
  15.7 1.3 collective-permute-start.3
  17.1 4.1 %collective-permute-done.3 = bf16[2,2,68,128]{3,2,1,0:T(8,128)(2,1)S(1)} collective-permute-done((bf16[2,2,68,128]{3,2,1,0:T(8,128)(2,1)S(1)}, bf16[2,2,68,128]{3,2,1,0:T(8,128)(2,1)S(1)}, u32[]{:S(2)}, u32[]{:S(2)}) %collective-permute-start.3) | collective-permute-done | bytes 69664 | tf_op jit(solution)/shard_map/ppermute | solution.py:19
  21.1 0.3 pad_maximum_fusion
  22.2 0.1 slice_dynamic-update-slice_fusion.12
  23.0 0.1 slice_dynamic-update-slice_fusion.21
  24.3 0.2 slice_dynamic-update-slice_fusion.9
  24.6 1.1 fusion.4
  25.7 0.8 fusion
  27.5 0.8 convolution_bitcast_fusion
  28.3 0.8 convolution_bitcast_fusion.1
  29.1 0.8 copy-done.1
  29.9 1.2 fusion.1
  31.1 8.8 %collective-permute-start.4 = (f32[1152,128]{1,0:T(8,128)}, f32[1152,128]{1,0:T(8,128)}, u32[]{:S(2)}, u32[]{:S(2)}) collective-permute-start(f32[1152,128]{1,0:T(8,128)} %fusion.1), channel_id=1, source_target_pairs={{0,16},{16,0},{1,17},{17,1},{2,18},{18,2},{3,19},{19,3},{4,20},{20... | collective-permute-start | bytes 1769480 | tf_op jit(solution)/shard_map/ppermute | solution.py:86
  39.9 1.9 %collective-permute-done.4 = f32[1152,128]{1,0:T(8,128)} collective-permute-done((f32[1152,128]{1,0:T(8,128)}, f32[1152,128]{1,0:T(8,128)}, u32[]{:S(2)}, u32[]{:S(2)}) %collective-permute-start.4) | collective-permute-done | bytes 589856 | tf_op jit(solution)/shard_map/ppermute | solution.py:86
  41.8 1.3 fusion.3
  43.1 22.5 %all_to_all.15 = f32[16,72,128]{2,1,0:T(8,128)S(1)} all-to-all(f32[16,72,128]{2,1,0:T(8,128)S(1)} %bitcast.39), channel_id=1, replica_groups=mesh['lon_chip'=16,'core'=2,'lat'=16] {'lon_chip'}, dimensions={0} | all-to-all | bytes 1179648 | tf_op jit(solution)/shard_map/all_to_all | solution.py:32
  65.7 0.7 reduce_sum.18
  66.3 0.8 broadcast_in_dim.20
  67.1 31.7 %all_to_all.16 = f32[16,72,128]{2,1,0:T(8,128)S(1)} all-to-all(f32[16,72,128]{2,1,0:T(8,128)S(1)} %broadcast_in_dim.20), channel_id=1, replica_groups=mesh['lon_chip'=16,'core'=2,'lat'=16] {'lat'}, dimensions={0} | all-to-all | bytes 1179648 | tf_op jit(solution)/shard_map/all_to_all | solution.py:38
  98.8 0.7 reduce_sum.19
  99.4 0.8 broadcast_in_dim.21
  100.2 19.9 %all_to_all.17 = f32[16,72,128]{2,1,0:T(8,128)S(1)} all-to-all(f32[16,72,128]{2,1,0:T(8,128)S(1)} %broadcast_in_dim.21), channel_id=1, replica_groups=mesh['lon_chip'=16,'core'=2,'lat'=16] {'lon_chip'}, dimensions={0} | all-to-all | bytes 1179648 | tf_op jit(solution)/shard_map/all_to_all | solution.py:38
  120.2 6.2 %collective-permute-start.5 = (f32[1152,128]{1,0:T(8,128)S(1)}, f32[1152,128]{1,0:T(8,128)}, u32[]{:S(2)}, u32[]{:S(2)}) collective-permute-start(f32[1152,128]{1,0:T(8,128)S(1)} %bitcast.38), channel_id=1, source_target_pairs={{0,16},{16,0},{1,17},{17,1},{2,18},{18,2},{3,19},{19,3},{4,20},{20... | collective-permute-start | bytes 1769480 | tf_op jit(solution)/shard_map/ppermute | solution.py:86
  126.4 1.5 %convolution_convert_fusion = bf16[16,64,128]{2,1,0:T(8,128)(2,1)} fusion(bf16[16,64,1152]{2,1,0:T(8,128)(2,1)S(1)} %slice_dynamic-update-slice_fusion.27, bf16[1152,128,1]{1,0,2:T(8,128)(2,1)S(1)} %bitcast.46), kind=kOutput, calls=%fused_computation.7 | convolution fusion | flops 302120960 | bytes 2916352 | tf_op jit(solution)/shard_map/dot_general | solution.py:69
  127.9 0.2 collective-permute-done.5
  128.1 2.2 %broadcast_select_fusion = (f32[1152,128]{1,0:T(8,128)}, f32[1152,128]{1,0:T(8,128)}) fusion(f32[1152,128]{1,0:T(8,128)} %collective-permute-done.5, pred[]{:T(512)S(6)} %eq.4, f32[16,72,128]{2,1,0:T(8,128)S(1)} %all_to_all.17), kind=kLoop, calls=%fused_computation.26 | loop fusion | flops 294912 | bytes 2359297 | tf_op jit(solution)/shard_map/jit(_where)/select_n | solution.py:99
  (47 shorter events, 3.5 us)
Async XLA Ops:
  0.6 23.9 %copy-start = (bf16[3,3,128,128]{3,2,1,0:T(8,128)(2,1)S(1)}, bf16[3,3,128,128]{3,2,1,0:T(8,128)(2,1)}, u32[]{:S(2)}) copy-start(bf16[3,3,128,128]{3,2,1,0:T(8,128)(2,1)} %param.5) | copy-start | bytes 884740
  0.6 20.5 %copy-start.2 = (bf16[16,64,128]{2,1,0:T(8,128)(2,1)S(1)}, bf16[16,64,128]{2,1,0:T(8,128)(2,1)}, u32[]{:S(2)}) copy-start(bf16[16,64,128]{2,1,0:T(8,128)(2,1)} %param.4) | copy-start | bytes 786436
  0.7 20.5 %copy-start.3 = (bf16[16,64,128]{2,1,0:T(8,128)(2,1)S(1)}, bf16[16,64,128]{2,1,0:T(8,128)(2,1)}, u32[]{:S(2)}) copy-start(bf16[16,64,128]{2,1,0:T(8,128)(2,1)} %param.7) | copy-start | bytes 786436
  1.6 11.9 %collective-permute-start = (bf16[2,16,2,128]{3,2,1,0:T(2,128)(2,1)S(1)}, bf16[2,16,2,128]{3,2,1,0:T(2,128)(2,1)S(1)}, u32[]{:S(2)}, u32[]{:S(2)}) collective-permute-start(bf16[2,16,2,128]{3,2,1,0:T(2,128)(2,1)S(1)} %get-tuple-element.9), channel_id=1, source_target_pairs={{0,16},{16,32},{32,48},{48,64},{64,80},{80,96},{96,112},{112,128},... | collective-permute-start | bytes 49160 | tf_op jit(solution)/shard_map/ppermute | solution.py:16
  6.1 7.4 %collective-permute-start.1 = (bf16[2,16,2,128]{3,2,1,0:T(2,128)(2,1)S(1)}, bf16[2,16,2,128]{3,2,1,0:T(2,128)(2,1)S(1)}, u32[]{:S(2)}, u32[]{:S(2)}) collective-permute-start(bf16[2,16,2,128]{3,2,1,0:T(2,128)(2,1)S(1)} %get-tuple-element.10), channel_id=1, source_target_pairs={{16,0},{32,16},{48,32},{64,48},{80,64},{96,80},{112,96},{128,112},... | collective-permute-start | bytes 49160 | tf_op jit(solution)/shard_map/ppermute | solution.py:19
  14.4 2.7 %collective-permute-start.2 = (bf16[2,2,68,128]{3,2,1,0:T(8,128)(2,1)S(1)}, bf16[2,2,68,128]{3,2,1,0:T(8,128)(2,1)S(1)}, u32[]{:S(2)}, u32[]{:S(2)}) collective-permute-start(bf16[2,2,68,128]{3,2,1,0:T(8,128)(2,1)S(1)} %get-tuple-element.7), channel_id=1, source_target_pairs={{0,1},{1,2},{2,3},{3,4},{4,5},{5,6},{6,7},{7,8},{8,9},{9,10},{10,1... | collective-permute-start | bytes 208904 | tf_op jit(solution)/shard_map/ppermute | solution.py:16
  15.7 5.5 %collective-permute-start.3 = (bf16[2,2,68,128]{3,2,1,0:T(8,128)(2,1)S(1)}, bf16[2,2,68,128]{3,2,1,0:T(8,128)(2,1)S(1)}, u32[]{:S(2)}, u32[]{:S(2)}) collective-permute-start(bf16[2,2,68,128]{3,2,1,0:T(8,128)(2,1)S(1)} %get-tuple-element.8), channel_id=1, source_target_pairs={{1,0},{2,1},{3,2},{4,3},{5,4},{6,5},{7,6},{8,7},{9,8},{10,9},{11,1... | collective-permute-start | bytes 208904 | tf_op jit(solution)/shard_map/ppermute | solution.py:19
  29.1 0.8 copy-start.1
  31.1 10.8 %collective-permute-start.4 = (f32[1152,128]{1,0:T(8,128)}, f32[1152,128]{1,0:T(8,128)}, u32[]{:S(2)}, u32[]{:S(2)}) collective-permute-start(f32[1152,128]{1,0:T(8,128)} %fusion.1), channel_id=1, source_target_pairs={{0,16},{16,0},{1,17},{17,1},{2,18},{18,2},{3,19},{19,3},{4,20},{20... | collective-permute-start | bytes 1769480 | tf_op jit(solution)/shard_map/ppermute | solution.py:86
  65.7 60.7 %copy-start.4 = (bf16[3,3,128,128]{3,2,1,0:T(8,128)(2,1)S(1)}, bf16[3,3,128,128]{3,2,1,0:T(8,128)(2,1)}, u32[]{:S(2)}) copy-start(bf16[3,3,128,128]{3,2,1,0:T(8,128)(2,1)} %param.6) | copy-start | bytes 884740
  120.2 8.0 %collective-permute-start.5 = (f32[1152,128]{1,0:T(8,128)S(1)}, f32[1152,128]{1,0:T(8,128)}, u32[]{:S(2)}, u32[]{:S(2)}) collective-permute-start(f32[1152,128]{1,0:T(8,128)S(1)} %bitcast.38), channel_id=1, source_target_pairs={{0,16},{16,0},{1,17},{17,1},{2,18},{18,2},{3,19},{19,3},{4,20},{20... | collective-permute-start | bytes 1769480 | tf_op jit(solution)/shard_map/ppermute | solution.py:86

commit v6 on v5

--- a/solution.py
+++ b/solution.py
@@ -53,33 +53,40 @@
     return in_order(sent_to_all(x, axis), dim)
 
 
-def windows(padded, rows_out, cols_out):
-    taps = [
-        padded[row_tap : row_tap + rows_out, col_tap : col_tap + cols_out]
-        for row_tap in range(3)
-        for col_tap in range(3)
-    ]
-    return jnp.concatenate(taps, axis=-1).reshape(rows_out * cols_out, 9 * padded.shape[2])
+def column_taps(padded, cols_out):
+    return jnp.concatenate(
+        [padded[:, col_tap : col_tap + cols_out] for col_tap in range(3)], axis=-1
+    )
 
 
 def conv_tile(padded, weights):
     rows_out = padded.shape[0] - 2
     cols_out = padded.shape[1] - 2
-    stacked = windows(padded, rows_out, cols_out)
-    summed = jnp.dot(
-        stacked, weights.reshape(-1, weights.shape[3]), preferred_element_type=jnp.float32
-    )
-    return summed.reshape(rows_out, cols_out, weights.shape[3])
+    stacked = column_taps(padded, cols_out)
+    summed = None
+    for row_tap in range(3):
+        part = jnp.dot(
+            stacked[row_tap : row_tap + rows_out],
+            weights[row_tap].reshape(-1, weights.shape[3]),
+            preferred_element_type=jnp.float32,
+        )
+        summed = part if summed is None else summed + part
+    return summed
 
 
 def weight_terms(padded, gradient):
     rows_out, cols_out, channels = gradient.shape
-    flat_grad = gradient.reshape(rows_out * cols_out, channels)
-    stacked = windows(padded, rows_out, cols_out)
-    terms = lax.dot_general(
-        stacked, flat_grad, (((0,), (0,)), ((), ())), preferred_element_type=jnp.float32
-    )
-    return terms.reshape(3, 3, padded.shape[2], channels)
+    stacked = column_taps(padded, cols_out)
+    taps = [
+        lax.dot_general(
+            stacked[row_tap : row_tap + rows_out],
+            gradient,
+            (((0, 1), (0, 1)), ((), ())),
+            preferred_element_type=jnp.float32,
+        )
+        for row_tap in range(3)
+    ]
+    return jnp.stack(taps).reshape(3, 3, padded.shape[2], channels)
 
 
 def with_partner(x):

time: 131 us -> 122 us (0.931)
  the two profiles are of different devices: /device:TPU:1 before, /device:TPU:9 now
where the time goes in v6:
time: 122 us
  blocking collectives  55.6 us (46%)
  waiting for transfers between devices  28.8 us (24%)
  starting transfers between devices  23.9 us (20%)
  matrix products  6.91 us (6%)
  other arithmetic  3.16 us (3%)
  local copies, waits for them, and re-layouts  2.37 us (2%)
    all_to_all x1, blocking collectives, sent_to_all(): return lax.all_to_all(copies, axis, split_axis=0, concat_axis=0, tiled=True)  28.3 us
    all_to_all x1, blocking collectives, sent_and_summed(): lax.all_to_all(blocks, axis, split_axis=0, concat_axis=0, tiled=True)  27.4 us
    all_to_all x1, waiting for transfers between devices, sent_to_all(): return lax.all_to_all(copies, axis, split_axis=0, concat_axis=0, tiled=True)  19.8 us
    ppermute x2, starting transfers between devices, with_partner(): return lax.ppermute(x, 'core', [(0, 1), (1, 0)])  8.46 us
    ppermute x2, starting transfers between devices, with_halo(): lax.ppermute(lax.slice_in_dim(block, block.shape[dim] - width, None, axis...  7.57 us
    ppermute x2, waiting for transfers between devices, with_halo(): lax.ppermute(lax.slice_in_dim(block, 0, width, axis=dim), axis, backward)  7.37 us
    dot_general x9, matrix products, conv_tile(): jnp.dot(stacked[row_tap:row_tap + rows_out], weights[row_tap].reshape(-1,...  4.49 us
    all_to_all x1, starting transfers between devices, sent_to_all(): return lax.all_to_all(copies, axis, split_axis=0, concat_axis=0, tiled=True)  4.06 us
  transfers between devices with their start and end apart: 7, of which 4 were waited for; matrix products, arithmetic and copies ran while one was open for 2% of the time, Pallas kernels for 0%

profile of v6, /device:TPU:9, one launch (start us, length us, event | category | flops | bytes accessed | tf_op | source)
XLA Modules:
  0.0 121.8 jit_solution(11325376287969633284)
XLA Ops:
  0.7 0.9 pad_maximum_fusion.12
  1.6 3.7 %collective-permute-start = (bf16[2,16,2,128]{3,2,1,0:T(2,128)(2,1)S(1)}, bf16[2,16,2,128]{3,2,1,0:T(2,128)(2,1)S(1)}, u32[]{:S(2)}, u32[]{:S(2)}) collective-permute-start(bf16[2,16,2,128]{3,2,1,0:T(2,128)(2,1)S(1)} %get-tuple-element.9), channel_id=1, source_target_pairs={{0,16},{16,32},{32,48},{48,64},{64,80},{80,96},{96,112},{112,128},... | collective-permute-start | bytes 49160 | tf_op jit(solution)/shard_map/ppermute | solution.py:16
  5.2 1.9 %collective-permute-start.1 = (bf16[2,16,2,128]{3,2,1,0:T(2,128)(2,1)S(1)}, bf16[2,16,2,128]{3,2,1,0:T(2,128)(2,1)S(1)}, u32[]{:S(2)}, u32[]{:S(2)}) collective-permute-start(bf16[2,16,2,128]{3,2,1,0:T(2,128)(2,1)S(1)} %get-tuple-element.10), channel_id=1, source_target_pairs={{16,0},{32,16},{48,32},{64,48},{80,64},{96,80},{112,96},{128,112},... | collective-permute-start | bytes 49160 | tf_op jit(solution)/shard_map/ppermute | solution.py:19
  7.7 2.9 %collective-permute-done.1 = bf16[2,16,2,128]{3,2,1,0:T(2,128)(2,1)S(1)} collective-permute-done((bf16[2,16,2,128]{3,2,1,0:T(2,128)(2,1)S(1)}, bf16[2,16,2,128]{3,2,1,0:T(2,128)(2,1)S(1)}, u32[]{:S(2)}, u32[]{:S(2)}) %collective-permute-start.1) | collective-permute-done | bytes 16416 | tf_op jit(solution)/shard_map/ppermute | solution.py:19
  10.7 3.9 %collective-permute-start.2 = (bf16[2,2,68,128]{3,2,1,0:T(8,128)(2,1)S(1)}, bf16[2,2,68,128]{3,2,1,0:T(8,128)(2,1)S(1)}, u32[]{:S(2)}, u32[]{:S(2)}) collective-permute-start(bf16[2,2,68,128]{3,2,1,0:T(8,128)(2,1)S(1)} %get-tuple-element.7), channel_id=1, source_target_pairs={{0,1},{1,2},{2,3},{3,4},{4,5},{5,6},{6,7},{7,8},{8,9},{9,10},{10,1... | collective-permute-start | bytes 208904 | tf_op jit(solution)/shard_map/ppermute | solution.py:16
  14.5 1.9 %collective-permute-start.3 = (bf16[2,2,68,128]{3,2,1,0:T(8,128)(2,1)S(1)}, bf16[2,2,68,128]{3,2,1,0:T(8,128)(2,1)S(1)}, u32[]{:S(2)}, u32[]{:S(2)}) collective-permute-start(bf16[2,2,68,128]{3,2,1,0:T(8,128)(2,1)S(1)} %get-tuple-element.8), channel_id=1, source_target_pairs={{1,0},{2,1},{3,2},{4,3},{5,4},{6,5},{7,6},{8,7},{9,8},{10,9},{11,1... | collective-permute-start | bytes 208904 | tf_op jit(solution)/shard_map/ppermute | solution.py:19
  16.5 4.5 %collective-permute-done.3 = bf16[2,2,68,128]{3,2,1,0:T(8,128)(2,1)S(1)} collective-permute-done((bf16[2,2,68,128]{3,2,1,0:T(8,128)(2,1)S(1)}, bf16[2,2,68,128]{3,2,1,0:T(8,128)(2,1)S(1)}, u32[]{:S(2)}, u32[]{:S(2)}) %collective-permute-start.3) | collective-permute-done | bytes 69664 | tf_op jit(solution)/shard_map/ppermute | solution.py:19
  21.6 0.5 fusion.8
  22.1 0.5 convolution_add_fusion.1
  22.6 0.5 fusion.6
  23.3 0.4 convolution_bitcast_fusion.1
  23.7 0.4 convolution_bitcast_fusion
  24.1 0.4 convolution_bitcast_fusion.2
  24.5 0.5 fusion.10
  25.1 0.4 fusion.7
  25.4 0.4 convolution_add_fusion.3
  25.8 0.4 fusion.1
  26.2 0.4 convolution_bitcast_fusion.3
  26.6 0.4 convolution_bitcast_fusion.4
  27.1 0.4 convolution_bitcast_fusion.5
  27.9 5.7 %collective-permute-start.4 = (f32[1152,128]{1,0:T(8,128)S(1)}, f32[1152,128]{1,0:T(8,128)S(1)}, u32[]{:S(2)}, u32[]{:S(2)}) collective-permute-start(f32[1152,128]{1,0:T(8,128)S(1)} %fusion.3), channel_id=1, source_target_pairs={{0,16},{16,0},{1,17},{17,1},{2,18},{18,2},{3,19},{19,3},{4,20},{20... | collective-permute-start | bytes 1769480 | tf_op jit(solution)/shard_map/ppermute | solution.py:93
  33.7 1.6 %collective-permute-done.4 = f32[1152,128]{1,0:T(8,128)S(1)} collective-permute-done((f32[1152,128]{1,0:T(8,128)S(1)}, f32[1152,128]{1,0:T(8,128)S(1)}, u32[]{:S(2)}, u32[]{:S(2)}) %collective-permute-start.4) | collective-permute-done | bytes 589856 | tf_op jit(solution)/shard_map/ppermute | solution.py:93
  35.6 27.4 %all_to_all.15 = f32[16,72,128]{2,1,0:T(8,128)S(1)} all-to-all(f32[16,72,128]{2,1,0:T(8,128)S(1)} %bitcast.81), channel_id=1, replica_groups=mesh['lon_chip'=16,'core'=2,'lat'=16] {'lon_chip'}, dimensions={0} | all-to-all | bytes 1179648 | tf_op jit(solution)/shard_map/all_to_all | solution.py:32
  63.1 28.3 %all_to_all.16 = f32[16,72,128]{2,1,0:T(8,128)S(1)} all-to-all(f32[16,72,128]{2,1,0:T(8,128)S(1)} %broadcast_in_dim.20), channel_id=1, replica_groups=mesh['lon_chip'=16,'core'=2,'lat'=16] {'lat'}, dimensions={0} | all-to-all | bytes 1179648 | tf_op jit(solution)/shard_map/all_to_all | solution.py:38
  91.4 0.9 broadcast_in_dim.21
  92.2 4.1 %all-to-all-start.2 = ((f32[16,72,128]{2,1,0:T(8,128)}), f32[16,72,128]{2,1,0:T(8,128)S(1)}, u32[]{:S(2)}, u32[]{:S(2)}) async-start(f32[16,72,128]{2,1,0:T(8,128)} %broadcast_in_dim.21), calls=%async_computation.2 | async-start | bytes 1179648 | tf_op jit(solution)/shard_map/all_to_all | solution.py:38
  96.3 19.8 %all-to-all-done.2 = f32[16,72,128]{2,1,0:T(8,128)S(1)} async-done(((f32[16,72,128]{2,1,0:T(8,128)}), f32[16,72,128]{2,1,0:T(8,128)S(1)}, u32[]{:S(2)}, u32[]{:S(2)}) %all-to-all-start.2) | async-done | bytes 589856 | tf_op jit(solution)/shard_map/all_to_all | solution.py:38
  116.2 2.7 %collective-permute-start.5 = (f32[1152,128]{1,0:T(8,128)S(1)}, f32[1152,128]{1,0:T(8,128)S(1)}, u32[]{:S(2)}, u32[]{:S(2)}) collective-permute-start(f32[1152,128]{1,0:T(8,128)S(1)} %bitcast.80), channel_id=1, source_target_pairs={{0,16},{16,0},{1,17},{17,1},{2,18},{18,2},{3,19},{19,3},{4,20},{20... | collective-permute-start | bytes 1769480 | tf_op jit(solution)/shard_map/ppermute | solution.py:93
  118.9 0.4 fusion.9
  119.3 0.4 convolution_add_fusion.5
  119.7 1.1 fusion.2
  120.7 1.1 broadcast_select_fusion
  (31 shorter events, 2.2 us)
Async XLA Ops:
  0.6 6.5 %copy-start.2 = (bf16[3,3,128,128]{3,2,1,0:T(8,128)(2,1)S(1)}, bf16[3,3,128,128]{3,2,1,0:T(8,128)(2,1)}, u32[]{:S(2)}) copy-start(bf16[3,3,128,128]{3,2,1,0:T(8,128)(2,1)} %param.6) | copy-start | bytes 884740
  0.6 6.6 %copy-start.3 = (bf16[3,3,128,128]{3,2,1,0:T(8,128)(2,1)S(1)}, bf16[3,3,128,128]{3,2,1,0:T(8,128)(2,1)}, u32[]{:S(2)}) copy-start(bf16[3,3,128,128]{3,2,1,0:T(8,128)(2,1)} %param.5) | copy-start | bytes 884740
  1.6 6.2 %collective-permute-start = (bf16[2,16,2,128]{3,2,1,0:T(2,128)(2,1)S(1)}, bf16[2,16,2,128]{3,2,1,0:T(2,128)(2,1)S(1)}, u32[]{:S(2)}, u32[]{:S(2)}) collective-permute-start(bf16[2,16,2,128]{3,2,1,0:T(2,128)(2,1)S(1)} %get-tuple-element.9), channel_id=1, source_target_pairs={{0,16},{16,32},{32,48},{48,64},{64,80},{80,96},{96,112},{112,128},... | collective-permute-start | bytes 49160 | tf_op jit(solution)/shard_map/ppermute | solution.py:16
  5.2 5.4 %collective-permute-start.1 = (bf16[2,16,2,128]{3,2,1,0:T(2,128)(2,1)S(1)}, bf16[2,16,2,128]{3,2,1,0:T(2,128)(2,1)S(1)}, u32[]{:S(2)}, u32[]{:S(2)}) collective-permute-start(bf16[2,16,2,128]{3,2,1,0:T(2,128)(2,1)S(1)} %get-tuple-element.10), channel_id=1, source_target_pairs={{16,0},{32,16},{48,32},{64,48},{80,64},{96,80},{112,96},{128,112},... | collective-permute-start | bytes 49160 | tf_op jit(solution)/shard_map/ppermute | solution.py:19
  7.2 3.3 %copy-start = (bf16[16,64,128]{2,1,0:T(8,128)(2,1)S(1)}, bf16[16,64,128]{2,1,0:T(8,128)(2,1)}, u32[]{:S(2)}) copy-start(bf16[16,64,128]{2,1,0:T(8,128)(2,1)} %param.4) | copy-start | bytes 786436
  7.3 3.3 %copy-start.1 = (bf16[16,64,128]{2,1,0:T(8,128)(2,1)S(1)}, bf16[16,64,128]{2,1,0:T(8,128)(2,1)}, u32[]{:S(2)}) copy-start(bf16[16,64,128]{2,1,0:T(8,128)(2,1)} %param.7) | copy-start | bytes 786436
  10.7 5.8 %collective-permute-start.2 = (bf16[2,2,68,128]{3,2,1,0:T(8,128)(2,1)S(1)}, bf16[2,2,68,128]{3,2,1,0:T(8,128)(2,1)S(1)}, u32[]{:S(2)}, u32[]{:S(2)}) collective-permute-start(bf16[2,2,68,128]{3,2,1,0:T(8,128)(2,1)S(1)} %get-tuple-element.7), channel_id=1, source_target_pairs={{0,1},{1,2},{2,3},{3,4},{4,5},{5,6},{6,7},{7,8},{8,9},{9,10},{10,1... | collective-permute-start | bytes 208904 | tf_op jit(solution)/shard_map/ppermute | solution.py:16
  14.5 6.5 %collective-permute-start.3 = (bf16[2,2,68,128]{3,2,1,0:T(8,128)(2,1)S(1)}, bf16[2,2,68,128]{3,2,1,0:T(8,128)(2,1)S(1)}, u32[]{:S(2)}, u32[]{:S(2)}) collective-permute-start(bf16[2,2,68,128]{3,2,1,0:T(8,128)(2,1)S(1)} %get-tuple-element.8), channel_id=1, source_target_pairs={{1,0},{2,1},{3,2},{4,3},{5,4},{6,5},{7,6},{8,7},{9,8},{10,9},{11,1... | collective-permute-start | bytes 208904 | tf_op jit(solution)/shard_map/ppermute | solution.py:19
  27.9 7.3 %collective-permute-start.4 = (f32[1152,128]{1,0:T(8,128)S(1)}, f32[1152,128]{1,0:T(8,128)S(1)}, u32[]{:S(2)}, u32[]{:S(2)}) collective-permute-start(f32[1152,128]{1,0:T(8,128)S(1)} %fusion.3), channel_id=1, source_target_pairs={{0,16},{16,0},{1,17},{17,1},{2,18},{18,2},{3,19},{19,3},{4,20},{20... | collective-permute-start | bytes 1769480 | tf_op jit(solution)/shard_map/ppermute | solution.py:93
  92.2 23.9 %all-to-all-start.2 = ((f32[16,72,128]{2,1,0:T(8,128)}), f32[16,72,128]{2,1,0:T(8,128)S(1)}, u32[]{:S(2)}, u32[]{:S(2)}) async-start(f32[16,72,128]{2,1,0:T(8,128)} %broadcast_in_dim.21), calls=%async_computation.2 | async-start | bytes 1179648 | tf_op jit(solution)/shard_map/all_to_all | solution.py:38
  116.2 4.6 %collective-permute-start.5 = (f32[1152,128]{1,0:T(8,128)S(1)}, f32[1152,128]{1,0:T(8,128)S(1)}, u32[]{:S(2)}, u32[]{:S(2)}) collective-permute-start(f32[1152,128]{1,0:T(8,128)S(1)} %bitcast.80), channel_id=1, source_target_pairs={{0,16},{16,0},{1,17},{17,1},{2,18},{18,2},{3,19},{19,3},{4,20},{20... | collective-permute-start | bytes 1769480 | tf_op jit(solution)/shard_map/ppermute | solution.py:93

commit v7 on v6

--- a/solution.py
+++ b/solution.py
@@ -4,6 +4,7 @@
 from jax.sharding import Mesh, PartitionSpec as P
 
 LON = ("lon_chip", "core")
+LAT = ("lat_z", "lat_pair")
 
 
 def with_halo(block, sides, width, periodic):
@@ -93,17 +94,23 @@
     return lax.ppermute(x, "core", [(0, 1), (1, 0)])
 
 
-def reduced_everywhere(terms):
+def reduced_everywhere(terms, decoded):
     core = lax.axis_index("core")
     half = terms.shape[0] // 2
     mine = lax.dynamic_slice_in_dim(terms, core * half, half, 0)
     other = lax.dynamic_slice_in_dim(terms, (1 - core) * half, half, 0)
-    chip_sum = mine + with_partner(other)
+    received, decoded = lax.optimization_barrier((with_partner(other), decoded))
+    chip_sum = mine + received
     portion = sent_and_summed(chip_sum, "lon_chip", 0)
-    portion = taken_together(portion, "lat")
+    portion = portion + lax.ppermute(portion, "lat_pair", [(0, 1), (1, 0)])
+    portion = taken_together(portion, "lat_z")
     gathered = collect(portion, "lon_chip", 0)
     partner = with_partner(gathered)
-    return jnp.where(core == 0, gathered, partner), jnp.where(core == 0, partner, gathered)
+    return (
+        decoded,
+        jnp.where(core == 0, gathered, partner),
+        jnp.where(core == 0, partner, gathered),
+    )
 
 
 def shards(latent_frame, weights_in, weights_out, cotangent):
@@ -112,13 +119,13 @@
     stacked = jnp.stack([latent_frame, cotangent])
     margin = 2
     widened = with_halo(stacked, ((LON, 2),), margin, True)
-    extended = with_halo(widened, (("lat", 1),), margin, False)
+    extended = with_halo(widened, ((LAT, 1),), margin, False)
     input_pad = extended[0]
     grad_pad = extended[1][1:-1, 1:-1]
     preact_wide = conv_tile(input_pad, weights_in)
     hidden_wide = jax.nn.silu(preact_wide).astype(jnp.bfloat16)
-    global_row = lax.axis_index("lat") * tile_rows - 1 + jnp.arange(tile_rows + 2, dtype=jnp.int32)
-    inside = (global_row >= 0) & (global_row < tile_rows * lax.axis_size("lat"))
+    global_row = lax.axis_index(LAT) * tile_rows - 1 + jnp.arange(tile_rows + 2, dtype=jnp.int32)
+    inside = (global_row >= 0) & (global_row < tile_rows * lax.axis_size(LAT))
     hidden_pad = jnp.where(inside[:, None, None], hidden_wide, jnp.zeros_like(hidden_wide))
     preact = preact_wide[1:-1, 1:-1]
     input_use = input_pad[1:-1, 1:-1]
@@ -135,7 +142,7 @@
     all_terms = jnp.concatenate(
         [term_in.reshape(9 * channels, channels), term_out.reshape(9 * channels, channels)], axis=0
     )
-    grad_in, grad_out = reduced_everywhere(all_terms)
+    decoded, grad_in, grad_out = reduced_everywhere(all_terms, decoded)
     grad_in = grad_in.reshape(3, 3, channels, channels)
     grad_out = grad_out.reshape(3, 3, channels, channels)
     return (decoded, grad_in, grad_out)
@@ -143,8 +150,8 @@
 
 def solution(mesh):
     n_lon, n_lat = mesh.shape["lon"], mesh.shape["lat"]
-    split = Mesh(mesh.devices.reshape(n_lon // 2, 2, n_lat), (*LON, "lat"))
-    tiled = P("lat", LON, None)
+    split = Mesh(mesh.devices.reshape(n_lon // 2, 2, n_lat // 2, 2), (*LON, *LAT))
+    tiled = P(LAT, LON, None)
     return jax.shard_map(
         shards,
         mesh=split,

time: 122 us -> 118 us (0.967)
  the two profiles are of different devices: /device:TPU:9 before, /device:TPU:1 now
where the time goes in v7:
time: 118 us
  blocking collectives  60.6 us (51%)
  starting transfers between devices  36.6 us (31%)
  waiting for transfers between devices  7.42 us (6%)
  matrix products  6.93 us (6%)
  other arithmetic  3.15 us (3%)
  local copies, waits for them, and re-layouts  1.86 us (2%)
    all_to_all x2, blocking collectives, sent_to_all(): return lax.all_to_all(copies, axis, split_axis=0, concat_axis=0, tiled=True)  38.2 us
    all_to_all x1, blocking collectives, sent_and_summed(): lax.all_to_all(blocks, axis, split_axis=0, concat_axis=0, tiled=True)  22.4 us
    ppermute x2, starting transfers between devices, with_partner(): return lax.ppermute(x, 'core', [(0, 1), (1, 0)])  17 us
    ppermute x2, starting transfers between devices, with_halo(): lax.ppermute(lax.slice_in_dim(block, 0, width, axis=dim), axis, backward)  7.46 us
    ppermute x1, starting transfers between devices, reduced_everywhere(): portion = portion + lax.ppermute(portion, 'lat_pair', [(0, 1), (1, 0)])  6.36 us
    ppermute x2, starting transfers between devices, with_halo(): lax.ppermute(lax.slice_in_dim(block, block.shape[dim] - width, None, axis...  5.79 us
    dot_general x9, matrix products, conv_tile(): jnp.dot(stacked[row_tap:row_tap + rows_out], weights[row_tap].reshape(-1,...  4.5 us
    ppermute x2, waiting for transfers between devices, with_halo(): lax.ppermute(lax.slice_in_dim(block, 0, width, axis=dim), axis, backward)  4.41 us
  transfers between devices with their start and end apart: 7, of which 5 were waited for; matrix products, arithmetic and copies ran while one was open for 2% of the time, Pallas kernels for 0%

profile of v7, /device:TPU:1, one launch (start us, length us, event | category | flops | bytes accessed | tf_op | source)
XLA Modules:
  0.0 117.6 jit_solution(15812506300384395410)
XLA Ops:
  0.7 0.9 pad_maximum_fusion.12
  1.6 4.5 %collective-permute-start = (bf16[2,16,2,128]{3,2,1,0:T(2,128)(2,1)S(1)}, bf16[2,16,2,128]{3,2,1,0:T(2,128)(2,1)S(1)}, u32[]{:S(2)}, u32[]{:S(2)}) collective-permute-start(bf16[2,16,2,128]{3,2,1,0:T(2,128)(2,1)S(1)} %get-tuple-element.13), channel_id=1, source_target_pairs={{0,16},{16,32},{32,48},{48,64},{64,80},{80,96},{96,112},{112,128},... | collective-permute-start | bytes 49160 | tf_op jit(solution)/shard_map/ppermute | solution.py:17
  6.1 6.2 %collective-permute-start.1 = (bf16[2,16,2,128]{3,2,1,0:T(2,128)(2,1)S(1)}, bf16[2,16,2,128]{3,2,1,0:T(2,128)(2,1)S(1)}, u32[]{:S(2)}, u32[]{:S(2)}) collective-permute-start(bf16[2,16,2,128]{3,2,1,0:T(2,128)(2,1)S(1)} %get-tuple-element.14), channel_id=1, source_target_pairs={{16,0},{32,16},{48,32},{64,48},{80,64},{96,80},{112,96},{128,112},... | collective-permute-start | bytes 49160 | tf_op jit(solution)/shard_map/ppermute | solution.py:20
  13.4 1.3 %collective-permute-start.2 = (bf16[2,2,68,128]{3,2,1,0:T(8,128)(2,1)S(1)}, bf16[2,2,68,128]{3,2,1,0:T(8,128)(2,1)S(1)}, u32[]{:S(2)}, u32[]{:S(2)}) collective-permute-start(bf16[2,2,68,128]{3,2,1,0:T(8,128)(2,1)S(1)} %get-tuple-element.11), channel_id=1, source_target_pairs={{0,1},{1,2},{2,3},{3,4},{4,5},{5,6},{6,7},{7,8},{8,9},{9,10},{10,1... | collective-permute-start | bytes 208904 | tf_op jit(solution)/shard_map/ppermute | solution.py:17
  14.7 1.3 %collective-permute-start.3 = (bf16[2,2,68,128]{3,2,1,0:T(8,128)(2,1)S(1)}, bf16[2,2,68,128]{3,2,1,0:T(8,128)(2,1)S(1)}, u32[]{:S(2)}, u32[]{:S(2)}) collective-permute-start(bf16[2,2,68,128]{3,2,1,0:T(8,128)(2,1)S(1)} %get-tuple-element.12), channel_id=1, source_target_pairs={{1,0},{2,1},{3,2},{4,3},{5,4},{6,5},{7,6},{8,7},{9,8},{10,9},{11,1... | collective-permute-start | bytes 208904 | tf_op jit(solution)/shard_map/ppermute | solution.py:20
  16.1 4.2 %collective-permute-done.3 = bf16[2,2,68,128]{3,2,1,0:T(8,128)(2,1)S(1)} collective-permute-done((bf16[2,2,68,128]{3,2,1,0:T(8,128)(2,1)S(1)}, bf16[2,2,68,128]{3,2,1,0:T(8,128)(2,1)S(1)}, u32[]{:S(2)}, u32[]{:S(2)}) %collective-permute-start.3) | collective-permute-done | bytes 69664 | tf_op jit(solution)/shard_map/ppermute | solution.py:20
  20.9 0.5 fusion.8
  21.4 0.5 convolution_add_fusion.1
  21.9 0.5 fusion.6
  22.6 0.4 convolution_bitcast_fusion.2
  23.0 0.4 convolution_bitcast_fusion.1
  23.4 0.4 convolution_bitcast_fusion
  23.8 0.5 fusion.10
  24.4 0.4 fusion.7
  24.7 0.4 convolution_add_fusion.5
  25.1 0.4 fusion.1
  25.5 0.4 convolution_bitcast_fusion.5
  26.0 0.4 convolution_bitcast_fusion.4
  26.4 0.4 convolution_bitcast_fusion.3
  26.9 0.4 fusion.5
  27.2 8.8 %collective-permute-start.4 = (f32[1152,128]{1,0:T(8,128)S(1)}, f32[1152,128]{1,0:T(8,128)S(1)}, u32[]{:S(2)}, u32[]{:S(2)}) collective-permute-start(f32[1152,128]{1,0:T(8,128)S(1)} %fusion.5), channel_id=1, source_target_pairs={{0,16},{16,0},{1,17},{17,1},{2,18},{18,2},{3,19},{19,3},{4,20},{20... | collective-permute-start | bytes 1769480 | tf_op jit(solution)/shard_map/ppermute | solution.py:94
  36.0 0.4 fusion.9
  36.4 0.4 convolution_add_fusion.3
  36.8 1.1 fusion.2
  38.2 22.4 %all_to_all.15 = f32[16,72,128]{2,1,0:T(8,128)S(1)} all-to-all(f32[16,72,128]{2,1,0:T(8,128)S(1)} %bitcast.81), channel_id=1, replica_groups=mesh['lon_chip'=16,'core'=2,'lat_z'=8,'lat_pair'=2] {'lon_chip'}, dimensions={0} | all-to-all | bytes 1179648 | tf_op jit(solution)/shard_map/all_to_all | solution.py:33
  60.7 6.4 %collective-permute-start.5 = (f32[72,128]{1,0:T(8,128)S(1)}, f32[72,128]{1,0:T(8,128)S(1)}, u32[]{:S(2)}, u32[]{:S(2)}) collective-permute-start(f32[72,128]{1,0:T(8,128)S(1)} %reduce_sum.18), channel_id=1, source_target_pairs={{0,1},{1,0},{2,3},{3,2},{4,5},{5,4},{6,7},{7,6},{8,9},{9,8},{10,11... | collective-permute-start | bytes 110600 | tf_op jit(solution)/shard_map/ppermute | solution.py:105
  67.0 1.3 %collective-permute-done.5 = f32[72,128]{1,0:T(8,128)S(1)} collective-permute-done((f32[72,128]{1,0:T(8,128)S(1)}, f32[72,128]{1,0:T(8,128)S(1)}, u32[]{:S(2)}, u32[]{:S(2)}) %collective-permute-start.5) | collective-permute-done | bytes 36896 | tf_op jit(solution)/shard_map/ppermute | solution.py:105
  68.4 18.7 %all_to_all.16 = f32[8,72,128]{2,1,0:T(8,128)S(1)} all-to-all(f32[8,72,128]{2,1,0:T(8,128)S(1)} %broadcast_in_dim.20), channel_id=1, replica_groups=mesh['lon_chip'=16,'core'=2,'lat_z'=8,'lat_pair'=2] {'lat_z'}, dimensions={0} | all-to-all | bytes 589824 | tf_op jit(solution)/shard_map/all_to_all | solution.py:39
  87.2 19.5 %all_to_all.17 = f32[16,72,128]{2,1,0:T(8,128)S(1)} all-to-all(f32[16,72,128]{2,1,0:T(8,128)S(1)} %broadcast_in_dim.21), channel_id=1, replica_groups=mesh['lon_chip'=16,'core'=2,'lat_z'=8,'lat_pair'=2] {'lon_chip'}, dimensions={0} | all-to-all | bytes 1179648 | tf_op jit(solution)/shard_map/all_to_all | solution.py:39
  106.6 8.2 %collective-permute-start.6 = (f32[1152,128]{1,0:T(8,128)S(1)}, f32[1152,128]{1,0:T(8,128)S(1)}, u32[]{:S(2)}, u32[]{:S(2)}) collective-permute-start(f32[1152,128]{1,0:T(8,128)S(1)} %bitcast.80), channel_id=1, source_target_pairs={{0,16},{16,0},{1,17},{17,1},{2,18},{18,2},{3,19},{19,3},{4,20},{20... | collective-permute-start | bytes 1769480 | tf_op jit(solution)/shard_map/ppermute | solution.py:94
  114.9 1.6 %collective-permute-done.6 = f32[1152,128]{1,0:T(8,128)S(1)} collective-permute-done((f32[1152,128]{1,0:T(8,128)S(1)}, f32[1152,128]{1,0:T(8,128)S(1)}, u32[]{:S(2)}, u32[]{:S(2)}) %collective-permute-start.6) | collective-permute-done | bytes 589856 | tf_op jit(solution)/shard_map/ppermute | solution.py:94
  116.5 1.1 broadcast_select_fusion
  (33 shorter events, 2.5 us)
Async XLA Ops:
  0.6 11.6 %copy-start.2 = (bf16[3,3,128,128]{3,2,1,0:T(8,128)(2,1)S(1)}, bf16[3,3,128,128]{3,2,1,0:T(8,128)(2,1)}, u32[]{:S(2)}) copy-start(bf16[3,3,128,128]{3,2,1,0:T(8,128)(2,1)} %param.6) | copy-start | bytes 884740
  0.6 11.7 %copy-start.3 = (bf16[3,3,128,128]{3,2,1,0:T(8,128)(2,1)S(1)}, bf16[3,3,128,128]{3,2,1,0:T(8,128)(2,1)}, u32[]{:S(2)}) copy-start(bf16[3,3,128,128]{3,2,1,0:T(8,128)(2,1)} %param.5) | copy-start | bytes 884740
  1.6 11.3 %collective-permute-start = (bf16[2,16,2,128]{3,2,1,0:T(2,128)(2,1)S(1)}, bf16[2,16,2,128]{3,2,1,0:T(2,128)(2,1)S(1)}, u32[]{:S(2)}, u32[]{:S(2)}) collective-permute-start(bf16[2,16,2,128]{3,2,1,0:T(2,128)(2,1)S(1)} %get-tuple-element.13), channel_id=1, source_target_pairs={{0,16},{16,32},{32,48},{48,64},{64,80},{80,96},{96,112},{112,128},... | collective-permute-start | bytes 49160 | tf_op jit(solution)/shard_map/ppermute | solution.py:17
  6.1 7.0 %collective-permute-start.1 = (bf16[2,16,2,128]{3,2,1,0:T(2,128)(2,1)S(1)}, bf16[2,16,2,128]{3,2,1,0:T(2,128)(2,1)S(1)}, u32[]{:S(2)}, u32[]{:S(2)}) collective-permute-start(bf16[2,16,2,128]{3,2,1,0:T(2,128)(2,1)S(1)} %get-tuple-element.14), channel_id=1, source_target_pairs={{16,0},{32,16},{48,32},{64,48},{80,64},{96,80},{112,96},{128,112},... | collective-permute-start | bytes 49160 | tf_op jit(solution)/shard_map/ppermute | solution.py:20
  12.3 1.0 copy-start
  12.4 1.0 copy-start.1
  13.4 2.7 %collective-permute-start.2 = (bf16[2,2,68,128]{3,2,1,0:T(8,128)(2,1)S(1)}, bf16[2,2,68,128]{3,2,1,0:T(8,128)(2,1)S(1)}, u32[]{:S(2)}, u32[]{:S(2)}) collective-permute-start(bf16[2,2,68,128]{3,2,1,0:T(8,128)(2,1)S(1)} %get-tuple-element.11), channel_id=1, source_target_pairs={{0,1},{1,2},{2,3},{3,4},{4,5},{5,6},{6,7},{7,8},{8,9},{9,10},{10,1... | collective-permute-start | bytes 208904 | tf_op jit(solution)/shard_map/ppermute | solution.py:17
  14.7 5.6 %collective-permute-start.3 = (bf16[2,2,68,128]{3,2,1,0:T(8,128)(2,1)S(1)}, bf16[2,2,68,128]{3,2,1,0:T(8,128)(2,1)S(1)}, u32[]{:S(2)}, u32[]{:S(2)}) collective-permute-start(bf16[2,2,68,128]{3,2,1,0:T(8,128)(2,1)S(1)} %get-tuple-element.12), channel_id=1, source_target_pairs={{1,0},{2,1},{3,2},{4,3},{5,4},{6,5},{7,6},{8,7},{9,8},{10,9},{11,1... | collective-permute-start | bytes 208904 | tf_op jit(solution)/shard_map/ppermute | solution.py:20
  27.2 10.6 %collective-permute-start.4 = (f32[1152,128]{1,0:T(8,128)S(1)}, f32[1152,128]{1,0:T(8,128)S(1)}, u32[]{:S(2)}, u32[]{:S(2)}) collective-permute-start(f32[1152,128]{1,0:T(8,128)S(1)} %fusion.5), channel_id=1, source_target_pairs={{0,16},{16,0},{1,17},{17,1},{2,18},{18,2},{3,19},{19,3},{4,20},{20... | collective-permute-start | bytes 1769480 | tf_op jit(solution)/shard_map/ppermute | solution.py:94
  60.7 7.7 %collective-permute-start.5 = (f32[72,128]{1,0:T(8,128)S(1)}, f32[72,128]{1,0:T(8,128)S(1)}, u32[]{:S(2)}, u32[]{:S(2)}) collective-permute-start(f32[72,128]{1,0:T(8,128)S(1)} %reduce_sum.18), channel_id=1, source_target_pairs={{0,1},{1,0},{2,3},{3,2},{4,5},{5,4},{6,7},{7,6},{8,9},{9,8},{10,11... | collective-permute-start | bytes 110600 | tf_op jit(solution)/shard_map/ppermute | solution.py:105
  106.6 9.8 %collective-permute-start.6 = (f32[1152,128]{1,0:T(8,128)S(1)}, f32[1152,128]{1,0:T(8,128)S(1)}, u32[]{:S(2)}, u32[]{:S(2)}) collective-permute-start(f32[1152,128]{1,0:T(8,128)S(1)} %bitcast.80), channel_id=1, source_target_pairs={{0,16},{16,0},{1,17},{17,1},{2,18},{18,2},{3,19},{19,3},{4,20},{20... | collective-permute-start | bytes 1769480 | tf_op jit(solution)/shard_map/ppermute | solution.py:94

commit v8 on v7

--- a/solution.py
+++ b/solution.py
@@ -101,10 +101,10 @@
     other = lax.dynamic_slice_in_dim(terms, (1 - core) * half, half, 0)
     received, decoded = lax.optimization_barrier((with_partner(other), decoded))
     chip_sum = mine + received
-    portion = sent_and_summed(chip_sum, "lon_chip", 0)
-    portion = portion + lax.ppermute(portion, "lat_pair", [(0, 1), (1, 0)])
+    spread = ("lon_chip", "lat_pair")
+    portion = sent_and_summed(chip_sum, spread, 0)
     portion = taken_together(portion, "lat_z")
-    gathered = collect(portion, "lon_chip", 0)
+    gathered = collect(portion, spread, 0)
     partner = with_partner(gathered)
     return (
         decoded,

time: 118 us -> 113 us (0.958)
  starting transfers between devices: 36.6 us -> 29.4 us
  blocking collectives: 60.6 us -> 64.3 us
  waiting for transfers between devices: 7.42 us -> 6.09 us
    ppermute x1 -> x0, starting transfers between devices: 6.36 us -> none  [reduced_everywhere(): portion = portion + lax.ppermute(portion, 'lat_pair', [(0, 1), (1, 0)])]
    all_to_all x1, blocking collectives: 22.4 us -> 26.8 us  [sent_and_summed(): lax.all_to_all(blocks, axis, split_axis=0, concat_axis=0, tiled=True)]
    ppermute x1 -> x0, waiting for transfers between devices: 1.33 us -> none  [reduced_everywhere(): portion = portion + lax.ppermute(portion, 'lat_pair', [(0, 1), (1, 0)])]
  transfers between devices with their start and end apart: 7 -> 6, of which waited for: 5 -> 4; matrix products, arithmetic and copies ran while one was open for 2% -> 2% of each run, Pallas kernels for 0% -> 0%
where the time goes in v8:
time: 113 us
  blocking collectives  64.3 us (57%)
  starting transfers between devices  29.4 us (26%)
  matrix products  6.93 us (6%)
  waiting for transfers between devices  6.09 us (5%)
  other arithmetic  3.15 us (3%)
  local copies, waits for them, and re-layouts  1.95 us (2%)
    all_to_all x2, blocking collectives, sent_to_all(): return lax.all_to_all(copies, axis, split_axis=0, concat_axis=0, tiled=True)  37.5 us
    all_to_all x1, blocking collectives, sent_and_summed(): lax.all_to_all(blocks, axis, split_axis=0, concat_axis=0, tiled=True)  26.8 us
    ppermute x2, starting transfers between devices, with_partner(): return lax.ppermute(x, 'core', [(0, 1), (1, 0)])  16.1 us
    ppermute x2, starting transfers between devices, with_halo(): lax.ppermute(lax.slice_in_dim(block, 0, width, axis=dim), axis, backward)  7.46 us
    ppermute x2, starting transfers between devices, with_halo(): lax.ppermute(lax.slice_in_dim(block, block.shape[dim] - width, None, axis...  5.79 us
    dot_general x9, matrix products, conv_tile(): jnp.dot(stacked[row_tap:row_tap + rows_out], weights[row_tap].reshape(-1,...  4.5 us
    ppermute x2, waiting for transfers between devices, with_halo(): lax.ppermute(lax.slice_in_dim(block, 0, width, axis=dim), axis, backward)  4.41 us
    dot_general x6, matrix products, weight_terms(): lax.dot_general(stacked[row_tap:row_tap + rows_out], gradient, (((0, 1),...  2.43 us
  transfers between devices with their start and end apart: 6, of which 4 were waited for; matrix products, arithmetic and copies ran while one was open for 2% of the time, Pallas kernels for 0%

profile of v8, /device:TPU:1, one launch (start us, length us, event | category | flops | bytes accessed | tf_op | source)
XLA Modules:
  0.0 112.8 jit_solution(11778335785536137813)
XLA Ops:
  0.7 0.9 pad_maximum_fusion.12
  1.6 4.5 %collective-permute-start = (bf16[2,16,2,128]{3,2,1,0:T(2,128)(2,1)S(1)}, bf16[2,16,2,128]{3,2,1,0:T(2,128)(2,1)S(1)}, u32[]{:S(2)}, u32[]{:S(2)}) collective-permute-start(bf16[2,16,2,128]{3,2,1,0:T(2,128)(2,1)S(1)} %get-tuple-element.13), channel_id=1, source_target_pairs={{0,16},{16,32},{32,48},{48,64},{64,80},{80,96},{96,112},{112,128},... | collective-permute-start | bytes 49160 | tf_op jit(solution)/shard_map/ppermute | solution.py:17
  6.1 6.2 %collective-permute-start.1 = (bf16[2,16,2,128]{3,2,1,0:T(2,128)(2,1)S(1)}, bf16[2,16,2,128]{3,2,1,0:T(2,128)(2,1)S(1)}, u32[]{:S(2)}, u32[]{:S(2)}) collective-permute-start(bf16[2,16,2,128]{3,2,1,0:T(2,128)(2,1)S(1)} %get-tuple-element.14), channel_id=1, source_target_pairs={{16,0},{32,16},{48,32},{64,48},{80,64},{96,80},{112,96},{128,112},... | collective-permute-start | bytes 49160 | tf_op jit(solution)/shard_map/ppermute | solution.py:20
  13.4 1.3 %collective-permute-start.2 = (bf16[2,2,68,128]{3,2,1,0:T(8,128)(2,1)S(1)}, bf16[2,2,68,128]{3,2,1,0:T(8,128)(2,1)S(1)}, u32[]{:S(2)}, u32[]{:S(2)}) collective-permute-start(bf16[2,2,68,128]{3,2,1,0:T(8,128)(2,1)S(1)} %get-tuple-element.11), channel_id=1, source_target_pairs={{0,1},{1,2},{2,3},{3,4},{4,5},{5,6},{6,7},{7,8},{8,9},{9,10},{10,1... | collective-permute-start | bytes 208904 | tf_op jit(solution)/shard_map/ppermute | solution.py:17
  14.7 1.3 %collective-permute-start.3 = (bf16[2,2,68,128]{3,2,1,0:T(8,128)(2,1)S(1)}, bf16[2,2,68,128]{3,2,1,0:T(8,128)(2,1)S(1)}, u32[]{:S(2)}, u32[]{:S(2)}) collective-permute-start(bf16[2,2,68,128]{3,2,1,0:T(8,128)(2,1)S(1)} %get-tuple-element.12), channel_id=1, source_target_pairs={{1,0},{2,1},{3,2},{4,3},{5,4},{6,5},{7,6},{8,7},{9,8},{10,9},{11,1... | collective-permute-start | bytes 208904 | tf_op jit(solution)/shard_map/ppermute | solution.py:20
  16.1 4.2 %collective-permute-done.3 = bf16[2,2,68,128]{3,2,1,0:T(8,128)(2,1)S(1)} collective-permute-done((bf16[2,2,68,128]{3,2,1,0:T(8,128)(2,1)S(1)}, bf16[2,2,68,128]{3,2,1,0:T(8,128)(2,1)S(1)}, u32[]{:S(2)}, u32[]{:S(2)}) %collective-permute-start.3) | collective-permute-done | bytes 69664 | tf_op jit(solution)/shard_map/ppermute | solution.py:20
  20.3 0.3 pad_maximum_fusion.4
  20.9 0.5 fusion.8
  21.4 0.5 convolution_add_fusion.1
  21.9 0.5 fusion.6
  22.6 0.4 convolution_bitcast_fusion.2
  23.0 0.4 convolution_bitcast_fusion.1
  23.4 0.4 convolution_bitcast_fusion
  23.8 0.5 fusion.10
  24.4 0.4 fusion.7
  24.7 0.4 convolution_add_fusion.5
  25.1 0.4 fusion.1
  25.5 0.4 convolution_bitcast_fusion.5
  26.0 0.4 convolution_bitcast_fusion.4
  26.4 0.4 convolution_bitcast_fusion.3
  26.9 0.4 fusion.5
  27.2 8.8 %collective-permute-start.4 = (f32[1152,128]{1,0:T(8,128)S(1)}, f32[1152,128]{1,0:T(8,128)S(1)}, u32[]{:S(2)}, u32[]{:S(2)}) collective-permute-start(f32[1152,128]{1,0:T(8,128)S(1)} %fusion.5), channel_id=1, source_target_pairs={{0,16},{16,0},{1,17},{17,1},{2,18},{18,2},{3,19},{19,3},{4,20},{20... | collective-permute-start | bytes 1769480 | tf_op jit(solution)/shard_map/ppermute | solution.py:94
  36.0 0.4 fusion.9
  36.4 0.4 convolution_add_fusion.3
  36.8 1.1 fusion.2
  37.9 0.3 fusion.4
  38.3 26.8 %all_to_all.15 = f32[32,36,128]{2,1,0:T(8,128)S(1)} all-to-all(f32[32,36,128]{2,1,0:T(8,128)S(1)} %reshape.25), channel_id=1, replica_groups=mesh['lon_chip'=16,'core'=2,'lat_z'=8,'lat_pair'=2] {'lon_chip','lat_pair'}, dimensions={0} | all-to-all | bytes 1179648 | tf_op jit(solution)/shard_map/all_to_all | solution.py:33
  65.1 17.3 %all_to_all.16 = f32[8,36,128]{2,1,0:T(8,128)S(1)} all-to-all(f32[8,36,128]{2,1,0:T(8,128)S(1)} %broadcast_in_dim.20), channel_id=1, replica_groups=mesh['lon_chip'=16,'core'=2,'lat_z'=8,'lat_pair'=2] {'lat_z'}, dimensions={0} | all-to-all | bytes 294912 | tf_op jit(solution)/shard_map/all_to_all | solution.py:39
  82.5 20.3 %all_to_all.17 = f32[32,36,128]{2,1,0:T(8,128)S(1)} all-to-all(f32[32,36,128]{2,1,0:T(8,128)S(1)} %broadcast_in_dim.21), channel_id=1, replica_groups=mesh['lon_chip'=16,'core'=2,'lat_z'=8,'lat_pair'=2] {'lon_chip','lat_pair'}, dimensions={0} | all-to-all | bytes 1179648 | tf_op jit(solution)/shard_map/all_to_all | solution.py:39
  102.8 7.3 %collective-permute-start.5 = (f32[1152,128]{1,0:T(8,128)S(1)}, f32[1152,128]{1,0:T(8,128)S(1)}, u32[]{:S(2)}, u32[]{:S(2)}) collective-permute-start(f32[1152,128]{1,0:T(8,128)S(1)} %reshape.26), channel_id=1, source_target_pairs={{0,16},{16,0},{1,17},{17,1},{2,18},{18,2},{3,19},{19,3},{4,20},{20... | collective-permute-start | bytes 1769480 | tf_op jit(solution)/shard_map/ppermute | solution.py:94
  110.1 1.6 %collective-permute-done.5 = f32[1152,128]{1,0:T(8,128)S(1)} collective-permute-done((f32[1152,128]{1,0:T(8,128)S(1)}, f32[1152,128]{1,0:T(8,128)S(1)}, u32[]{:S(2)}, u32[]{:S(2)}) %collective-permute-start.5) | collective-permute-done | bytes 589856 | tf_op jit(solution)/shard_map/ppermute | solution.py:94
  111.7 1.1 broadcast_select_fusion
  (32 shorter events, 2.0 us)
Async XLA Ops:
  0.6 11.6 %copy-start.2 = (bf16[3,3,128,128]{3,2,1,0:T(8,128)(2,1)S(1)}, bf16[3,3,128,128]{3,2,1,0:T(8,128)(2,1)}, u32[]{:S(2)}) copy-start(bf16[3,3,128,128]{3,2,1,0:T(8,128)(2,1)} %param.6) | copy-start | bytes 884740
  0.6 11.7 %copy-start.3 = (bf16[3,3,128,128]{3,2,1,0:T(8,128)(2,1)S(1)}, bf16[3,3,128,128]{3,2,1,0:T(8,128)(2,1)}, u32[]{:S(2)}) copy-start(bf16[3,3,128,128]{3,2,1,0:T(8,128)(2,1)} %param.5) | copy-start | bytes 884740
  1.6 11.3 %collective-permute-start = (bf16[2,16,2,128]{3,2,1,0:T(2,128)(2,1)S(1)}, bf16[2,16,2,128]{3,2,1,0:T(2,128)(2,1)S(1)}, u32[]{:S(2)}, u32[]{:S(2)}) collective-permute-start(bf16[2,16,2,128]{3,2,1,0:T(2,128)(2,1)S(1)} %get-tuple-element.13), channel_id=1, source_target_pairs={{0,16},{16,32},{32,48},{48,64},{64,80},{80,96},{96,112},{112,128},... | collective-permute-start | bytes 49160 | tf_op jit(solution)/shard_map/ppermute | solution.py:17
  6.1 7.0 %collective-permute-start.1 = (bf16[2,16,2,128]{3,2,1,0:T(2,128)(2,1)S(1)}, bf16[2,16,2,128]{3,2,1,0:T(2,128)(2,1)S(1)}, u32[]{:S(2)}, u32[]{:S(2)}) collective-permute-start(bf16[2,16,2,128]{3,2,1,0:T(2,128)(2,1)S(1)} %get-tuple-element.14), channel_id=1, source_target_pairs={{16,0},{32,16},{48,32},{64,48},{80,64},{96,80},{112,96},{128,112},... | collective-permute-start | bytes 49160 | tf_op jit(solution)/shard_map/ppermute | solution.py:20
  12.3 1.0 copy-start
  12.4 1.0 copy-start.1
  13.4 2.7 %collective-permute-start.2 = (bf16[2,2,68,128]{3,2,1,0:T(8,128)(2,1)S(1)}, bf16[2,2,68,128]{3,2,1,0:T(8,128)(2,1)S(1)}, u32[]{:S(2)}, u32[]{:S(2)}) collective-permute-start(bf16[2,2,68,128]{3,2,1,0:T(8,128)(2,1)S(1)} %get-tuple-element.11), channel_id=1, source_target_pairs={{0,1},{1,2},{2,3},{3,4},{4,5},{5,6},{6,7},{7,8},{8,9},{9,10},{10,1... | collective-permute-start | bytes 208904 | tf_op jit(solution)/shard_map/ppermute | solution.py:17
  14.7 5.6 %collective-permute-start.3 = (bf16[2,2,68,128]{3,2,1,0:T(8,128)(2,1)S(1)}, bf16[2,2,68,128]{3,2,1,0:T(8,128)(2,1)S(1)}, u32[]{:S(2)}, u32[]{:S(2)}) collective-permute-start(bf16[2,2,68,128]{3,2,1,0:T(8,128)(2,1)S(1)} %get-tuple-element.12), channel_id=1, source_target_pairs={{1,0},{2,1},{3,2},{4,3},{5,4},{6,5},{7,6},{8,7},{9,8},{10,9},{11,1... | collective-permute-start | bytes 208904 | tf_op jit(solution)/shard_map/ppermute | solution.py:20
  27.2 10.6 %collective-permute-start.4 = (f32[1152,128]{1,0:T(8,128)S(1)}, f32[1152,128]{1,0:T(8,128)S(1)}, u32[]{:S(2)}, u32[]{:S(2)}) collective-permute-start(f32[1152,128]{1,0:T(8,128)S(1)} %fusion.5), channel_id=1, source_target_pairs={{0,16},{16,0},{1,17},{17,1},{2,18},{18,2},{3,19},{19,3},{4,20},{20... | collective-permute-start | bytes 1769480 | tf_op jit(solution)/shard_map/ppermute | solution.py:94
  102.8 8.9 %collective-permute-start.5 = (f32[1152,128]{1,0:T(8,128)S(1)}, f32[1152,128]{1,0:T(8,128)S(1)}, u32[]{:S(2)}, u32[]{:S(2)}) collective-permute-start(f32[1152,128]{1,0:T(8,128)S(1)} %reshape.26), channel_id=1, source_target_pairs={{0,16},{16,0},{1,17},{17,1},{2,18},{18,2},{3,19},{19,3},{4,20},{20... | collective-permute-start | bytes 1769480 | tf_op jit(solution)/shard_map/ppermute | solution.py:94

commit v9 on v8

--- a/solution.py
+++ b/solution.py
@@ -56,8 +56,40 @@
 
 def column_taps(padded, cols_out):
     return jnp.concatenate(
-        [padded[:, col_tap : col_tap + cols_out] for col_tap in range(3)], axis=-1
+        [lax.slice_in_dim(padded, col_tap, col_tap + cols_out, axis=-2) for col_tap in range(3)],
+        axis=-1,
     )
+
+
+def paired_conv(padded, weights):
+    rows_out = padded.shape[1] - 2
+    cols_out = padded.shape[2] - 2
+    stacked = column_taps(padded, cols_out)
+    summed = None
+    for row_tap in range(3):
+        part = lax.dot_general(
+            stacked[:, row_tap : row_tap + rows_out],
+            weights[:, row_tap].reshape(weights.shape[0], -1, weights.shape[4]),
+            (((3,), (1,)), ((0,), (0,))),
+            preferred_element_type=jnp.float32,
+        )
+        summed = part if summed is None else summed + part
+    return summed
+
+
+def paired_weight_terms(padded, gradient):
+    pairs, rows_out, cols_out, channels = gradient.shape
+    stacked = column_taps(padded, cols_out)
+    taps = [
+        lax.dot_general(
+            stacked[:, row_tap : row_tap + rows_out],
+            gradient,
+            (((1, 2), (1, 2)), ((0,), (0,))),
+            preferred_element_type=jnp.float32,
+        )
+        for row_tap in range(3)
+    ]
+    return jnp.stack(taps, axis=1).reshape(pairs * 9 * padded.shape[3], channels)
 
 
 def conv_tile(padded, weights):
@@ -73,21 +105,6 @@
         )
         summed = part if summed is None else summed + part
     return summed
-
-
-def weight_terms(padded, gradient):
-    rows_out, cols_out, channels = gradient.shape
-    stacked = column_taps(padded, cols_out)
-    taps = [
-        lax.dot_general(
-            stacked[row_tap : row_tap + rows_out],
-            gradient,
-            (((0, 1), (0, 1)), ((), ())),
-            preferred_element_type=jnp.float32,
-        )
-        for row_tap in range(3)
-    ]
-    return jnp.stack(taps).reshape(3, 3, padded.shape[2], channels)
 
 
 def with_partner(x):
@@ -120,27 +137,24 @@
     margin = 2
     widened = with_halo(stacked, ((LON, 2),), margin, True)
     extended = with_halo(widened, ((LAT, 1),), margin, False)
-    input_pad = extended[0]
-    grad_pad = extended[1][1:-1, 1:-1]
-    preact_wide = conv_tile(input_pad, weights_in)
+    flipped = jnp.transpose(weights_out[::-1, ::-1], (0, 1, 3, 2))
+    wide = paired_conv(extended, jnp.stack([weights_in, flipped]))
+    preact_wide = wide[0]
+    grad_hidden = wide[1][1:-1, 1:-1]
     hidden_wide = jax.nn.silu(preact_wide).astype(jnp.bfloat16)
     global_row = lax.axis_index(LAT) * tile_rows - 1 + jnp.arange(tile_rows + 2, dtype=jnp.int32)
     inside = (global_row >= 0) & (global_row < tile_rows * lax.axis_size(LAT))
     hidden_pad = jnp.where(inside[:, None, None], hidden_wide, jnp.zeros_like(hidden_wide))
     preact = preact_wide[1:-1, 1:-1]
-    input_use = input_pad[1:-1, 1:-1]
+    input_use = extended[0][1:-1, 1:-1]
     decoded = conv_tile(hidden_pad, weights_out).astype(jnp.bfloat16)
-    term_out = weight_terms(hidden_pad, cotangent)
-    flipped = jnp.transpose(weights_out[::-1, ::-1], (0, 1, 3, 2))
-    grad_hidden = conv_tile(grad_pad, flipped)
     sigmoid_pre = jax.nn.sigmoid(preact)
     grad_pre = (grad_hidden * (sigmoid_pre * (1.0 + preact * (1.0 - sigmoid_pre)))).astype(
         jnp.bfloat16
     )
     grad_pre = lax.optimization_barrier(grad_pre)
-    term_in = weight_terms(input_use, grad_pre)
-    all_terms = jnp.concatenate(
-        [term_in.reshape(9 * channels, channels), term_out.reshape(9 * channels, channels)], axis=0
+    all_terms = paired_weight_terms(
+        jnp.stack([input_use, hidden_pad]), jnp.stack([grad_pre, cotangent])
     )
     decoded, grad_in, grad_out = reduced_everywhere(all_terms, decoded)
     grad_in = grad_in.reshape(3, 3, channels, channels)

time: 113 us -> 113 us (level)
  local copies, waits for them, and re-layouts: 1.95 us -> 3.23 us
    dot_general x9 -> x3, matrix products: 4.5 us -> 1.8 us  [conv_tile(): jnp.dot(stacked[row_tap:row_tap + rows_out], weights[row_tap].reshape(-1,...]
    dot_general x6, matrix products: 2.43 us -> 4.75 us  [the longest x3 2.53 us: paired_conv(): lax.dot_general(stacked[:, row_tap:row_tap + rows_out], weights[:, row_ta...]
    another operation x2 -> x4, other arithmetic: 0.08 us -> 1.27 us  [the longest x1 0.9 us: shards(): stacked = jnp.stack([latent_frame, cotangent])]
    another operation x0 -> x3, local copies, waits for them, and re-layouts: none -> 1.15 us  [the longest x1 0.98 us: shards(): wide = paired_conv(extended, jnp.stack([weights_in, flipped]))]
  transfers between devices with their start and end apart: 6 -> 6, of which waited for: 4 -> 3; matrix products, arithmetic and copies ran while one was open for 2% -> 3% of each run, Pallas kernels for 0% -> 0%
where the time goes in v9:
time: 113 us
  blocking collectives  63.4 us (56%)
  starting transfers between devices  29.6 us (26%)
  matrix products  6.55 us (6%)
  waiting for transfers between devices  5.39 us (5%)
  other arithmetic  3.48 us (3%)
  local copies, waits for them, and re-layouts  3.23 us (3%)
    all_to_all x2, blocking collectives, sent_to_all(): return lax.all_to_all(copies, axis, split_axis=0, concat_axis=0, tiled=True)  37.5 us
    all_to_all x1, blocking collectives, sent_and_summed(): lax.all_to_all(blocks, axis, split_axis=0, concat_axis=0, tiled=True)  25.9 us
    ppermute x2, starting transfers between devices, with_partner(): return lax.ppermute(x, 'core', [(0, 1), (1, 0)])  16.3 us
    ppermute x2, starting transfers between devices, with_halo(): lax.ppermute(lax.slice_in_dim(block, 0, width, axis=dim), axis, backward)  7.46 us
    ppermute x2, starting transfers between devices, with_halo(): lax.ppermute(lax.slice_in_dim(block, block.shape[dim] - width, None, axis...  5.79 us
    ppermute x2, waiting for transfers between devices, with_halo(): lax.ppermute(lax.slice_in_dim(block, 0, width, axis=dim), axis, backward)  3.71 us
    dot_general x3, matrix products, paired_conv(): lax.dot_general(stacked[:, row_tap:row_tap + rows_out], weights[:, row_ta...  2.53 us
  transfers between devices with their start and end apart: 6, of which 3 were waited for; matrix products, arithmetic and copies ran while one was open for 3% of the time, Pallas kernels for 0%

profile of v9, /device:TPU:1, one launch (start us, length us, event | category | flops | bytes accessed | tf_op | source)
XLA Modules:
  0.0 112.6 jit_solution(369511766725874365)
XLA Ops:
  0.7 0.9 fusion.9
  1.6 4.5 %collective-permute-start = (bf16[2,16,2,128]{3,2,1,0:T(2,128)(2,1)S(1)}, bf16[2,16,2,128]{3,2,1,0:T(2,128)(2,1)S(1)}, u32[]{:S(2)}, u32[]{:S(2)}) collective-permute-start(bf16[2,16,2,128]{3,2,1,0:T(2,128)(2,1)S(1)} %get-tuple-element.21), channel_id=1, source_target_pairs={{0,16},{16,32},{32,48},{48,64},{64,80},{80,96},{96,112},{112,128},... | collective-permute-start | bytes 49160 | tf_op jit(solution)/shard_map/ppermute | solution.py:17
  6.1 6.2 %collective-permute-start.1 = (bf16[2,16,2,128]{3,2,1,0:T(2,128)(2,1)S(1)}, bf16[2,16,2,128]{3,2,1,0:T(2,128)(2,1)S(1)}, u32[]{:S(2)}, u32[]{:S(2)}) collective-permute-start(bf16[2,16,2,128]{3,2,1,0:T(2,128)(2,1)S(1)} %get-tuple-element.22), channel_id=1, source_target_pairs={{16,0},{32,16},{48,32},{64,48},{80,64},{96,80},{112,96},{128,112},... | collective-permute-start | bytes 49160 | tf_op jit(solution)/shard_map/ppermute | solution.py:20
  12.2 1.0 reverse_bitcast_fusion
  13.3 0.2 copy.21
  14.1 0.3 copy-done
  14.6 1.3 %collective-permute-start.2 = (bf16[2,2,68,128]{3,2,1,0:T(8,128)(2,1)S(1)}, bf16[2,2,68,128]{3,2,1,0:T(8,128)(2,1)S(1)}, u32[]{:S(2)}, u32[]{:S(2)}) collective-permute-start(bf16[2,2,68,128]{3,2,1,0:T(8,128)(2,1)S(1)} %get-tuple-element.19), channel_id=1, source_target_pairs={{0,1},{1,2},{2,3},{3,4},{4,5},{5,6},{6,7},{7,8},{8,9},{9,10},{10,1... | collective-permute-start | bytes 208904 | tf_op jit(solution)/shard_map/ppermute | solution.py:17
  15.9 1.3 %collective-permute-start.3 = (bf16[2,2,68,128]{3,2,1,0:T(8,128)(2,1)S(1)}, bf16[2,2,68,128]{3,2,1,0:T(8,128)(2,1)S(1)}, u32[]{:S(2)}, u32[]{:S(2)}) collective-permute-start(bf16[2,2,68,128]{3,2,1,0:T(8,128)(2,1)S(1)} %get-tuple-element.20), channel_id=1, source_target_pairs={{1,0},{2,1},{3,2},{4,3},{5,4},{6,5},{7,6},{8,7},{9,8},{10,9},{11,1... | collective-permute-start | bytes 208904 | tf_op jit(solution)/shard_map/ppermute | solution.py:20
  17.3 3.7 %collective-permute-done.3 = bf16[2,2,68,128]{3,2,1,0:T(8,128)(2,1)S(1)} collective-permute-done((bf16[2,2,68,128]{3,2,1,0:T(8,128)(2,1)S(1)}, bf16[2,2,68,128]{3,2,1,0:T(8,128)(2,1)S(1)}, u32[]{:S(2)}, u32[]{:S(2)}) %collective-permute-start.3) | collective-permute-done | bytes 69664 | tf_op jit(solution)/shard_map/ppermute | solution.py:20
  21.0 0.3 pad_maximum_fusion.4
  21.3 0.4 fusion.18
  21.7 0.8 fusion.14
  22.5 0.8 convolution_add_fusion.1
  23.4 0.8 convolution_add_fusion
  24.2 0.2 fusion.5
  24.4 0.2 fusion.6
  24.8 0.3 fusion.4
  25.1 0.2 fusion.3
  25.4 0.7 convolution_bitcast_fusion.1
  26.1 0.7 convolution_bitcast_fusion
  26.8 0.7 convolution_bitcast_fusion.2
  27.6 0.2 fusion.19
  28.0 9.0 %collective-permute-start.4 = (f32[1152,128]{1,0:T(8,128)S(1)}, f32[1152,128]{1,0:T(8,128)S(1)}, u32[]{:S(2)}, u32[]{:S(2)}) collective-permute-start(f32[1152,128]{1,0:T(8,128)S(1)} %constant_dynamic-slice_fusion), channel_id=1, source_target_pairs={{0,16},{16,0},{1,17},{17,1},{2,18},{18,2},{3,19},{19,3},{4,20},{20... | collective-permute-start | bytes 1769480 | tf_op jit(solution)/shard_map/ppermute | solution.py:111
  37.1 0.4 fusion.13
  37.4 0.4 convolution_add_fusion.3
  37.8 1.1 fusion.1
  39.0 25.9 %all_to_all.15 = f32[32,36,128]{2,1,0:T(8,128)S(1)} all-to-all(f32[32,36,128]{2,1,0:T(8,128)S(1)} %reshape.29), channel_id=1, replica_groups=mesh['lon_chip'=16,'core'=2,'lat_z'=8,'lat_pair'=2] {'lon_chip','lat_pair'}, dimensions={0} | all-to-all | bytes 1179648 | tf_op jit(solution)/shard_map/all_to_all | solution.py:33
  65.0 17.2 %all_to_all.16 = f32[8,36,128]{2,1,0:T(8,128)S(1)} all-to-all(f32[8,36,128]{2,1,0:T(8,128)S(1)} %broadcast_in_dim.26), channel_id=1, replica_groups=mesh['lon_chip'=16,'core'=2,'lat_z'=8,'lat_pair'=2] {'lat_z'}, dimensions={0} | all-to-all | bytes 294912 | tf_op jit(solution)/shard_map/all_to_all | solution.py:39
  82.3 20.3 %all_to_all.17 = f32[32,36,128]{2,1,0:T(8,128)S(1)} all-to-all(f32[32,36,128]{2,1,0:T(8,128)S(1)} %broadcast_in_dim.27), channel_id=1, replica_groups=mesh['lon_chip'=16,'core'=2,'lat_z'=8,'lat_pair'=2] {'lon_chip','lat_pair'}, dimensions={0} | all-to-all | bytes 1179648 | tf_op jit(solution)/shard_map/all_to_all | solution.py:39
  102.6 7.3 %collective-permute-start.5 = (f32[1152,128]{1,0:T(8,128)S(1)}, f32[1152,128]{1,0:T(8,128)S(1)}, u32[]{:S(2)}, u32[]{:S(2)}) collective-permute-start(f32[1152,128]{1,0:T(8,128)S(1)} %reshape.30), channel_id=1, source_target_pairs={{0,16},{16,0},{1,17},{17,1},{2,18},{18,2},{3,19},{19,3},{4,20},{20... | collective-permute-start | bytes 1769480 | tf_op jit(solution)/shard_map/ppermute | solution.py:111
  109.9 1.6 %collective-permute-done.5 = f32[1152,128]{1,0:T(8,128)S(1)} collective-permute-done((f32[1152,128]{1,0:T(8,128)S(1)}, f32[1152,128]{1,0:T(8,128)S(1)}, u32[]{:S(2)}, u32[]{:S(2)}) %collective-permute-start.5) | collective-permute-done | bytes 589856 | tf_op jit(solution)/shard_map/ppermute | solution.py:111
  111.5 1.1 broadcast_select_fusion
  (31 shorter events, 1.5 us)
Async XLA Ops:
  0.6 12.6 %copy-start.2 = (bf16[3,3,128,128]{3,2,1,0:T(8,128)(2,1)S(1)}, bf16[3,3,128,128]{3,2,1,0:T(8,128)(2,1)}, u32[]{:S(2)}) copy-start(bf16[3,3,128,128]{3,2,1,0:T(8,128)(2,1)} %param.6) | copy-start | bytes 884740
  0.6 12.6 %copy-start.3 = (bf16[3,3,128,128]{3,2,1,0:T(8,128)(2,1)S(1)}, bf16[3,3,128,128]{3,2,1,0:T(8,128)(2,1)}, u32[]{:S(2)}) copy-start(bf16[3,3,128,128]{3,2,1,0:T(8,128)(2,1)} %param.5) | copy-start | bytes 884740
  1.6 12.6 %collective-permute-start = (bf16[2,16,2,128]{3,2,1,0:T(2,128)(2,1)S(1)}, bf16[2,16,2,128]{3,2,1,0:T(2,128)(2,1)S(1)}, u32[]{:S(2)}, u32[]{:S(2)}) collective-permute-start(bf16[2,16,2,128]{3,2,1,0:T(2,128)(2,1)S(1)} %get-tuple-element.21), channel_id=1, source_target_pairs={{0,16},{16,32},{32,48},{48,64},{64,80},{80,96},{96,112},{112,128},... | collective-permute-start | bytes 49160 | tf_op jit(solution)/shard_map/ppermute | solution.py:17
  6.1 8.1 %collective-permute-start.1 = (bf16[2,16,2,128]{3,2,1,0:T(2,128)(2,1)S(1)}, bf16[2,16,2,128]{3,2,1,0:T(2,128)(2,1)S(1)}, u32[]{:S(2)}, u32[]{:S(2)}) collective-permute-start(bf16[2,16,2,128]{3,2,1,0:T(2,128)(2,1)S(1)} %get-tuple-element.22), channel_id=1, source_target_pairs={{16,0},{32,16},{48,32},{64,48},{80,64},{96,80},{112,96},{128,112},... | collective-permute-start | bytes 49160 | tf_op jit(solution)/shard_map/ppermute | solution.py:20
  13.5 1.0 copy-start
  13.5 1.0 copy-start.1
  14.6 2.7 %collective-permute-start.2 = (bf16[2,2,68,128]{3,2,1,0:T(8,128)(2,1)S(1)}, bf16[2,2,68,128]{3,2,1,0:T(8,128)(2,1)S(1)}, u32[]{:S(2)}, u32[]{:S(2)}) collective-permute-start(bf16[2,2,68,128]{3,2,1,0:T(8,128)(2,1)S(1)} %get-tuple-element.19), channel_id=1, source_target_pairs={{0,1},{1,2},{2,3},{3,4},{4,5},{5,6},{6,7},{7,8},{8,9},{9,10},{10,1... | collective-permute-start | bytes 208904 | tf_op jit(solution)/shard_map/ppermute | solution.py:17
  15.9 5.1 %collective-permute-start.3 = (bf16[2,2,68,128]{3,2,1,0:T(8,128)(2,1)S(1)}, bf16[2,2,68,128]{3,2,1,0:T(8,128)(2,1)S(1)}, u32[]{:S(2)}, u32[]{:S(2)}) collective-permute-start(bf16[2,2,68,128]{3,2,1,0:T(8,128)(2,1)S(1)} %get-tuple-element.20), channel_id=1, source_target_pairs={{1,0},{2,1},{3,2},{4,3},{5,4},{6,5},{7,6},{8,7},{9,8},{10,9},{11,1... | collective-permute-start | bytes 208904 | tf_op jit(solution)/shard_map/ppermute | solution.py:20
  28.0 10.8 %collective-permute-start.4 = (f32[1152,128]{1,0:T(8,128)S(1)}, f32[1152,128]{1,0:T(8,128)S(1)}, u32[]{:S(2)}, u32[]{:S(2)}) collective-permute-start(f32[1152,128]{1,0:T(8,128)S(1)} %constant_dynamic-slice_fusion), channel_id=1, source_target_pairs={{0,16},{16,0},{1,17},{17,1},{2,18},{18,2},{3,19},{19,3},{4,20},{20... | collective-permute-start | bytes 1769480 | tf_op jit(solution)/shard_map/ppermute | solution.py:111
  102.6 8.9 %collective-permute-start.5 = (f32[1152,128]{1,0:T(8,128)S(1)}, f32[1152,128]{1,0:T(8,128)S(1)}, u32[]{:S(2)}, u32[]{:S(2)}) collective-permute-start(f32[1152,128]{1,0:T(8,128)S(1)} %reshape.30), channel_id=1, source_target_pairs={{0,16},{16,0},{1,17},{17,1},{2,18},{18,2},{3,19},{19,3},{4,20},{20... | collective-permute-start | bytes 1769480 | tf_op jit(solution)/shard_map/ppermute | solution.py:111

commit v10 on v8

--- a/solution.py
+++ b/solution.py
@@ -118,8 +118,8 @@
     channels = latent_frame.shape[2]
     stacked = jnp.stack([latent_frame, cotangent])
     margin = 2
-    widened = with_halo(stacked, ((LON, 2),), margin, True)
-    extended = with_halo(widened, ((LAT, 1),), margin, False)
+    widened = with_halo(stacked, ((LAT, 1),), margin, False)
+    extended = with_halo(widened, ((LON, 2),), margin, True)
     input_pad = extended[0]
     grad_pad = extended[1][1:-1, 1:-1]
     preact_wide = conv_tile(input_pad, weights_in)

time: 113 us -> 115 us (1.018)
  blocking collectives: 64.3 us -> 65.7 us
    ppermute x2, starting transfers between devices: 5.79 us -> 8.98 us  [with_halo(): lax.ppermute(lax.slice_in_dim(block, block.shape[dim] - width, None, axis...]
    ppermute x2, starting transfers between devices: 7.46 us -> 5.03 us  [with_halo(): lax.ppermute(lax.slice_in_dim(block, 0, width, axis=dim), axis, backward)]
    all_to_all x1, blocking collectives: 26.8 us -> 28.1 us  [sent_and_summed(): lax.all_to_all(blocks, axis, split_axis=0, concat_axis=0, tiled=True)]
  transfers between devices with their start and end apart: 6 -> 6, of which waited for: 4 -> 3; matrix products, arithmetic and copies ran while one was open for 2% -> 2% of each run, Pallas kernels for 0% -> 0%
where the time goes in v10:
time: 115 us; the launch traced here: 114 us
  blocking collectives  65.7 us (57%)
  starting transfers between devices  29.3 us (25%)
  matrix products  6.93 us (6%)
  waiting for transfers between devices  6.6 us (6%)
  other arithmetic  3.16 us (3%)
  local copies, waits for them, and re-layouts  1.63 us (1%)
    all_to_all x2, blocking collectives, sent_to_all(): return lax.all_to_all(copies, axis, split_axis=0, concat_axis=0, tiled=True)  37.6 us
    all_to_all x1, blocking collectives, sent_and_summed(): lax.all_to_all(blocks, axis, split_axis=0, concat_axis=0, tiled=True)  28.1 us
    ppermute x2, starting transfers between devices, with_partner(): return lax.ppermute(x, 'core', [(0, 1), (1, 0)])  15.3 us
    ppermute x2, starting transfers between devices, with_halo(): lax.ppermute(lax.slice_in_dim(block, block.shape[dim] - width, None, axis...  8.98 us
    ppermute x2, starting transfers between devices, with_halo(): lax.ppermute(lax.slice_in_dim(block, 0, width, axis=dim), axis, backward)  5.03 us
    ppermute x2, waiting for transfers between devices, with_halo(): lax.ppermute(lax.slice_in_dim(block, 0, width, axis=dim), axis, backward)  4.98 us
    dot_general x9, matrix products, conv_tile(): jnp.dot(stacked[row_tap:row_tap + rows_out], weights[row_tap].reshape(-1,...  4.5 us
    dot_general x6, matrix products, weight_terms(): lax.dot_general(stacked[row_tap:row_tap + rows_out], gradient, (((0, 1),...  2.43 us
  transfers between devices with their start and end apart: 6, of which 3 were waited for; matrix products, arithmetic and copies ran while one was open for 2% of the time, Pallas kernels for 0%

profile of v10, /device:TPU:1, one launch (start us, length us, event | category | flops | bytes accessed | tf_op | source)
XLA Modules:
  0.0 114.3 jit_solution(3067746117612847816)
XLA Ops:
  0.6 0.9 pad_maximum_fusion.8
  1.5 4.2 %collective-permute-start = (bf16[2,2,64,128]{3,2,1,0:T(8,128)(2,1)S(1)}, bf16[2,2,64,128]{3,2,1,0:T(8,128)(2,1)S(1)}, u32[]{:S(2)}, u32[]{:S(2)}) collective-permute-start(bf16[2,2,64,128]{3,2,1,0:T(8,128)(2,1)S(1)} %get-tuple-element.13), channel_id=1, source_target_pairs={{0,1},{1,2},{2,3},{3,4},{4,5},{5,6},{6,7},{7,8},{8,9},{9,10},{10,1... | collective-permute-start | bytes 196616 | tf_op jit(solution)/shard_map/ppermute | solution.py:17
  5.7 1.3 %collective-permute-start.1 = (bf16[2,2,64,128]{3,2,1,0:T(8,128)(2,1)S(1)}, bf16[2,2,64,128]{3,2,1,0:T(8,128)(2,1)S(1)}, u32[]{:S(2)}, u32[]{:S(2)}) collective-permute-start(bf16[2,2,64,128]{3,2,1,0:T(8,128)(2,1)S(1)} %get-tuple-element.14), channel_id=1, source_target_pairs={{1,0},{2,1},{3,2},{4,3},{5,4},{6,5},{7,6},{8,7},{9,8},{10,9},{11,1... | collective-permute-start | bytes 196616 | tf_op jit(solution)/shard_map/ppermute | solution.py:20
  7.2 4.1 %collective-permute-done.1 = bf16[2,2,64,128]{3,2,1,0:T(8,128)(2,1)S(1)} collective-permute-done((bf16[2,2,64,128]{3,2,1,0:T(8,128)(2,1)S(1)}, bf16[2,2,64,128]{3,2,1,0:T(8,128)(2,1)S(1)}, u32[]{:S(2)}, u32[]{:S(2)}) %collective-permute-start.1) | collective-permute-done | bytes 65568 | tf_op jit(solution)/shard_map/ppermute | solution.py:20
  11.3 4.8 %collective-permute-start.2 = (bf16[2,20,2,128]{3,2,1,0:T(2,128)(2,1)S(1)}, bf16[2,20,2,128]{3,2,1,0:T(2,128)(2,1)S(1)}, u32[]{:S(2)}, u32[]{:S(2)}) collective-permute-start(bf16[2,20,2,128]{3,2,1,0:T(2,128)(2,1)S(1)} %get-tuple-element.11), channel_id=1, source_target_pairs={{0,16},{16,32},{32,48},{48,64},{64,80},{80,96},{96,112},{112,128},... | collective-permute-start | bytes 61448 | tf_op jit(solution)/shard_map/ppermute | solution.py:17
  16.1 3.7 %collective-permute-start.3 = (bf16[2,20,2,128]{3,2,1,0:T(2,128)(2,1)S(1)}, bf16[2,20,2,128]{3,2,1,0:T(2,128)(2,1)S(1)}, u32[]{:S(2)}, u32[]{:S(2)}) collective-permute-start(bf16[2,20,2,128]{3,2,1,0:T(2,128)(2,1)S(1)} %get-tuple-element.12), channel_id=1, source_target_pairs={{16,0},{32,16},{48,32},{64,48},{80,64},{96,80},{112,96},{128,112},... | collective-permute-start | bytes 61448 | tf_op jit(solution)/shard_map/ppermute | solution.py:20
  20.3 0.9 collective-permute-done.3
  21.8 0.5 fusion.8
  22.3 0.5 convolution_add_fusion.1
  22.8 0.5 fusion.6
  23.6 0.4 convolution_bitcast_fusion.2
  24.0 0.4 convolution_bitcast_fusion.1
  24.4 0.4 convolution_bitcast_fusion
  24.8 0.5 fusion.10
  25.3 0.4 fusion.7
  25.7 0.4 convolution_add_fusion.5
  26.1 0.4 fusion.1
  26.5 0.4 convolution_bitcast_fusion.5
  26.9 0.4 convolution_bitcast_fusion.4
  27.3 0.4 convolution_bitcast_fusion.3
  27.8 0.4 fusion.5
  28.2 8.0 %collective-permute-start.4 = (f32[1152,128]{1,0:T(8,128)S(1)}, f32[1152,128]{1,0:T(8,128)S(1)}, u32[]{:S(2)}, u32[]{:S(2)}) collective-permute-start(f32[1152,128]{1,0:T(8,128)S(1)} %fusion.5), channel_id=1, source_target_pairs={{0,16},{16,0},{1,17},{17,1},{2,18},{18,2},{3,19},{19,3},{4,20},{20... | collective-permute-start | bytes 1769480 | tf_op jit(solution)/shard_map/ppermute | solution.py:94
  36.2 0.4 fusion.9
  36.5 0.4 convolution_add_fusion.3
  36.9 1.1 fusion.2
  38.0 0.3 fusion.4
  38.4 28.1 %all_to_all.15 = f32[32,36,128]{2,1,0:T(8,128)S(1)} all-to-all(f32[32,36,128]{2,1,0:T(8,128)S(1)} %reshape.25), channel_id=1, replica_groups=mesh['lon_chip'=16,'core'=2,'lat_z'=8,'lat_pair'=2] {'lon_chip','lat_pair'}, dimensions={0} | all-to-all | bytes 1179648 | tf_op jit(solution)/shard_map/all_to_all | solution.py:33
  66.5 17.3 %all_to_all.16 = f32[8,36,128]{2,1,0:T(8,128)S(1)} all-to-all(f32[8,36,128]{2,1,0:T(8,128)S(1)} %broadcast_in_dim.20), channel_id=1, replica_groups=mesh['lon_chip'=16,'core'=2,'lat_z'=8,'lat_pair'=2] {'lat_z'}, dimensions={0} | all-to-all | bytes 294912 | tf_op jit(solution)/shard_map/all_to_all | solution.py:39
  83.9 20.3 %all_to_all.17 = f32[32,36,128]{2,1,0:T(8,128)S(1)} all-to-all(f32[32,36,128]{2,1,0:T(8,128)S(1)} %broadcast_in_dim.21), channel_id=1, replica_groups=mesh['lon_chip'=16,'core'=2,'lat_z'=8,'lat_pair'=2] {'lon_chip','lat_pair'}, dimensions={0} | all-to-all | bytes 1179648 | tf_op jit(solution)/shard_map/all_to_all | solution.py:39
  104.3 7.3 %collective-permute-start.5 = (f32[1152,128]{1,0:T(8,128)S(1)}, f32[1152,128]{1,0:T(8,128)S(1)}, u32[]{:S(2)}, u32[]{:S(2)}) collective-permute-start(f32[1152,128]{1,0:T(8,128)S(1)} %reshape.26), channel_id=1, source_target_pairs={{0,16},{16,0},{1,17},{17,1},{2,18},{18,2},{3,19},{19,3},{4,20},{20... | collective-permute-start | bytes 1769480 | tf_op jit(solution)/shard_map/ppermute | solution.py:94
  111.6 1.6 %collective-permute-done.5 = f32[1152,128]{1,0:T(8,128)S(1)} collective-permute-done((f32[1152,128]{1,0:T(8,128)S(1)}, f32[1152,128]{1,0:T(8,128)S(1)}, u32[]{:S(2)}, u32[]{:S(2)}) %collective-permute-start.5) | collective-permute-done | bytes 589856 | tf_op jit(solution)/shard_map/ppermute | solution.py:94
  113.2 1.1 broadcast_select_fusion
  (32 shorter events, 1.6 us)
Async XLA Ops:
  0.6 6.4 %copy-start.2 = (bf16[3,3,128,128]{3,2,1,0:T(8,128)(2,1)S(1)}, bf16[3,3,128,128]{3,2,1,0:T(8,128)(2,1)}, u32[]{:S(2)}) copy-start(bf16[3,3,128,128]{3,2,1,0:T(8,128)(2,1)} %param.6) | copy-start | bytes 884740
  1.5 5.5 %copy-start.3 = (bf16[3,3,128,128]{3,2,1,0:T(8,128)(2,1)S(1)}, bf16[3,3,128,128]{3,2,1,0:T(8,128)(2,1)}, u32[]{:S(2)}) copy-start(bf16[3,3,128,128]{3,2,1,0:T(8,128)(2,1)} %param.5) | copy-start | bytes 884740
  1.5 5.6 %collective-permute-start = (bf16[2,2,64,128]{3,2,1,0:T(8,128)(2,1)S(1)}, bf16[2,2,64,128]{3,2,1,0:T(8,128)(2,1)S(1)}, u32[]{:S(2)}, u32[]{:S(2)}) collective-permute-start(bf16[2,2,64,128]{3,2,1,0:T(8,128)(2,1)S(1)} %get-tuple-element.13), channel_id=1, source_target_pairs={{0,1},{1,2},{2,3},{3,4},{4,5},{5,6},{6,7},{7,8},{8,9},{9,10},{10,1... | collective-permute-start | bytes 196616 | tf_op jit(solution)/shard_map/ppermute | solution.py:17
  5.7 5.5 %collective-permute-start.1 = (bf16[2,2,64,128]{3,2,1,0:T(8,128)(2,1)S(1)}, bf16[2,2,64,128]{3,2,1,0:T(8,128)(2,1)S(1)}, u32[]{:S(2)}, u32[]{:S(2)}) collective-permute-start(bf16[2,2,64,128]{3,2,1,0:T(8,128)(2,1)S(1)} %get-tuple-element.14), channel_id=1, source_target_pairs={{1,0},{2,1},{3,2},{4,3},{5,4},{6,5},{7,6},{8,7},{9,8},{10,9},{11,1... | collective-permute-start | bytes 196616 | tf_op jit(solution)/shard_map/ppermute | solution.py:20
  7.1 4.2 %copy-start = (bf16[16,64,128]{2,1,0:T(8,128)(2,1)S(1)}, bf16[16,64,128]{2,1,0:T(8,128)(2,1)}, u32[]{:S(2)}) copy-start(bf16[16,64,128]{2,1,0:T(8,128)(2,1)} %param.4) | copy-start | bytes 786436
  7.1 4.2 %copy-start.1 = (bf16[16,64,128]{2,1,0:T(8,128)(2,1)S(1)}, bf16[16,64,128]{2,1,0:T(8,128)(2,1)}, u32[]{:S(2)}) copy-start(bf16[16,64,128]{2,1,0:T(8,128)(2,1)} %param.7) | copy-start | bytes 786436
  11.3 9.0 %collective-permute-start.2 = (bf16[2,20,2,128]{3,2,1,0:T(2,128)(2,1)S(1)}, bf16[2,20,2,128]{3,2,1,0:T(2,128)(2,1)S(1)}, u32[]{:S(2)}, u32[]{:S(2)}) collective-permute-start(bf16[2,20,2,128]{3,2,1,0:T(2,128)(2,1)S(1)} %get-tuple-element.11), channel_id=1, source_target_pairs={{0,16},{16,32},{32,48},{48,64},{64,80},{80,96},{96,112},{112,128},... | collective-permute-start | bytes 61448 | tf_op jit(solution)/shard_map/ppermute | solution.py:17
  16.1 5.1 %collective-permute-start.3 = (bf16[2,20,2,128]{3,2,1,0:T(2,128)(2,1)S(1)}, bf16[2,20,2,128]{3,2,1,0:T(2,128)(2,1)S(1)}, u32[]{:S(2)}, u32[]{:S(2)}) collective-permute-start(bf16[2,20,2,128]{3,2,1,0:T(2,128)(2,1)S(1)} %get-tuple-element.12), channel_id=1, source_target_pairs={{16,0},{32,16},{48,32},{64,48},{80,64},{96,80},{112,96},{128,112},... | collective-permute-start | bytes 61448 | tf_op jit(solution)/shard_map/ppermute | solution.py:20
  28.2 9.8 %collective-permute-start.4 = (f32[1152,128]{1,0:T(8,128)S(1)}, f32[1152,128]{1,0:T(8,128)S(1)}, u32[]{:S(2)}, u32[]{:S(2)}) collective-permute-start(f32[1152,128]{1,0:T(8,128)S(1)} %fusion.5), channel_id=1, source_target_pairs={{0,16},{16,0},{1,17},{17,1},{2,18},{18,2},{3,19},{19,3},{4,20},{20... | collective-permute-start | bytes 1769480 | tf_op jit(solution)/shard_map/ppermute | solution.py:94
  104.3 8.9 %collective-permute-start.5 = (f32[1152,128]{1,0:T(8,128)S(1)}, f32[1152,128]{1,0:T(8,128)S(1)}, u32[]{:S(2)}, u32[]{:S(2)}) collective-permute-start(f32[1152,128]{1,0:T(8,128)S(1)} %reshape.26), channel_id=1, source_target_pairs={{0,16},{16,0},{1,17},{17,1},{2,18},{18,2},{3,19},{19,3},{4,20},{20... | collective-permute-start | bytes 1769480 | tf_op jit(solution)/shard_map/ppermute | solution.py:94

commit v11 on v8

--- a/solution.py
+++ b/solution.py
@@ -103,13 +103,13 @@
     chip_sum = mine + received
     spread = ("lon_chip", "lat_pair")
     portion = sent_and_summed(chip_sum, spread, 0)
-    portion = taken_together(portion, "lat_z")
+    portion = taken_together(portion, "lat_z").astype(jnp.bfloat16)
     gathered = collect(portion, spread, 0)
     partner = with_partner(gathered)
     return (
         decoded,
-        jnp.where(core == 0, gathered, partner),
-        jnp.where(core == 0, partner, gathered),
+        jnp.where(core == 0, gathered, partner).astype(jnp.float32),
+        jnp.where(core == 0, partner, gathered).astype(jnp.float32),
     )
 
 

time: 113 us -> 108 us (0.956)
  blocking collectives: 64.3 us -> 59.5 us
    all_to_all x2, blocking collectives: 37.5 us -> 32.7 us  [sent_to_all(): return lax.all_to_all(copies, axis, split_axis=0, concat_axis=0, tiled=True)]
    reshape x0 -> x2, other arithmetic: none -> 1.72 us  [the longest x1 0.86 us: shards(): grad_in = grad_in.reshape(3, 3, channels, channels)]
where the time goes in v11:
time: 108 us; the launch traced here: 107 us
  blocking collectives  59.5 us (55%)
  starting transfers between devices  28.4 us (26%)
  matrix products  6.93 us (6%)
  waiting for transfers between devices  5.67 us (5%)
  other arithmetic  3.84 us (4%)
  local copies, waits for them, and re-layouts  1.96 us (2%)
    all_to_all x2, blocking collectives, sent_to_all(): return lax.all_to_all(copies, axis, split_axis=0, concat_axis=0, tiled=True)  32.7 us
    all_to_all x1, blocking collectives, sent_and_summed(): lax.all_to_all(blocks, axis, split_axis=0, concat_axis=0, tiled=True)  26.8 us
    ppermute x2, starting transfers between devices, with_partner(): return lax.ppermute(x, 'core', [(0, 1), (1, 0)])  15.2 us
    ppermute x2, starting transfers between devices, with_halo(): lax.ppermute(lax.slice_in_dim(block, 0, width, axis=dim), axis, backward)  7.46 us
    ppermute x2, starting transfers between devices, with_halo(): lax.ppermute(lax.slice_in_dim(block, block.shape[dim] - width, None, axis...  5.79 us
    dot_general x9, matrix products, conv_tile(): jnp.dot(stacked[row_tap:row_tap + rows_out], weights[row_tap].reshape(-1,...  4.5 us
    ppermute x2, waiting for transfers between devices, with_halo(): lax.ppermute(lax.slice_in_dim(block, 0, width, axis=dim), axis, backward)  4.41 us
    dot_general x6, matrix products, weight_terms(): lax.dot_general(stacked[row_tap:row_tap + rows_out], gradient, (((0, 1),...  2.43 us
  transfers between devices with their start and end apart: 6, of which 4 were waited for; matrix products, arithmetic and copies ran while one was open for 2% of the time, Pallas kernels for 0%

profile of v11, /device:TPU:1, one launch (start us, length us, event | category | flops | bytes accessed | tf_op | source)
XLA Modules:
  0.0 107.3 jit_solution(6361022818143452584)
XLA Ops:
  0.7 0.9 pad_maximum_fusion.12
  1.6 4.5 %collective-permute-start = (bf16[2,16,2,128]{3,2,1,0:T(2,128)(2,1)S(1)}, bf16[2,16,2,128]{3,2,1,0:T(2,128)(2,1)S(1)}, u32[]{:S(2)}, u32[]{:S(2)}) collective-permute-start(bf16[2,16,2,128]{3,2,1,0:T(2,128)(2,1)S(1)} %get-tuple-element.13), channel_id=1, source_target_pairs={{0,16},{16,32},{32,48},{48,64},{64,80},{80,96},{96,112},{112,128},... | collective-permute-start | bytes 49160 | tf_op jit(solution)/shard_map/ppermute | solution.py:17
  6.1 6.2 %collective-permute-start.1 = (bf16[2,16,2,128]{3,2,1,0:T(2,128)(2,1)S(1)}, bf16[2,16,2,128]{3,2,1,0:T(2,128)(2,1)S(1)}, u32[]{:S(2)}, u32[]{:S(2)}) collective-permute-start(bf16[2,16,2,128]{3,2,1,0:T(2,128)(2,1)S(1)} %get-tuple-element.14), channel_id=1, source_target_pairs={{16,0},{32,16},{48,32},{64,48},{80,64},{96,80},{112,96},{128,112},... | collective-permute-start | bytes 49160 | tf_op jit(solution)/shard_map/ppermute | solution.py:20
  13.4 1.3 %collective-permute-start.2 = (bf16[2,2,68,128]{3,2,1,0:T(8,128)(2,1)S(1)}, bf16[2,2,68,128]{3,2,1,0:T(8,128)(2,1)S(1)}, u32[]{:S(2)}, u32[]{:S(2)}) collective-permute-start(bf16[2,2,68,128]{3,2,1,0:T(8,128)(2,1)S(1)} %get-tuple-element.11), channel_id=1, source_target_pairs={{0,1},{1,2},{2,3},{3,4},{4,5},{5,6},{6,7},{7,8},{8,9},{9,10},{10,1... | collective-permute-start | bytes 208904 | tf_op jit(solution)/shard_map/ppermute | solution.py:17
  14.7 1.3 %collective-permute-start.3 = (bf16[2,2,68,128]{3,2,1,0:T(8,128)(2,1)S(1)}, bf16[2,2,68,128]{3,2,1,0:T(8,128)(2,1)S(1)}, u32[]{:S(2)}, u32[]{:S(2)}) collective-permute-start(bf16[2,2,68,128]{3,2,1,0:T(8,128)(2,1)S(1)} %get-tuple-element.12), channel_id=1, source_target_pairs={{1,0},{2,1},{3,2},{4,3},{5,4},{6,5},{7,6},{8,7},{9,8},{10,9},{11,1... | collective-permute-start | bytes 208904 | tf_op jit(solution)/shard_map/ppermute | solution.py:20
  16.1 4.2 %collective-permute-done.3 = bf16[2,2,68,128]{3,2,1,0:T(8,128)(2,1)S(1)} collective-permute-done((bf16[2,2,68,128]{3,2,1,0:T(8,128)(2,1)S(1)}, bf16[2,2,68,128]{3,2,1,0:T(8,128)(2,1)S(1)}, u32[]{:S(2)}, u32[]{:S(2)}) %collective-permute-start.3) | collective-permute-done | bytes 69664 | tf_op jit(solution)/shard_map/ppermute | solution.py:20
  20.9 0.5 fusion.8
  21.4 0.5 convolution_add_fusion.1
  21.9 0.5 fusion.6
  22.6 0.4 convolution_bitcast_fusion.2
  23.0 0.4 convolution_bitcast_fusion.1
  23.4 0.4 convolution_bitcast_fusion
  23.8 0.5 fusion.10
  24.4 0.4 fusion.7
  24.7 0.4 convolution_add_fusion.5
  25.1 0.4 fusion.1
  25.5 0.4 convolution_bitcast_fusion.5
  26.0 0.4 convolution_bitcast_fusion.4
  26.4 0.4 convolution_bitcast_fusion.3
  26.9 0.4 fusion.5
  27.2 8.8 %collective-permute-start.4 = (f32[1152,128]{1,0:T(8,128)S(1)}, f32[1152,128]{1,0:T(8,128)S(1)}, u32[]{:S(2)}, u32[]{:S(2)}) collective-permute-start(f32[1152,128]{1,0:T(8,128)S(1)} %fusion.5), channel_id=1, source_target_pairs={{0,16},{16,0},{1,17},{17,1},{2,18},{18,2},{3,19},{19,3},{4,20},{20... | collective-permute-start | bytes 1769480 | tf_op jit(solution)/shard_map/ppermute | solution.py:94
  36.0 0.4 fusion.9
  36.4 0.4 convolution_add_fusion.3
  36.8 1.1 %fusion.2 = bf16[16,64,128]{2,1,0:T(8,128)(2,1)} fusion(f32[16,64,128]{2,1,0:T(8,128)S(1)} %convolution_add_fusion.3, bf16[384,128,1]{1,0,2:T(8,128)(2,1)S(1)} %bitcast.86, bf16[18,64,128]{2,1,0:T(8,128)(2,1)S(1)} %get-tuple-element.25, bf16[18,64,128]{2,1,0:T(8,128)(2,1)S(1)} %get-tuple-element.26, bf16[18,64,128]{2,1,0:T(8,128)(2,1)S(1)} %get-tuple-element.24), kind=kOutput, calls=%fused_computation.12 | convolution fusion | flops 103579648 | bytes 1769472 | tf_op jit(solution)/shard_map/dot_general | solution.py:69
  37.9 0.3 fusion.4
  38.3 26.8 %all_to_all.15 = f32[32,36,128]{2,1,0:T(8,128)S(1)} all-to-all(f32[32,36,128]{2,1,0:T(8,128)S(1)} %reshape.31), channel_id=1, replica_groups=mesh['lon_chip'=16,'core'=2,'lat_z'=8,'lat_pair'=2] {'lon_chip','lat_pair'}, dimensions={0} | all-to-all | bytes 1179648 | tf_op jit(solution)/shard_map/all_to_all | solution.py:33
  65.1 17.3 %all_to_all.16 = f32[8,36,128]{2,1,0:T(8,128)S(1)} all-to-all(f32[8,36,128]{2,1,0:T(8,128)S(1)} %broadcast_in_dim.20), channel_id=1, replica_groups=mesh['lon_chip'=16,'core'=2,'lat_z'=8,'lat_pair'=2] {'lat_z'}, dimensions={0} | all-to-all | bytes 294912 | tf_op jit(solution)/shard_map/all_to_all | solution.py:39
  82.5 15.4 %all_to_all.17 = bf16[32,36,128]{2,1,0:T(8,128)(2,1)S(1)} all-to-all(bf16[32,36,128]{2,1,0:T(8,128)(2,1)S(1)} %broadcast_in_dim.21), channel_id=1, replica_groups=mesh['lon_chip'=16,'core'=2,'lat_z'=8,'lat_pair'=2] {'lon_chip','lat_pair'}, dimensions={0} | all-to-all | bytes 589824 | tf_op jit(solution)/shard_map/all_to_all | solution.py:39
  98.0 6.4 %collective-permute-start.5 = (bf16[1152,128]{1,0:T(8,128)(2,1)S(1)}, bf16[1152,128]{1,0:T(8,128)(2,1)S(1)}, u32[]{:S(2)}, u32[]{:S(2)}) collective-permute-start(bf16[1152,128]{1,0:T(8,128)(2,1)S(1)} %reshape.32), channel_id=1, source_target_pairs={{0,16},{16,0},{1,17},{17,1},{2,18},{18,2},{3,19},{19,3},{4,20},{20... | collective-permute-start | bytes 884744 | tf_op jit(solution)/shard_map/ppermute | solution.py:94
  104.4 1.2 %collective-permute-done.5 = bf16[1152,128]{1,0:T(8,128)(2,1)S(1)} collective-permute-done((bf16[1152,128]{1,0:T(8,128)(2,1)S(1)}, bf16[1152,128]{1,0:T(8,128)(2,1)S(1)}, u32[]{:S(2)}, u32[]{:S(2)}) %collective-permute-start.5) | collective-permute-done | bytes 294944 | tf_op jit(solution)/shard_map/ppermute | solution.py:94
  105.6 0.9 convert.2
  106.4 0.9 convert.3
  (34 shorter events, 2.3 us)
Async XLA Ops:
  0.6 11.6 %copy-start.2 = (bf16[3,3,128,128]{3,2,1,0:T(8,128)(2,1)S(1)}, bf16[3,3,128,128]{3,2,1,0:T(8,128)(2,1)}, u32[]{:S(2)}) copy-start(bf16[3,3,128,128]{3,2,1,0:T(8,128)(2,1)} %param.6) | copy-start | bytes 884740
  0.6 11.7 %copy-start.3 = (bf16[3,3,128,128]{3,2,1,0:T(8,128)(2,1)S(1)}, bf16[3,3,128,128]{3,2,1,0:T(8,128)(2,1)}, u32[]{:S(2)}) copy-start(bf16[3,3,128,128]{3,2,1,0:T(8,128)(2,1)} %param.5) | copy-start | bytes 884740
  1.6 11.3 %collective-permute-start = (bf16[2,16,2,128]{3,2,1,0:T(2,128)(2,1)S(1)}, bf16[2,16,2,128]{3,2,1,0:T(2,128)(2,1)S(1)}, u32[]{:S(2)}, u32[]{:S(2)}) collective-permute-start(bf16[2,16,2,128]{3,2,1,0:T(2,128)(2,1)S(1)} %get-tuple-element.13), channel_id=1, source_target_pairs={{0,16},{16,32},{32,48},{48,64},{64,80},{80,96},{96,112},{112,128},... | collective-permute-start | bytes 49160 | tf_op jit(solution)/shard_map/ppermute | solution.py:17
  6.1 7.0 %collective-permute-start.1 = (bf16[2,16,2,128]{3,2,1,0:T(2,128)(2,1)S(1)}, bf16[2,16,2,128]{3,2,1,0:T(2,128)(2,1)S(1)}, u32[]{:S(2)}, u32[]{:S(2)}) collective-permute-start(bf16[2,16,2,128]{3,2,1,0:T(2,128)(2,1)S(1)} %get-tuple-element.14), channel_id=1, source_target_pairs={{16,0},{32,16},{48,32},{64,48},{80,64},{96,80},{112,96},{128,112},... | collective-permute-start | bytes 49160 | tf_op jit(solution)/shard_map/ppermute | solution.py:20
  12.3 1.0 copy-start
  12.4 1.0 copy-start.1
  13.4 2.7 %collective-permute-start.2 = (bf16[2,2,68,128]{3,2,1,0:T(8,128)(2,1)S(1)}, bf16[2,2,68,128]{3,2,1,0:T(8,128)(2,1)S(1)}, u32[]{:S(2)}, u32[]{:S(2)}) collective-permute-start(bf16[2,2,68,128]{3,2,1,0:T(8,128)(2,1)S(1)} %get-tuple-element.11), channel_id=1, source_target_pairs={{0,1},{1,2},{2,3},{3,4},{4,5},{5,6},{6,7},{7,8},{8,9},{9,10},{10,1... | collective-permute-start | bytes 208904 | tf_op jit(solution)/shard_map/ppermute | solution.py:17
  14.7 5.6 %collective-permute-start.3 = (bf16[2,2,68,128]{3,2,1,0:T(8,128)(2,1)S(1)}, bf16[2,2,68,128]{3,2,1,0:T(8,128)(2,1)S(1)}, u32[]{:S(2)}, u32[]{:S(2)}) collective-permute-start(bf16[2,2,68,128]{3,2,1,0:T(8,128)(2,1)S(1)} %get-tuple-element.12), channel_id=1, source_target_pairs={{1,0},{2,1},{3,2},{4,3},{5,4},{6,5},{7,6},{8,7},{9,8},{10,9},{11,1... | collective-permute-start | bytes 208904 | tf_op jit(solution)/shard_map/ppermute | solution.py:20
  27.2 10.6 %collective-permute-start.4 = (f32[1152,128]{1,0:T(8,128)S(1)}, f32[1152,128]{1,0:T(8,128)S(1)}, u32[]{:S(2)}, u32[]{:S(2)}) collective-permute-start(f32[1152,128]{1,0:T(8,128)S(1)} %fusion.5), channel_id=1, source_target_pairs={{0,16},{16,0},{1,17},{17,1},{2,18},{18,2},{3,19},{19,3},{4,20},{20... | collective-permute-start | bytes 1769480 | tf_op jit(solution)/shard_map/ppermute | solution.py:94
  98.0 7.6 %collective-permute-start.5 = (bf16[1152,128]{1,0:T(8,128)(2,1)S(1)}, bf16[1152,128]{1,0:T(8,128)(2,1)S(1)}, u32[]{:S(2)}, u32[]{:S(2)}) collective-permute-start(bf16[1152,128]{1,0:T(8,128)(2,1)S(1)} %reshape.32), channel_id=1, source_target_pairs={{0,16},{16,0},{1,17},{17,1},{2,18},{18,2},{3,19},{19,3},{4,20},{20... | collective-permute-start | bytes 884744 | tf_op jit(solution)/shard_map/ppermute | solution.py:94

commit v12 on v11

--- a/solution.py
+++ b/solution.py
@@ -105,12 +105,11 @@
     portion = sent_and_summed(chip_sum, spread, 0)
     portion = taken_together(portion, "lat_z").astype(jnp.bfloat16)
     gathered = collect(portion, spread, 0)
+    slots = jnp.zeros((2, *gathered.shape), jnp.float32)
+    slots = lax.dynamic_update_slice_in_dim(slots, gathered.astype(jnp.float32)[None], core, 0)
     partner = with_partner(gathered)
-    return (
-        decoded,
-        jnp.where(core == 0, gathered, partner).astype(jnp.float32),
-        jnp.where(core == 0, partner, gathered).astype(jnp.float32),
-    )
+    slots = lax.dynamic_update_slice_in_dim(slots, partner.astype(jnp.float32)[None], 1 - core, 0)
+    return decoded, slots[0], slots[1]
 
 
 def shards(latent_frame, weights_in, weights_out, cotangent):

time: 108 us -> 107 us (level)
  local copies, waits for them, and re-layouts: 1.96 us -> 4.37 us
  other arithmetic: 3.84 us -> 2.11 us
    reshape x2 -> x0, other arithmetic: 1.72 us -> none  [the longest x1 0.86 us: shards(): grad_in = grad_in.reshape(3, 3, channels, channels)]
    slice x0 -> x1, local copies, waits for them, and re-layouts: none -> 1.09 us  [reduced_everywhere(): return (decoded, slots[0], slots[1])]
  transfers between devices with their start and end apart: 6 -> 6, of which waited for: 4 -> 3; matrix products, arithmetic and copies ran while one was open for 2% -> 3% of each run, Pallas kernels for 0% -> 0%
where the time goes in v12:
time: 107 us
  blocking collectives  58.8 us (55%)
  starting transfers between devices  28.6 us (27%)
  matrix products  6.94 us (6%)
  waiting for transfers between devices  4.77 us (4%)
  local copies, waits for them, and re-layouts  4.37 us (4%)
  other arithmetic  2.11 us (2%)
    all_to_all x2, blocking collectives, sent_to_all(): return lax.all_to_all(copies, axis, split_axis=0, concat_axis=0, tiled=True)  32.7 us
    all_to_all x1, blocking collectives, sent_and_summed(): lax.all_to_all(blocks, axis, split_axis=0, concat_axis=0, tiled=True)  26.1 us
    ppermute x2, starting transfers between devices, with_partner(): return lax.ppermute(x, 'core', [(0, 1), (1, 0)])  15.4 us
    ppermute x2, starting transfers between devices, with_halo(): lax.ppermute(lax.slice_in_dim(block, 0, width, axis=dim), axis, backward)  7.46 us
    ppermute x2, starting transfers between devices, with_halo(): lax.ppermute(lax.slice_in_dim(block, block.shape[dim] - width, None, axis...  5.79 us
    dot_general x9, matrix products, conv_tile(): jnp.dot(stacked[row_tap:row_tap + rows_out], weights[row_tap].reshape(-1,...  4.5 us
    ppermute x2, waiting for transfers between devices, with_halo(): lax.ppermute(lax.slice_in_dim(block, 0, width, axis=dim), axis, backward)  3.71 us
    dot_general x6, matrix products, weight_terms(): lax.dot_general(stacked[row_tap:row_tap + rows_out], gradient, (((0, 1),...  2.44 us
  transfers between devices with their start and end apart: 6, of which 3 were waited for; matrix products, arithmetic and copies ran while one was open for 3% of the time, Pallas kernels for 0%

profile of v12, /device:TPU:1, one launch (start us, length us, event | category | flops | bytes accessed | tf_op | source)
XLA Modules:
  0.0 106.7 jit_solution(2636046592284838409)
XLA Ops:
  0.7 0.9 pad_maximum_fusion.12
  1.6 4.5 %collective-permute-start = (bf16[2,16,2,128]{3,2,1,0:T(2,128)(2,1)S(1)}, bf16[2,16,2,128]{3,2,1,0:T(2,128)(2,1)S(1)}, u32[]{:S(2)}, u32[]{:S(2)}) collective-permute-start(bf16[2,16,2,128]{3,2,1,0:T(2,128)(2,1)S(1)} %get-tuple-element.13), channel_id=1, source_target_pairs={{0,16},{16,32},{32,48},{48,64},{64,80},{80,96},{96,112},{112,128},... | collective-permute-start | bytes 49160 | tf_op jit(solution)/shard_map/ppermute | solution.py:17
  6.1 6.2 %collective-permute-start.1 = (bf16[2,16,2,128]{3,2,1,0:T(2,128)(2,1)S(1)}, bf16[2,16,2,128]{3,2,1,0:T(2,128)(2,1)S(1)}, u32[]{:S(2)}, u32[]{:S(2)}) collective-permute-start(bf16[2,16,2,128]{3,2,1,0:T(2,128)(2,1)S(1)} %get-tuple-element.14), channel_id=1, source_target_pairs={{16,0},{32,16},{48,32},{64,48},{80,64},{96,80},{112,96},{128,112},... | collective-permute-start | bytes 49160 | tf_op jit(solution)/shard_map/ppermute | solution.py:20
  12.2 1.0 fusion.15
  13.8 0.4 copy-done
  14.4 1.3 %collective-permute-start.2 = (bf16[2,2,68,128]{3,2,1,0:T(8,128)(2,1)S(1)}, bf16[2,2,68,128]{3,2,1,0:T(8,128)(2,1)S(1)}, u32[]{:S(2)}, u32[]{:S(2)}) collective-permute-start(bf16[2,2,68,128]{3,2,1,0:T(8,128)(2,1)S(1)} %get-tuple-element.11), channel_id=1, source_target_pairs={{0,1},{1,2},{2,3},{3,4},{4,5},{5,6},{6,7},{7,8},{8,9},{9,10},{10,1... | collective-permute-start | bytes 208904 | tf_op jit(solution)/shard_map/ppermute | solution.py:17
  15.7 1.3 %collective-permute-start.3 = (bf16[2,2,68,128]{3,2,1,0:T(8,128)(2,1)S(1)}, bf16[2,2,68,128]{3,2,1,0:T(8,128)(2,1)S(1)}, u32[]{:S(2)}, u32[]{:S(2)}) collective-permute-start(bf16[2,2,68,128]{3,2,1,0:T(8,128)(2,1)S(1)} %get-tuple-element.12), channel_id=1, source_target_pairs={{1,0},{2,1},{3,2},{4,3},{5,4},{6,5},{7,6},{8,7},{9,8},{10,9},{11,1... | collective-permute-start | bytes 208904 | tf_op jit(solution)/shard_map/ppermute | solution.py:20
  17.0 3.7 %collective-permute-done.3 = bf16[2,2,68,128]{3,2,1,0:T(8,128)(2,1)S(1)} collective-permute-done((bf16[2,2,68,128]{3,2,1,0:T(8,128)(2,1)S(1)}, bf16[2,2,68,128]{3,2,1,0:T(8,128)(2,1)S(1)}, u32[]{:S(2)}, u32[]{:S(2)}) %collective-permute-start.3) | collective-permute-done | bytes 69664 | tf_op jit(solution)/shard_map/ppermute | solution.py:20
  21.3 0.5 fusion.8
  21.8 0.5 convolution_add_fusion.1
  22.3 0.5 fusion.6
  23.1 0.4 convolution_bitcast_fusion.2
  23.5 0.4 convolution_bitcast_fusion.1
  23.9 0.4 convolution_bitcast_fusion
  24.3 0.5 fusion.11
  24.8 0.4 fusion.7
  25.2 0.4 convolution_add_fusion.5
  25.6 0.4 fusion.1
  26.0 0.4 convolution_bitcast_fusion.5
  26.4 0.4 convolution_bitcast_fusion.4
  26.8 0.4 convolution_bitcast_fusion.3
  27.3 0.4 fusion.5
  27.7 9.0 %collective-permute-start.4 = (f32[1152,128]{1,0:T(8,128)S(1)}, f32[1152,128]{1,0:T(8,128)S(1)}, u32[]{:S(2)}, u32[]{:S(2)}) collective-permute-start(f32[1152,128]{1,0:T(8,128)S(1)} %fusion.5), channel_id=1, source_target_pairs={{0,16},{16,0},{1,17},{17,1},{2,18},{18,2},{3,19},{19,3},{4,20},{20... | collective-permute-start | bytes 1769480 | tf_op jit(solution)/shard_map/ppermute | solution.py:94
  36.7 0.4 fusion.9
  37.1 0.4 convolution_add_fusion.3
  37.4 1.1 %fusion.2 = bf16[16,64,128]{2,1,0:T(8,128)(2,1)} fusion(f32[16,64,128]{2,1,0:T(8,128)S(1)} %convolution_add_fusion.3, bf16[384,128,1]{1,0,2:T(8,128)(2,1)S(1)} %bitcast.87, bf16[18,64,128]{2,1,0:T(8,128)(2,1)S(1)} %get-tuple-element.25, bf16[18,64,128]{2,1,0:T(8,128)(2,1)S(1)} %get-tuple-element.26, bf16[18,64,128]{2,1,0:T(8,128)(2,1)S(1)} %get-tuple-element.24), kind=kOutput, calls=%fused_computation.12 | convolution fusion | flops 103579648 | bytes 1769472 | tf_op jit(solution)/shard_map/dot_general | solution.py:69
  38.9 26.1 %all_to_all.15 = f32[32,36,128]{2,1,0:T(8,128)S(1)} all-to-all(f32[32,36,128]{2,1,0:T(8,128)S(1)} %reshape.31), channel_id=1, replica_groups=mesh['lon_chip'=16,'core'=2,'lat_z'=8,'lat_pair'=2] {'lon_chip','lat_pair'}, dimensions={0} | all-to-all | bytes 1179648 | tf_op jit(solution)/shard_map/all_to_all | solution.py:33
  65.1 17.3 %all_to_all.16 = f32[8,36,128]{2,1,0:T(8,128)S(1)} all-to-all(f32[8,36,128]{2,1,0:T(8,128)S(1)} %broadcast_in_dim.31), channel_id=1, replica_groups=mesh['lon_chip'=16,'core'=2,'lat_z'=8,'lat_pair'=2] {'lat_z'}, dimensions={0} | all-to-all | bytes 294912 | tf_op jit(solution)/shard_map/all_to_all | solution.py:39
  82.5 15.4 %all_to_all.17 = bf16[32,36,128]{2,1,0:T(8,128)(2,1)S(1)} all-to-all(bf16[32,36,128]{2,1,0:T(8,128)(2,1)S(1)} %broadcast_in_dim.32), channel_id=1, replica_groups=mesh['lon_chip'=16,'core'=2,'lat_z'=8,'lat_pair'=2] {'lon_chip','lat_pair'}, dimensions={0} | all-to-all | bytes 589824 | tf_op jit(solution)/shard_map/all_to_all | solution.py:39
  98.0 6.4 %collective-permute-start.5 = (bf16[1152,128]{1,0:T(8,128)(2,1)S(1)}, bf16[1152,128]{1,0:T(8,128)(2,1)S(1)}, u32[]{:S(2)}, u32[]{:S(2)}) collective-permute-start(bf16[1152,128]{1,0:T(8,128)(2,1)S(1)} %reshape.32), channel_id=1, source_target_pairs={{0,16},{16,0},{1,17},{17,1},{2,18},{18,2},{3,19},{19,3},{4,20},{20... | collective-permute-start | bytes 884744 | tf_op jit(solution)/shard_map/ppermute | solution.py:94
  104.5 1.0 collective-permute-done.5
  105.6 1.1 %fusion.10 = (f32[1,1152,128]{2,1,0:T(8,128)}, f32[1,1152,128]{2,1,0:T(8,128)}) fusion(f32[2,1152,128]{2,1,0:T(8,128)S(1)} %convert_dynamic-update-slice_fusion), kind=kLoop, calls=%fused_computation.46 | loop fusion | bytes 2359296 | tf_op jit(solution)/shard_map/slice | solution.py:112
  (36 shorter events, 2.3 us)
Async XLA Ops:
  0.6 12.6 %copy-start.2 = (bf16[3,3,128,128]{3,2,1,0:T(8,128)(2,1)S(1)}, bf16[3,3,128,128]{3,2,1,0:T(8,128)(2,1)}, u32[]{:S(2)}) copy-start(bf16[3,3,128,128]{3,2,1,0:T(8,128)(2,1)} %param.6) | copy-start | bytes 884740
  0.6 12.7 %copy-start.3 = (bf16[3,3,128,128]{3,2,1,0:T(8,128)(2,1)S(1)}, bf16[3,3,128,128]{3,2,1,0:T(8,128)(2,1)}, u32[]{:S(2)}) copy-start(bf16[3,3,128,128]{3,2,1,0:T(8,128)(2,1)} %param.5) | copy-start | bytes 884740
  1.6 12.3 %collective-permute-start = (bf16[2,16,2,128]{3,2,1,0:T(2,128)(2,1)S(1)}, bf16[2,16,2,128]{3,2,1,0:T(2,128)(2,1)S(1)}, u32[]{:S(2)}, u32[]{:S(2)}) collective-permute-start(bf16[2,16,2,128]{3,2,1,0:T(2,128)(2,1)S(1)} %get-tuple-element.13), channel_id=1, source_target_pairs={{0,16},{16,32},{32,48},{48,64},{64,80},{80,96},{96,112},{112,128},... | collective-permute-start | bytes 49160 | tf_op jit(solution)/shard_map/ppermute | solution.py:17
  6.1 7.8 %collective-permute-start.1 = (bf16[2,16,2,128]{3,2,1,0:T(2,128)(2,1)S(1)}, bf16[2,16,2,128]{3,2,1,0:T(2,128)(2,1)S(1)}, u32[]{:S(2)}, u32[]{:S(2)}) collective-permute-start(bf16[2,16,2,128]{3,2,1,0:T(2,128)(2,1)S(1)} %get-tuple-element.14), channel_id=1, source_target_pairs={{16,0},{32,16},{48,32},{64,48},{80,64},{96,80},{112,96},{128,112},... | collective-permute-start | bytes 49160 | tf_op jit(solution)/shard_map/ppermute | solution.py:20
  13.3 1.0 copy-start
  13.3 1.0 copy-start.1
  14.4 2.7 %collective-permute-start.2 = (bf16[2,2,68,128]{3,2,1,0:T(8,128)(2,1)S(1)}, bf16[2,2,68,128]{3,2,1,0:T(8,128)(2,1)S(1)}, u32[]{:S(2)}, u32[]{:S(2)}) collective-permute-start(bf16[2,2,68,128]{3,2,1,0:T(8,128)(2,1)S(1)} %get-tuple-element.11), channel_id=1, source_target_pairs={{0,1},{1,2},{2,3},{3,4},{4,5},{5,6},{6,7},{7,8},{8,9},{9,10},{10,1... | collective-permute-start | bytes 208904 | tf_op jit(solution)/shard_map/ppermute | solution.py:17
  15.7 5.1 %collective-permute-start.3 = (bf16[2,2,68,128]{3,2,1,0:T(8,128)(2,1)S(1)}, bf16[2,2,68,128]{3,2,1,0:T(8,128)(2,1)S(1)}, u32[]{:S(2)}, u32[]{:S(2)}) collective-permute-start(bf16[2,2,68,128]{3,2,1,0:T(8,128)(2,1)S(1)} %get-tuple-element.12), channel_id=1, source_target_pairs={{1,0},{2,1},{3,2},{4,3},{5,4},{6,5},{7,6},{8,7},{9,8},{10,9},{11,1... | collective-permute-start | bytes 208904 | tf_op jit(solution)/shard_map/ppermute | solution.py:20
  27.7 10.8 %collective-permute-start.4 = (f32[1152,128]{1,0:T(8,128)S(1)}, f32[1152,128]{1,0:T(8,128)S(1)}, u32[]{:S(2)}, u32[]{:S(2)}) collective-permute-start(f32[1152,128]{1,0:T(8,128)S(1)} %fusion.5), channel_id=1, source_target_pairs={{0,16},{16,0},{1,17},{17,1},{2,18},{18,2},{3,19},{19,3},{4,20},{20... | collective-permute-start | bytes 1769480 | tf_op jit(solution)/shard_map/ppermute | solution.py:94
  98.0 7.6 %collective-permute-start.5 = (bf16[1152,128]{1,0:T(8,128)(2,1)S(1)}, bf16[1152,128]{1,0:T(8,128)(2,1)S(1)}, u32[]{:S(2)}, u32[]{:S(2)}) collective-permute-start(bf16[1152,128]{1,0:T(8,128)(2,1)S(1)} %reshape.32), channel_id=1, source_target_pairs={{0,16},{16,0},{1,17},{17,1},{2,18},{18,2},{3,19},{19,3},{4,20},{20... | collective-permute-start | bytes 884744 | tf_op jit(solution)/shard_map/ppermute | solution.py:94

commit v13 on v12

--- a/solution.py
+++ b/solution.py
@@ -63,14 +63,13 @@
 def conv_tile(padded, weights):
     rows_out = padded.shape[0] - 2
     cols_out = padded.shape[1] - 2
+    channels, width = weights.shape[2], weights.shape[3]
     stacked = column_taps(padded, cols_out)
+    merged = jnp.transpose(weights, (1, 2, 0, 3)).reshape(3 * channels, 3 * width)
+    spread = jnp.dot(stacked, merged, preferred_element_type=jnp.float32)
     summed = None
     for row_tap in range(3):
-        part = jnp.dot(
-            stacked[row_tap : row_tap + rows_out],
-            weights[row_tap].reshape(-1, weights.shape[3]),
-            preferred_element_type=jnp.float32,
-        )
+        part = spread[row_tap : row_tap + rows_out, :, row_tap * width : (row_tap + 1) * width]
         summed = part if summed is None else summed + part
     return summed
 
@@ -78,16 +77,15 @@
 def weight_terms(padded, gradient):
     rows_out, cols_out, channels = gradient.shape
     stacked = column_taps(padded, cols_out)
-    taps = [
-        lax.dot_general(
-            stacked[row_tap : row_tap + rows_out],
-            gradient,
-            (((0, 1), (0, 1)), ((), ())),
-            preferred_element_type=jnp.float32,
-        )
-        for row_tap in range(3)
-    ]
-    return jnp.stack(taps).reshape(3, 3, padded.shape[2], channels)
+    shifted = jnp.concatenate(
+        [jnp.pad(gradient, ((row_tap, 2 - row_tap), (0, 0), (0, 0))) for row_tap in range(3)],
+        axis=-1,
+    )
+    terms = lax.dot_general(
+        stacked, shifted, (((0, 1), (0, 1)), ((), ())), preferred_element_type=jnp.float32
+    )
+    terms = terms.reshape(3, padded.shape[2], 3, channels)
+    return jnp.transpose(terms, (2, 0, 1, 3))
 
 
 def with_partner(x):

time: 107 us -> 109 us (1.019)
  local copies, waits for them, and re-layouts: 4.37 us -> 8.38 us
  matrix products: 6.94 us -> 4.71 us
  other arithmetic: 2.11 us -> 3.25 us
    dot_general x15 -> x5, matrix products: 6.94 us -> 4.71 us  [the longest x3 3.36 us: conv_tile(): spread = jnp.dot(stacked, merged, preferred_element_type=jnp.float32)]
    reshape x0 -> x5, local copies, waits for them, and re-layouts: none -> 1.95 us  [the longest x3 1.47 us: conv_tile(): jnp.transpose(weights, (1, 2, 0, 3)).reshape(3 * channels, 3 * width)]
    transpose x1 -> x4, local copies, waits for them, and re-layouts: 0.02 us -> 1.56 us  [the longest x2 1.48 us: conv_tile(): jnp.transpose(weights, (1, 2, 0, 3)).reshape(3 * channels, 3 * width)]
    slice x6 -> x0, local copies, waits for them, and re-layouts: 1.44 us -> none  [conv_tile(): weights[row_tap].reshape(-1, weights.shape[3])]
    all_to_all x1, blocking collectives: 26.1 us -> 24.7 us  [sent_and_summed(): lax.all_to_all(blocks, axis, split_axis=0, concat_axis=0, tiled=True)]
    another operation x0 -> x2, local copies, waits for them, and re-layouts: none -> 1.23 us  [conv_tile(): jnp.transpose(weights, (1, 2, 0, 3)).reshape(3 * channels, 3 * width)]
  transfers between devices with their start and end apart: 6 -> 6, of which waited for: 3 -> 3; matrix products, arithmetic and copies ran while one was open for 3% -> 6% of each run, Pallas kernels for 0% -> 0%
where the time goes in v13:
time: 109 us
  blocking collectives  57.8 us (53%)
  starting transfers between devices  28.6 us (26%)
  local copies, waits for them, and re-layouts  8.38 us (8%)
  waiting for transfers between devices  4.77 us (4%)
  matrix products  4.71 us (4%)
  other arithmetic  3.25 us (3%)
    all_to_all x2, blocking collectives, sent_to_all(): return lax.all_to_all(copies, axis, split_axis=0, concat_axis=0, tiled=True)  33.1 us
    all_to_all x1, blocking collectives, sent_and_summed(): lax.all_to_all(blocks, axis, split_axis=0, concat_axis=0, tiled=True)  24.7 us
    ppermute x2, starting transfers between devices, with_partner(): return lax.ppermute(x, 'core', [(0, 1), (1, 0)])  15.2 us
    ppermute x2, starting transfers between devices, with_halo(): lax.ppermute(lax.slice_in_dim(block, 0, width, axis=dim), axis, backward)  7.46 us
    ppermute x2, starting transfers between devices, with_halo(): lax.ppermute(lax.slice_in_dim(block, block.shape[dim] - width, None, axis...  5.92 us
    ppermute x2, waiting for transfers between devices, with_halo(): lax.ppermute(lax.slice_in_dim(block, 0, width, axis=dim), axis, backward)  3.71 us
    dot_general x3, matrix products, conv_tile(): spread = jnp.dot(stacked, merged, preferred_element_type=jnp.float32)  3.36 us
  transfers between devices with their start and end apart: 6, of which 3 were waited for; matrix products, arithmetic and copies ran while one was open for 6% of the time, Pallas kernels for 0%

profile of v13, /device:TPU:1, one launch (start us, length us, event | category | flops | bytes accessed | tf_op | source)
XLA Modules:
  0.0 108.5 jit_solution(18144096053958236690)
XLA Ops:
  0.6 0.8 pad_maximum_fusion.9
  1.5 4.6 %collective-permute-start = (bf16[2,16,2,128]{3,2,1,0:T(2,128)(2,1)S(1)}, bf16[2,16,2,128]{3,2,1,0:T(2,128)(2,1)S(1)}, u32[]{:S(2)}, u32[]{:S(2)}) collective-permute-start(bf16[2,16,2,128]{3,2,1,0:T(2,128)(2,1)S(1)} %get-tuple-element.15), channel_id=1, source_target_pairs={{0,16},{16,32},{32,48},{48,64},{64,80},{80,96},{96,112},{112,128},... | collective-permute-start | bytes 49160 | tf_op jit(solution)/shard_map/ppermute | solution.py:17
  6.1 6.2 %collective-permute-start.1 = (bf16[2,16,2,128]{3,2,1,0:T(2,128)(2,1)S(1)}, bf16[2,16,2,128]{3,2,1,0:T(2,128)(2,1)S(1)}, u32[]{:S(2)}, u32[]{:S(2)}) collective-permute-start(bf16[2,16,2,128]{3,2,1,0:T(2,128)(2,1)S(1)} %get-tuple-element.16), channel_id=1, source_target_pairs={{16,0},{32,16},{48,32},{64,48},{80,64},{96,80},{112,96},{128,112},... | collective-permute-start | bytes 49160 | tf_op jit(solution)/shard_map/ppermute | solution.py:20
  12.3 1.0 reverse_bitcast_fusion
  13.3 1.2 %copy.18 = bf16[3,128,3,128]{3,2,1,0:T(4,128)(2,1)S(1)} copy(bf16[3,128,3,128]{3,1,0,2:T(8,128)(2,1)} %bitcast.41) | data formatting | bytes 589824 | tf_op jit(solution)/shard_map/transpose | solution.py:68
  14.5 0.3 reshape.64
  15.0 1.0 reshape.63
  16.1 1.3 %collective-permute-start.2 = (bf16[2,2,68,128]{3,2,1,0:T(8,128)(2,1)S(1)}, bf16[2,2,68,128]{3,2,1,0:T(8,128)(2,1)S(1)}, u32[]{:S(2)}, u32[]{:S(2)}) collective-permute-start(bf16[2,2,68,128]{3,2,1,0:T(8,128)(2,1)S(1)} %get-tuple-element.13), channel_id=1, source_target_pairs={{0,1},{1,2},{2,3},{3,4},{4,5},{5,6},{6,7},{7,8},{8,9},{9,10},{10,1... | collective-permute-start | bytes 208904 | tf_op jit(solution)/shard_map/ppermute | solution.py:17
  17.4 1.3 %collective-permute-start.3 = (bf16[2,2,68,128]{3,2,1,0:T(8,128)(2,1)S(1)}, bf16[2,2,68,128]{3,2,1,0:T(8,128)(2,1)S(1)}, u32[]{:S(2)}, u32[]{:S(2)}) collective-permute-start(bf16[2,2,68,128]{3,2,1,0:T(8,128)(2,1)S(1)} %get-tuple-element.14), channel_id=1, source_target_pairs={{1,0},{2,1},{3,2},{4,3},{5,4},{6,5},{7,6},{8,7},{9,8},{10,9},{11,1... | collective-permute-start | bytes 208904 | tf_op jit(solution)/shard_map/ppermute | solution.py:20
  18.8 3.7 %collective-permute-done.3 = bf16[2,2,68,128]{3,2,1,0:T(8,128)(2,1)S(1)} collective-permute-done((bf16[2,2,68,128]{3,2,1,0:T(8,128)(2,1)S(1)}, bf16[2,2,68,128]{3,2,1,0:T(8,128)(2,1)S(1)}, u32[]{:S(2)}, u32[]{:S(2)}) %collective-permute-start.3) | collective-permute-done | bytes 69664 | tf_op jit(solution)/shard_map/ppermute | solution.py:20
  22.5 0.3 pad_maximum_fusion.1
  23.0 0.9 fusion.7
  24.4 0.7 copy-done.5
  25.2 0.7 convolution_bitcast_fusion
  26.2 0.5 fusion.66
  26.7 0.4 copy-done.7
  27.2 0.7 fusion.38
  27.9 0.3 fusion.49
  28.1 0.7 convolution_bitcast_fusion.1
  29.1 0.4 fusion.46
  29.5 9.0 %collective-permute-start.4 = (f32[1152,128]{1,0:T(8,128)S(1)}, f32[1152,128]{1,0:T(8,128)S(1)}, u32[]{:S(2)}, u32[]{:S(2)}) collective-permute-start(f32[1152,128]{1,0:T(8,128)S(1)} %fusion.46), channel_id=1, source_target_pairs={{0,16},{16,0},{1,17},{17,1},{2,18},{18,2},{3,19},{19,3},{4,20},{20... | collective-permute-start | bytes 1769480 | tf_op jit(solution)/shard_map/ppermute | solution.py:92
  38.5 0.3 copy.21
  38.8 0.3 reshape.67
  39.1 1.7 %fusion.52 = f32[18,64,384]{2,1,0:T(8,128)S(1)} fusion(bf16[384,384,1]{1,0,2:T(8,128)(2,1)S(1)} %reshape.67, bf16[18,64,128]{2,1,0:T(8,128)(2,1)} %copy-done.5, bf16[18,64,128]{2,1,0:T(8,128)(2,1)} %copy-done.6, bf16[18,64,128]{2,1,0:T(8,128)(2,1)S(1)} %copy-done.4), kind=kOutput, calls=%fused_computation.68 | convolution fusion | flops 342392832 | bytes 2949120 | tf_op jit(solution)/shard_map/dot_general | solution.py:69
  40.8 0.8 fusion.47
  41.6 0.3 fusion.45
  42.0 24.7 %all_to_all.15 = f32[32,36,128]{2,1,0:T(8,128)S(1)} all-to-all(f32[32,36,128]{2,1,0:T(8,128)S(1)} %reshape.59), channel_id=1, replica_groups=mesh['lon_chip'=16,'core'=2,'lat_z'=8,'lat_pair'=2] {'lon_chip','lat_pair'}, dimensions={0} | all-to-all | bytes 1179648 | tf_op jit(solution)/shard_map/all_to_all | solution.py:33
  66.8 17.5 %all_to_all.16 = f32[8,36,128]{2,1,0:T(8,128)S(1)} all-to-all(f32[8,36,128]{2,1,0:T(8,128)S(1)} %broadcast_in_dim.31), channel_id=1, replica_groups=mesh['lon_chip'=16,'core'=2,'lat_z'=8,'lat_pair'=2] {'lat_z'}, dimensions={0} | all-to-all | bytes 294912 | tf_op jit(solution)/shard_map/all_to_all | solution.py:39
  84.3 15.6 %all_to_all.17 = bf16[32,36,128]{2,1,0:T(8,128)(2,1)S(1)} all-to-all(bf16[32,36,128]{2,1,0:T(8,128)(2,1)S(1)} %broadcast_in_dim.32), channel_id=1, replica_groups=mesh['lon_chip'=16,'core'=2,'lat_z'=8,'lat_pair'=2] {'lon_chip','lat_pair'}, dimensions={0} | all-to-all | bytes 589824 | tf_op jit(solution)/shard_map/all_to_all | solution.py:39
  100.0 6.2 %collective-permute-start.5 = (bf16[1152,128]{1,0:T(8,128)(2,1)S(1)}, bf16[1152,128]{1,0:T(8,128)(2,1)S(1)}, u32[]{:S(2)}, u32[]{:S(2)}) collective-permute-start(bf16[1152,128]{1,0:T(8,128)(2,1)S(1)} %reshape.60), channel_id=1, source_target_pairs={{0,16},{16,0},{1,17},{17,1},{2,18},{18,2},{3,19},{19,3},{4,20},{20... | collective-permute-start | bytes 884744 | tf_op jit(solution)/shard_map/ppermute | solution.py:92
  106.4 1.0 collective-permute-done.5
  107.4 1.1 %fusion.65 = (f32[1,1152,128]{2,1,0:T(8,128)}, f32[1,1152,128]{2,1,0:T(8,128)}) fusion(f32[2,1152,128]{2,1,0:T(8,128)S(1)} %convert_dynamic-update-slice_fusion), kind=kLoop, calls=%fused_computation.90 | loop fusion | bytes 2359296 | tf_op jit(solution)/shard_map/slice | solution.py:110
  (39 shorter events, 2.2 us)
Async XLA Ops:
  1.5 14.5 %copy-start = (bf16[16,64,128]{2,1,0:T(8,128)(2,1)S(1)}, bf16[16,64,128]{2,1,0:T(8,128)(2,1)}, u32[]{:S(2)}) copy-start(bf16[16,64,128]{2,1,0:T(8,128)(2,1)} %param.4) | copy-start | bytes 786436
  1.5 14.5 %copy-start.1 = (bf16[16,64,128]{2,1,0:T(8,128)(2,1)S(1)}, bf16[16,64,128]{2,1,0:T(8,128)(2,1)}, u32[]{:S(2)}) copy-start(bf16[16,64,128]{2,1,0:T(8,128)(2,1)} %param.7) | copy-start | bytes 786436
  1.5 14.5 %collective-permute-start = (bf16[2,16,2,128]{3,2,1,0:T(2,128)(2,1)S(1)}, bf16[2,16,2,128]{3,2,1,0:T(2,128)(2,1)S(1)}, u32[]{:S(2)}, u32[]{:S(2)}) collective-permute-start(bf16[2,16,2,128]{3,2,1,0:T(2,128)(2,1)S(1)} %get-tuple-element.15), channel_id=1, source_target_pairs={{0,16},{16,32},{32,48},{48,64},{64,80},{80,96},{96,112},{112,128},... | collective-permute-start | bytes 49160 | tf_op jit(solution)/shard_map/ppermute | solution.py:17
  6.1 9.9 %collective-permute-start.1 = (bf16[2,16,2,128]{3,2,1,0:T(2,128)(2,1)S(1)}, bf16[2,16,2,128]{3,2,1,0:T(2,128)(2,1)S(1)}, u32[]{:S(2)}, u32[]{:S(2)}) collective-permute-start(bf16[2,16,2,128]{3,2,1,0:T(2,128)(2,1)S(1)} %get-tuple-element.16), channel_id=1, source_target_pairs={{16,0},{32,16},{48,32},{64,48},{80,64},{96,80},{112,96},{128,112},... | collective-permute-start | bytes 49160 | tf_op jit(solution)/shard_map/ppermute | solution.py:20
  16.1 2.7 %collective-permute-start.2 = (bf16[2,2,68,128]{3,2,1,0:T(8,128)(2,1)S(1)}, bf16[2,2,68,128]{3,2,1,0:T(8,128)(2,1)S(1)}, u32[]{:S(2)}, u32[]{:S(2)}) collective-permute-start(bf16[2,2,68,128]{3,2,1,0:T(8,128)(2,1)S(1)} %get-tuple-element.13), channel_id=1, source_target_pairs={{0,1},{1,2},{2,3},{3,4},{4,5},{5,6},{6,7},{7,8},{8,9},{9,10},{10,1... | collective-permute-start | bytes 208904 | tf_op jit(solution)/shard_map/ppermute | solution.py:17
  17.4 5.1 %collective-permute-start.3 = (bf16[2,2,68,128]{3,2,1,0:T(8,128)(2,1)S(1)}, bf16[2,2,68,128]{3,2,1,0:T(8,128)(2,1)S(1)}, u32[]{:S(2)}, u32[]{:S(2)}) collective-permute-start(bf16[2,2,68,128]{3,2,1,0:T(8,128)(2,1)S(1)} %get-tuple-element.14), channel_id=1, source_target_pairs={{1,0},{2,1},{3,2},{4,3},{5,4},{6,5},{7,6},{8,7},{9,8},{10,9},{11,1... | collective-permute-start | bytes 208904 | tf_op jit(solution)/shard_map/ppermute | solution.py:20
  24.4 0.7 copy-start.5
  24.4 0.8 copy-start.6
  24.4 1.5 %copy-start.3 = (bf16[18,64,128]{2,1,0:T(8,128)(2,1)}, bf16[18,64,128]{2,1,0:T(8,128)(2,1)S(1)}, u32[]{:S(2)}) copy-start(bf16[18,64,128]{2,1,0:T(8,128)(2,1)S(1)} %get-tuple-element.26) | copy-start | bytes 884740
  26.2 1.0 copy-start.7
  29.1 9.5 %copy-start.2 = (bf16[3,3,128,128]{3,2,1,0:T(8,128)(2,1)S(1)}, bf16[3,3,128,128]{3,2,1,0:T(8,128)(2,1)}, u32[]{:S(2)}) copy-start(bf16[3,3,128,128]{3,2,1,0:T(8,128)(2,1)} %param.6) | copy-start | bytes 884740
  29.1 9.9 %copy-start.4 = (bf16[18,64,128]{2,1,0:T(8,128)(2,1)S(1)}, bf16[18,64,128]{2,1,0:T(8,128)(2,1)}, u32[]{:S(2)}) copy-start(bf16[18,64,128]{2,1,0:T(8,128)(2,1)} %copy-done.3) | copy-start | bytes 884740
  29.5 12.1 %collective-permute-start.4 = (f32[1152,128]{1,0:T(8,128)S(1)}, f32[1152,128]{1,0:T(8,128)S(1)}, u32[]{:S(2)}, u32[]{:S(2)}) collective-permute-start(f32[1152,128]{1,0:T(8,128)S(1)} %fusion.46), channel_id=1, source_target_pairs={{0,16},{16,0},{1,17},{17,1},{2,18},{18,2},{3,19},{19,3},{4,20},{20... | collective-permute-start | bytes 1769480 | tf_op jit(solution)/shard_map/ppermute | solution.py:92
  100.0 7.4 %collective-permute-start.5 = (bf16[1152,128]{1,0:T(8,128)(2,1)S(1)}, bf16[1152,128]{1,0:T(8,128)(2,1)S(1)}, u32[]{:S(2)}, u32[]{:S(2)}) collective-permute-start(bf16[1152,128]{1,0:T(8,128)(2,1)S(1)} %reshape.60), channel_id=1, source_target_pairs={{0,16},{16,0},{1,17},{17,1},{2,18},{18,2},{3,19},{19,3},{4,20},{20... | collective-permute-start | bytes 884744 | tf_op jit(solution)/shard_map/ppermute | solution.py:92

commit v14 on v12

--- a/solution.py
+++ b/solution.py
@@ -75,6 +75,20 @@
     return summed
 
 
+def merged_conv(padded, weights):
+    rows_out = padded.shape[0] - 2
+    cols_out = padded.shape[1] - 2
+    channels, width = weights.shape[2], weights.shape[3]
+    stacked = column_taps(padded, cols_out)
+    merged = jnp.transpose(weights, (1, 2, 0, 3)).reshape(3 * channels, 3 * width)
+    spread = jnp.dot(stacked, merged, preferred_element_type=jnp.float32)
+    summed = None
+    for row_tap in range(3):
+        part = spread[row_tap : row_tap + rows_out, :, row_tap * width : (row_tap + 1) * width]
+        summed = part if summed is None else summed + part
+    return summed
+
+
 def weight_terms(padded, gradient):
     rows_out, cols_out, channels = gradient.shape
     stacked = column_taps(padded, cols_out)
@@ -121,7 +135,7 @@
     extended = with_halo(widened, ((LAT, 1),), margin, False)
     input_pad = extended[0]
     grad_pad = extended[1][1:-1, 1:-1]
-    preact_wide = conv_tile(input_pad, weights_in)
+    preact_wide = merged_conv(input_pad, weights_in)
     hidden_wide = jax.nn.silu(preact_wide).astype(jnp.bfloat16)
     global_row = lax.axis_index(LAT) * tile_rows - 1 + jnp.arange(tile_rows + 2, dtype=jnp.int32)
     inside = (global_row >= 0) & (global_row < tile_rows * lax.axis_size(LAT))
@@ -131,7 +145,7 @@
     decoded = conv_tile(hidden_pad, weights_out).astype(jnp.bfloat16)
     term_out = weight_terms(hidden_pad, cotangent)
     flipped = jnp.transpose(weights_out[::-1, ::-1], (0, 1, 3, 2))
-    grad_hidden = conv_tile(grad_pad, flipped)
+    grad_hidden = merged_conv(grad_pad, flipped)
     sigmoid_pre = jax.nn.sigmoid(preact)
     grad_pre = (grad_hidden * (sigmoid_pre * (1.0 + preact * (1.0 - sigmoid_pre)))).astype(
         jnp.bfloat16

time: 107 us -> 106 us (level)
  local copies, waits for them, and re-layouts: 4.37 us -> 5.49 us
  blocking collectives: 58.8 us -> 57.7 us
  matrix products: 6.94 us -> 5.85 us
    dot_general x9 -> x3, matrix products: 4.5 us -> 1.81 us  [conv_tile(): jnp.dot(stacked[row_tap:row_tap + rows_out], weights[row_tap].reshape(-1,...]
    dot_general x0 -> x2, matrix products: none -> 1.63 us  [merged_conv(): spread = jnp.dot(stacked, merged, preferred_element_type=jnp.float32)]
    another operation x0 -> x2, local copies, waits for them, and re-layouts: none -> 1.29 us  [merged_conv(): jnp.transpose(weights, (1, 2, 0, 3)).reshape(3 * channels, 3 * width)]
    all_to_all x1, blocking collectives: 26.1 us -> 25 us  [sent_and_summed(): lax.all_to_all(blocks, axis, split_axis=0, concat_axis=0, tiled=True)]
  transfers between devices with their start and end apart: 6 -> 6, of which waited for: 3 -> 3; matrix products, arithmetic and copies ran while one was open for 3% -> 5% of each run, Pallas kernels for 0% -> 0%
where the time goes in v14:
time: 106 us
  blocking collectives  57.7 us (54%)
  starting transfers between devices  28.6 us (27%)
  matrix products  5.85 us (6%)
  local copies, waits for them, and re-layouts  5.49 us (5%)
  waiting for transfers between devices  4.77 us (4%)
  other arithmetic  2.63 us (2%)
    all_to_all x2, blocking collectives, sent_to_all(): return lax.all_to_all(copies, axis, split_axis=0, concat_axis=0, tiled=True)  32.7 us
    all_to_all x1, blocking collectives, sent_and_summed(): lax.all_to_all(blocks, axis, split_axis=0, concat_axis=0, tiled=True)  25 us
    ppermute x2, starting transfers between devices, with_partner(): return lax.ppermute(x, 'core', [(0, 1), (1, 0)])  15.4 us
    ppermute x2, starting transfers between devices, with_halo(): lax.ppermute(lax.slice_in_dim(block, 0, width, axis=dim), axis, backward)  7.46 us
    ppermute x2, starting transfers between devices, with_halo(): lax.ppermute(lax.slice_in_dim(block, block.shape[dim] - width, None, axis...  5.79 us
    ppermute x2, waiting for transfers between devices, with_halo(): lax.ppermute(lax.slice_in_dim(block, 0, width, axis=dim), axis, backward)  3.71 us
    dot_general x6, matrix products, weight_terms(): lax.dot_general(stacked[row_tap:row_tap + rows_out], gradient, (((0, 1),...  2.42 us
  transfers between devices with their start and end apart: 6, of which 3 were waited for; matrix products, arithmetic and copies ran while one was open for 5% of the time, Pallas kernels for 0%

profile of v14, /device:TPU:1, one launch (start us, length us, event | category | flops | bytes accessed | tf_op | source)
XLA Modules:
  0.0 106.1 jit_solution(7627660244786390356)
XLA Ops:
  0.6 0.9 pad_maximum_fusion.10
  1.5 4.5 %collective-permute-start = (bf16[2,16,2,128]{3,2,1,0:T(2,128)(2,1)S(1)}, bf16[2,16,2,128]{3,2,1,0:T(2,128)(2,1)S(1)}, u32[]{:S(2)}, u32[]{:S(2)}) collective-permute-start(bf16[2,16,2,128]{3,2,1,0:T(2,128)(2,1)S(1)} %get-tuple-element.15), channel_id=1, source_target_pairs={{0,16},{16,32},{32,48},{48,64},{64,80},{80,96},{96,112},{112,128},... | collective-permute-start | bytes 49160 | tf_op jit(solution)/shard_map/ppermute | solution.py:17
  6.0 6.2 %collective-permute-start.1 = (bf16[2,16,2,128]{3,2,1,0:T(2,128)(2,1)S(1)}, bf16[2,16,2,128]{3,2,1,0:T(2,128)(2,1)S(1)}, u32[]{:S(2)}, u32[]{:S(2)}) collective-permute-start(bf16[2,16,2,128]{3,2,1,0:T(2,128)(2,1)S(1)} %get-tuple-element.16), channel_id=1, source_target_pairs={{16,0},{32,16},{48,32},{64,48},{80,64},{96,80},{112,96},{128,112},... | collective-permute-start | bytes 49160 | tf_op jit(solution)/shard_map/ppermute | solution.py:20
  12.2 1.0 fusion.27
  13.2 1.0 reverse_bitcast_fusion
  14.3 0.3 copy.12
  15.5 1.3 %collective-permute-start.2 = (bf16[2,2,68,128]{3,2,1,0:T(8,128)(2,1)S(1)}, bf16[2,2,68,128]{3,2,1,0:T(8,128)(2,1)S(1)}, u32[]{:S(2)}, u32[]{:S(2)}) collective-permute-start(bf16[2,2,68,128]{3,2,1,0:T(8,128)(2,1)S(1)} %get-tuple-element.13), channel_id=1, source_target_pairs={{0,1},{1,2},{2,3},{3,4},{4,5},{5,6},{6,7},{7,8},{8,9},{9,10},{10,1... | collective-permute-start | bytes 208904 | tf_op jit(solution)/shard_map/ppermute | solution.py:17
  16.8 1.3 %collective-permute-start.3 = (bf16[2,2,68,128]{3,2,1,0:T(8,128)(2,1)S(1)}, bf16[2,2,68,128]{3,2,1,0:T(8,128)(2,1)S(1)}, u32[]{:S(2)}, u32[]{:S(2)}) collective-permute-start(bf16[2,2,68,128]{3,2,1,0:T(8,128)(2,1)S(1)} %get-tuple-element.14), channel_id=1, source_target_pairs={{1,0},{2,1},{3,2},{4,3},{5,4},{6,5},{7,6},{8,7},{9,8},{10,9},{11,1... | collective-permute-start | bytes 208904 | tf_op jit(solution)/shard_map/ppermute | solution.py:20
  18.1 3.7 %collective-permute-done.3 = bf16[2,2,68,128]{3,2,1,0:T(8,128)(2,1)S(1)} collective-permute-done((bf16[2,2,68,128]{3,2,1,0:T(8,128)(2,1)S(1)}, bf16[2,2,68,128]{3,2,1,0:T(8,128)(2,1)S(1)}, u32[]{:S(2)}, u32[]{:S(2)}) %collective-permute-start.3) | collective-permute-done | bytes 69664 | tf_op jit(solution)/shard_map/ppermute | solution.py:20
  21.9 0.3 pad_maximum_fusion.2
  22.4 0.9 fusion.1
  23.8 0.4 convolution_bitcast_fusion.2
  24.2 0.4 convolution_bitcast_fusion.1
  24.6 0.4 convolution_bitcast_fusion
  25.0 0.5 fusion.23
  25.5 0.7 fusion.7
  26.2 0.3 fusion.17
  26.5 0.4 convolution_bitcast_fusion.5
  26.9 0.4 convolution_bitcast_fusion.4
  27.3 0.4 convolution_bitcast_fusion.3
  27.8 0.4 fusion.15
  28.2 9.0 %collective-permute-start.4 = (f32[1152,128]{1,0:T(8,128)S(1)}, f32[1152,128]{1,0:T(8,128)S(1)}, u32[]{:S(2)}, u32[]{:S(2)}) collective-permute-start(f32[1152,128]{1,0:T(8,128)S(1)} %fusion.15), channel_id=1, source_target_pairs={{0,16},{16,0},{1,17},{17,1},{2,18},{18,2},{3,19},{19,3},{4,20},{20... | collective-permute-start | bytes 1769480 | tf_op jit(solution)/shard_map/ppermute | solution.py:108
  37.2 0.4 fusion.21
  37.6 0.4 convolution_add_fusion.1
  38.0 1.1 %fusion = bf16[16,64,128]{2,1,0:T(8,128)(2,1)} fusion(f32[16,64,128]{2,1,0:T(8,128)S(1)} %convolution_add_fusion.1, bf16[384,128,1]{1,0,2:T(8,128)(2,1)S(1)} %bitcast.67, bf16[18,64,128]{2,1,0:T(8,128)(2,1)S(1)} %get-tuple-element.27, bf16[18,64,128]{2,1,0:T(8,128)(2,1)S(1)} %get-tuple-element.28, bf16[18,64,128]{2,1,0:T(8,128)(2,1)S(1)} %get-tuple-element.26), kind=kOutput, calls=%fused_computation.6 | convolution fusion | flops 103579648 | bytes 1769472 | tf_op jit(solution)/shard_map/dot_general | solution.py:69
  39.1 0.3 fusion.14
  39.5 25.0 %all_to_all.15 = f32[32,36,128]{2,1,0:T(8,128)S(1)} all-to-all(f32[32,36,128]{2,1,0:T(8,128)S(1)} %reshape.39), channel_id=1, replica_groups=mesh['lon_chip'=16,'core'=2,'lat_z'=8,'lat_pair'=2] {'lon_chip','lat_pair'}, dimensions={0} | all-to-all | bytes 1179648 | tf_op jit(solution)/shard_map/all_to_all | solution.py:33
  64.6 17.2 %all_to_all.16 = f32[8,36,128]{2,1,0:T(8,128)S(1)} all-to-all(f32[8,36,128]{2,1,0:T(8,128)S(1)} %broadcast_in_dim.31), channel_id=1, replica_groups=mesh['lon_chip'=16,'core'=2,'lat_z'=8,'lat_pair'=2] {'lat_z'}, dimensions={0} | all-to-all | bytes 294912 | tf_op jit(solution)/shard_map/all_to_all | solution.py:39
  81.8 15.5 %all_to_all.17 = bf16[32,36,128]{2,1,0:T(8,128)(2,1)S(1)} all-to-all(bf16[32,36,128]{2,1,0:T(8,128)(2,1)S(1)} %broadcast_in_dim.32), channel_id=1, replica_groups=mesh['lon_chip'=16,'core'=2,'lat_z'=8,'lat_pair'=2] {'lon_chip','lat_pair'}, dimensions={0} | all-to-all | bytes 589824 | tf_op jit(solution)/shard_map/all_to_all | solution.py:39
  97.4 6.4 %collective-permute-start.5 = (bf16[1152,128]{1,0:T(8,128)(2,1)S(1)}, bf16[1152,128]{1,0:T(8,128)(2,1)S(1)}, u32[]{:S(2)}, u32[]{:S(2)}) collective-permute-start(bf16[1152,128]{1,0:T(8,128)(2,1)S(1)} %reshape.40), channel_id=1, source_target_pairs={{0,16},{16,0},{1,17},{17,1},{2,18},{18,2},{3,19},{19,3},{4,20},{20... | collective-permute-start | bytes 884744 | tf_op jit(solution)/shard_map/ppermute | solution.py:108
  103.9 1.0 collective-permute-done.5
  105.0 1.1 %fusion.22 = (f32[1,1152,128]{2,1,0:T(8,128)}, f32[1,1152,128]{2,1,0:T(8,128)}) fusion(f32[2,1152,128]{2,1,0:T(8,128)S(1)} %convert_dynamic-update-slice_fusion), kind=kLoop, calls=%fused_computation.56 | loop fusion | bytes 2359296 | tf_op jit(solution)/shard_map/slice | solution.py:126
  (31 shorter events, 2.2 us)
Async XLA Ops:
  0.6 13.7 %copy-start.2 = (bf16[3,3,128,128]{3,2,1,0:T(8,128)(2,1)S(1)}, bf16[3,3,128,128]{3,2,1,0:T(8,128)(2,1)}, u32[]{:S(2)}) copy-start(bf16[3,3,128,128]{3,2,1,0:T(8,128)(2,1)} %param.5) | copy-start | bytes 884740
  1.5 13.8 %collective-permute-start = (bf16[2,16,2,128]{3,2,1,0:T(2,128)(2,1)S(1)}, bf16[2,16,2,128]{3,2,1,0:T(2,128)(2,1)S(1)}, u32[]{:S(2)}, u32[]{:S(2)}) collective-permute-start(bf16[2,16,2,128]{3,2,1,0:T(2,128)(2,1)S(1)} %get-tuple-element.15), channel_id=1, source_target_pairs={{0,16},{16,32},{32,48},{48,64},{64,80},{80,96},{96,112},{112,128},... | collective-permute-start | bytes 49160 | tf_op jit(solution)/shard_map/ppermute | solution.py:17
  6.0 9.3 %collective-permute-start.1 = (bf16[2,16,2,128]{3,2,1,0:T(2,128)(2,1)S(1)}, bf16[2,16,2,128]{3,2,1,0:T(2,128)(2,1)S(1)}, u32[]{:S(2)}, u32[]{:S(2)}) collective-permute-start(bf16[2,16,2,128]{3,2,1,0:T(2,128)(2,1)S(1)} %get-tuple-element.16), channel_id=1, source_target_pairs={{16,0},{32,16},{48,32},{64,48},{80,64},{96,80},{112,96},{128,112},... | collective-permute-start | bytes 49160 | tf_op jit(solution)/shard_map/ppermute | solution.py:20
  13.2 2.2 %copy-start = (bf16[16,64,128]{2,1,0:T(8,128)(2,1)S(1)}, bf16[16,64,128]{2,1,0:T(8,128)(2,1)}, u32[]{:S(2)}) copy-start(bf16[16,64,128]{2,1,0:T(8,128)(2,1)} %param.4) | copy-start | bytes 786436
  13.2 2.2 %copy-start.1 = (bf16[16,64,128]{2,1,0:T(8,128)(2,1)S(1)}, bf16[16,64,128]{2,1,0:T(8,128)(2,1)}, u32[]{:S(2)}) copy-start(bf16[16,64,128]{2,1,0:T(8,128)(2,1)} %param.7) | copy-start | bytes 786436
  15.5 2.7 %collective-permute-start.2 = (bf16[2,2,68,128]{3,2,1,0:T(8,128)(2,1)S(1)}, bf16[2,2,68,128]{3,2,1,0:T(8,128)(2,1)S(1)}, u32[]{:S(2)}, u32[]{:S(2)}) collective-permute-start(bf16[2,2,68,128]{3,2,1,0:T(8,128)(2,1)S(1)} %get-tuple-element.13), channel_id=1, source_target_pairs={{0,1},{1,2},{2,3},{3,4},{4,5},{5,6},{6,7},{7,8},{8,9},{9,10},{10,1... | collective-permute-start | bytes 208904 | tf_op jit(solution)/shard_map/ppermute | solution.py:17
  16.8 5.1 %collective-permute-start.3 = (bf16[2,2,68,128]{3,2,1,0:T(8,128)(2,1)S(1)}, bf16[2,2,68,128]{3,2,1,0:T(8,128)(2,1)S(1)}, u32[]{:S(2)}, u32[]{:S(2)}) collective-permute-start(bf16[2,2,68,128]{3,2,1,0:T(8,128)(2,1)S(1)} %get-tuple-element.14), channel_id=1, source_target_pairs={{1,0},{2,1},{3,2},{4,3},{5,4},{6,5},{7,6},{8,7},{9,8},{10,9},{11,1... | collective-permute-start | bytes 208904 | tf_op jit(solution)/shard_map/ppermute | solution.py:20
  28.2 10.8 %collective-permute-start.4 = (f32[1152,128]{1,0:T(8,128)S(1)}, f32[1152,128]{1,0:T(8,128)S(1)}, u32[]{:S(2)}, u32[]{:S(2)}) collective-permute-start(f32[1152,128]{1,0:T(8,128)S(1)} %fusion.15), channel_id=1, source_target_pairs={{0,16},{16,0},{1,17},{17,1},{2,18},{18,2},{3,19},{19,3},{4,20},{20... | collective-permute-start | bytes 1769480 | tf_op jit(solution)/shard_map/ppermute | solution.py:108
  97.4 7.6 %collective-permute-start.5 = (bf16[1152,128]{1,0:T(8,128)(2,1)S(1)}, bf16[1152,128]{1,0:T(8,128)(2,1)S(1)}, u32[]{:S(2)}, u32[]{:S(2)}) collective-permute-start(bf16[1152,128]{1,0:T(8,128)(2,1)S(1)} %reshape.40), channel_id=1, source_target_pairs={{0,16},{16,0},{1,17},{17,1},{2,18},{18,2},{3,19},{19,3},{4,20},{20... | collective-permute-start | bytes 884744 | tf_op jit(solution)/shard_map/ppermute | solution.py:108

commit v15 on v14

--- a/solution.py
+++ b/solution.py
@@ -92,16 +92,18 @@
 def weight_terms(padded, gradient):
     rows_out, cols_out, channels = gradient.shape
     stacked = column_taps(padded, cols_out)
-    taps = [
-        lax.dot_general(
-            stacked[row_tap : row_tap + rows_out],
-            gradient,
-            (((0, 1), (0, 1)), ((), ())),
-            preferred_element_type=jnp.float32,
-        )
-        for row_tap in range(3)
-    ]
-    return jnp.stack(taps).reshape(3, 3, padded.shape[2], channels)
+    shifted = jnp.concatenate(
+        [jnp.pad(gradient, ((row_tap, 2 - row_tap), (0, 0), (0, 0))) for row_tap in range(3)],
+        axis=-1,
+    )
+    terms = lax.dot_general(
+        stacked, shifted, (((0, 1), (0, 1)), ((), ())), preferred_element_type=jnp.float32
+    )
+    return terms.reshape(-1, channels)
+
+
+def tap_order(terms, channels):
+    return jnp.transpose(terms.reshape(3, channels, 3, channels), (2, 0, 1, 3))
 
 
 def with_partner(x):
@@ -152,12 +154,10 @@
     )
     grad_pre = lax.optimization_barrier(grad_pre)
     term_in = weight_terms(input_use, grad_pre)
-    all_terms = jnp.concatenate(
-        [term_in.reshape(9 * channels, channels), term_out.reshape(9 * channels, channels)], axis=0
-    )
+    all_terms = jnp.concatenate([term_in, term_out], axis=0)
     decoded, grad_in, grad_out = reduced_everywhere(all_terms, decoded)
-    grad_in = grad_in.reshape(3, 3, channels, channels)
-    grad_out = grad_out.reshape(3, 3, channels, channels)
+    grad_in = tap_order(grad_in, channels)
+    grad_out = tap_order(grad_out, channels)
     return (decoded, grad_in, grad_out)
 
 

time: 106 us -> 109 us (1.028)
  local copies, waits for them, and re-layouts: 5.49 us -> 9.29 us
    unnamed x6 -> x17, local copies, waits for them, and re-layouts: 0.02 us -> 2.74 us
    dot_general x6 -> x2, matrix products: 2.42 us -> 1.36 us  [weight_terms(): lax.dot_general(stacked, shifted, (((0, 1), (0, 1)), ((), ())), preferred...]
  transfers between devices with their start and end apart: 6 -> 6, of which waited for: 3 -> 3; matrix products, arithmetic and copies ran while one was open for 5% -> 6% of each run, Pallas kernels for 0% -> 0%
where the time goes in v15:
time: 109 us; the launch traced here: 108 us
  blocking collectives  58.2 us (53%)
  starting transfers between devices  28.4 us (26%)
  local copies, waits for them, and re-layouts  9.29 us (9%)
  matrix products  4.81 us (4%)
  waiting for transfers between devices  4.77 us (4%)
  other arithmetic  1.87 us (2%)
    all_to_all x2, blocking collectives, sent_to_all(): return lax.all_to_all(copies, axis, split_axis=0, concat_axis=0, tiled=True)  33.4 us
    all_to_all x1, blocking collectives, sent_and_summed(): lax.all_to_all(blocks, axis, split_axis=0, concat_axis=0, tiled=True)  24.7 us
    ppermute x2, starting transfers between devices, with_partner(): return lax.ppermute(x, 'core', [(0, 1), (1, 0)])  15.2 us
    ppermute x2, starting transfers between devices, with_halo(): lax.ppermute(lax.slice_in_dim(block, 0, width, axis=dim), axis, backward)  7.46 us
    ppermute x2, starting transfers between devices, with_halo(): lax.ppermute(lax.slice_in_dim(block, block.shape[dim] - width, None, axis...  5.79 us
    ppermute x2, waiting for transfers between devices, with_halo(): lax.ppermute(lax.slice_in_dim(block, 0, width, axis=dim), axis, backward)  3.71 us
    unnamed x17, local copies, waits for them, and re-layouts  2.74 us
  transfers between devices with their start and end apart: 6, of which 3 were waited for; matrix products, arithmetic and copies ran while one was open for 6% of the time, Pallas kernels for 0%

profile of v15, /device:TPU:1, one launch (start us, length us, event | category | flops | bytes accessed | tf_op | source)
XLA Modules:
  0.0 108.3 jit_solution(5623478946415432294)
XLA Ops:
  0.6 0.9 pad_maximum_fusion.7
  1.5 4.5 %collective-permute-start = (bf16[2,16,2,128]{3,2,1,0:T(2,128)(2,1)S(1)}, bf16[2,16,2,128]{3,2,1,0:T(2,128)(2,1)S(1)}, u32[]{:S(2)}, u32[]{:S(2)}) collective-permute-start(bf16[2,16,2,128]{3,2,1,0:T(2,128)(2,1)S(1)} %get-tuple-element.24), channel_id=1, source_target_pairs={{0,16},{16,32},{32,48},{48,64},{64,80},{80,96},{96,112},{112,128},... | collective-permute-start | bytes 49160 | tf_op jit(solution)/shard_map/ppermute | solution.py:17
  6.0 6.2 %collective-permute-start.1 = (bf16[2,16,2,128]{3,2,1,0:T(2,128)(2,1)S(1)}, bf16[2,16,2,128]{3,2,1,0:T(2,128)(2,1)S(1)}, u32[]{:S(2)}, u32[]{:S(2)}) collective-permute-start(bf16[2,16,2,128]{3,2,1,0:T(2,128)(2,1)S(1)} %get-tuple-element.25), channel_id=1, source_target_pairs={{16,0},{32,16},{48,32},{64,48},{80,64},{96,80},{112,96},{128,112},... | collective-permute-start | bytes 49160 | tf_op jit(solution)/shard_map/ppermute | solution.py:20
  12.2 1.7 %fusion.66 = (bf16[1,3,128,128]{3,2,1,0:T(8,128)(2,1)}, bf16[1,3,128,128]{3,2,1,0:T(8,128)(2,1)}, bf16[1,3,128,128]{3,2,1,0:T(8,128)(2,1)}) fusion(bf16[3,3,128,128]{3,2,1,0:T(8,128)(2,1)} %param.6), kind=kLoop, calls=%fused_computation.91 | loop fusion | bytes 589824 | tf_op jit(solution)/shard_map/slice | solution.py:71
  13.9 1.0 reverse_bitcast_fusion
  15.0 0.3 copy.16
  15.2 0.3 reshape.52
  15.8 1.0 reshape.51
  16.8 1.3 %collective-permute-start.2 = (bf16[2,2,68,128]{3,2,1,0:T(8,128)(2,1)S(1)}, bf16[2,2,68,128]{3,2,1,0:T(8,128)(2,1)S(1)}, u32[]{:S(2)}, u32[]{:S(2)}) collective-permute-start(bf16[2,2,68,128]{3,2,1,0:T(8,128)(2,1)S(1)} %get-tuple-element.22), channel_id=1, source_target_pairs={{0,1},{1,2},{2,3},{3,4},{4,5},{5,6},{6,7},{7,8},{8,9},{9,10},{10,1... | collective-permute-start | bytes 208904 | tf_op jit(solution)/shard_map/ppermute | solution.py:17
  18.1 1.3 %collective-permute-start.3 = (bf16[2,2,68,128]{3,2,1,0:T(8,128)(2,1)S(1)}, bf16[2,2,68,128]{3,2,1,0:T(8,128)(2,1)S(1)}, u32[]{:S(2)}, u32[]{:S(2)}) collective-permute-start(bf16[2,2,68,128]{3,2,1,0:T(8,128)(2,1)S(1)} %get-tuple-element.23), channel_id=1, source_target_pairs={{1,0},{2,1},{3,2},{4,3},{5,4},{6,5},{7,6},{8,7},{9,8},{10,9},{11,1... | collective-permute-start | bytes 208904 | tf_op jit(solution)/shard_map/ppermute | solution.py:20
  19.5 3.7 %collective-permute-done.3 = bf16[2,2,68,128]{3,2,1,0:T(8,128)(2,1)S(1)} collective-permute-done((bf16[2,2,68,128]{3,2,1,0:T(8,128)(2,1)S(1)}, bf16[2,2,68,128]{3,2,1,0:T(8,128)(2,1)S(1)}, u32[]{:S(2)}, u32[]{:S(2)}) %collective-permute-start.3) | collective-permute-done | bytes 69664 | tf_op jit(solution)/shard_map/ppermute | solution.py:20
  23.2 0.3 pad_maximum_fusion.1
  23.8 0.9 fusion.8
  25.2 0.7 convolution_bitcast_fusion
  25.9 0.5 fusion.62
  26.4 0.4 copy-done.3
  26.9 0.7 fusion.39
  27.6 0.3 fusion.46
  27.8 0.7 convolution_bitcast_fusion.1
  28.7 9.0 %collective-permute-start.4 = (f32[1152,128]{1,0:T(8,128)S(1)}, f32[1152,128]{1,0:T(8,128)S(1)}, u32[]{:S(2)}, u32[]{:S(2)}) collective-permute-start(f32[1152,128]{1,0:T(8,128)S(1)} %constant_dynamic-slice_fusion), channel_id=1, source_target_pairs={{0,16},{16,0},{1,17},{17,1},{2,18},{18,2},{3,19},{19,3},{4,20},{20... | collective-permute-start | bytes 1769480 | tf_op jit(solution)/shard_map/ppermute | solution.py:110
  37.8 0.4 fusion.60
  38.2 0.4 convolution_add_fusion.1
  38.5 0.5 copy-done.4
  39.0 1.1 fusion.7
  40.2 24.7 %all_to_all.15 = f32[32,36,128]{2,1,0:T(8,128)S(1)} all-to-all(f32[32,36,128]{2,1,0:T(8,128)S(1)} %reshape.47), channel_id=1, replica_groups=mesh['lon_chip'=16,'core'=2,'lat_z'=8,'lat_pair'=2] {'lon_chip','lat_pair'}, dimensions={0} | all-to-all | bytes 1179648 | tf_op jit(solution)/shard_map/all_to_all | solution.py:33
  65.0 17.5 %all_to_all.16 = f32[8,36,128]{2,1,0:T(8,128)S(1)} all-to-all(f32[8,36,128]{2,1,0:T(8,128)S(1)} %broadcast_in_dim.31), channel_id=1, replica_groups=mesh['lon_chip'=16,'core'=2,'lat_z'=8,'lat_pair'=2] {'lat_z'}, dimensions={0} | all-to-all | bytes 294912 | tf_op jit(solution)/shard_map/all_to_all | solution.py:39
  82.6 16.0 %all_to_all.17 = bf16[32,36,128]{2,1,0:T(8,128)(2,1)S(1)} all-to-all(bf16[32,36,128]{2,1,0:T(8,128)(2,1)S(1)} %broadcast_in_dim.32), channel_id=1, replica_groups=mesh['lon_chip'=16,'core'=2,'lat_z'=8,'lat_pair'=2] {'lon_chip','lat_pair'}, dimensions={0} | all-to-all | bytes 589824 | tf_op jit(solution)/shard_map/all_to_all | solution.py:39
  98.6 6.2 %collective-permute-start.5 = (bf16[1152,128]{1,0:T(8,128)(2,1)S(1)}, bf16[1152,128]{1,0:T(8,128)(2,1)S(1)}, u32[]{:S(2)}, u32[]{:S(2)}) collective-permute-start(bf16[1152,128]{1,0:T(8,128)(2,1)S(1)} %reshape.48), channel_id=1, source_target_pairs={{0,16},{16,0},{1,17},{17,1},{2,18},{18,2},{3,19},{19,3},{4,20},{20... | collective-permute-start | bytes 884744 | tf_op jit(solution)/shard_map/ppermute | solution.py:110
  105.0 1.0 collective-permute-done.5
  106.1 0.3 reshape_squeeze.18
  106.4 0.9 copy.18
  107.5 0.9 copy.19
  (41 shorter events, 2.2 us)
Async XLA Ops:
  0.6 14.3 %copy-start.2 = (bf16[3,3,128,128]{3,2,1,0:T(8,128)(2,1)S(1)}, bf16[3,3,128,128]{3,2,1,0:T(8,128)(2,1)}, u32[]{:S(2)}) copy-start(bf16[3,3,128,128]{3,2,1,0:T(8,128)(2,1)} %param.5) | copy-start | bytes 884740
  1.5 15.2 %collective-permute-start = (bf16[2,16,2,128]{3,2,1,0:T(2,128)(2,1)S(1)}, bf16[2,16,2,128]{3,2,1,0:T(2,128)(2,1)S(1)}, u32[]{:S(2)}, u32[]{:S(2)}) collective-permute-start(bf16[2,16,2,128]{3,2,1,0:T(2,128)(2,1)S(1)} %get-tuple-element.24), channel_id=1, source_target_pairs={{0,16},{16,32},{32,48},{48,64},{64,80},{80,96},{96,112},{112,128},... | collective-permute-start | bytes 49160 | tf_op jit(solution)/shard_map/ppermute | solution.py:17
  6.0 10.7 %collective-permute-start.1 = (bf16[2,16,2,128]{3,2,1,0:T(2,128)(2,1)S(1)}, bf16[2,16,2,128]{3,2,1,0:T(2,128)(2,1)S(1)}, u32[]{:S(2)}, u32[]{:S(2)}) collective-permute-start(bf16[2,16,2,128]{3,2,1,0:T(2,128)(2,1)S(1)} %get-tuple-element.25), channel_id=1, source_target_pairs={{16,0},{32,16},{48,32},{64,48},{80,64},{96,80},{112,96},{128,112},... | collective-permute-start | bytes 49160 | tf_op jit(solution)/shard_map/ppermute | solution.py:20
  13.9 2.8 %copy-start = (bf16[16,64,128]{2,1,0:T(8,128)(2,1)S(1)}, bf16[16,64,128]{2,1,0:T(8,128)(2,1)}, u32[]{:S(2)}) copy-start(bf16[16,64,128]{2,1,0:T(8,128)(2,1)} %param.4) | copy-start | bytes 786436
  13.9 2.8 %copy-start.1 = (bf16[16,64,128]{2,1,0:T(8,128)(2,1)S(1)}, bf16[16,64,128]{2,1,0:T(8,128)(2,1)}, u32[]{:S(2)}) copy-start(bf16[16,64,128]{2,1,0:T(8,128)(2,1)} %param.7) | copy-start | bytes 786436
  16.8 2.7 %collective-permute-start.2 = (bf16[2,2,68,128]{3,2,1,0:T(8,128)(2,1)S(1)}, bf16[2,2,68,128]{3,2,1,0:T(8,128)(2,1)S(1)}, u32[]{:S(2)}, u32[]{:S(2)}) collective-permute-start(bf16[2,2,68,128]{3,2,1,0:T(8,128)(2,1)S(1)} %get-tuple-element.22), channel_id=1, source_target_pairs={{0,1},{1,2},{2,3},{3,4},{4,5},{5,6},{6,7},{7,8},{8,9},{9,10},{10,1... | collective-permute-start | bytes 208904 | tf_op jit(solution)/shard_map/ppermute | solution.py:17
  18.1 5.1 %collective-permute-start.3 = (bf16[2,2,68,128]{3,2,1,0:T(8,128)(2,1)S(1)}, bf16[2,2,68,128]{3,2,1,0:T(8,128)(2,1)S(1)}, u32[]{:S(2)}, u32[]{:S(2)}) collective-permute-start(bf16[2,2,68,128]{3,2,1,0:T(8,128)(2,1)S(1)} %get-tuple-element.23), channel_id=1, source_target_pairs={{1,0},{2,1},{3,2},{4,3},{5,4},{6,5},{7,6},{8,7},{9,8},{10,9},{11,1... | collective-permute-start | bytes 208904 | tf_op jit(solution)/shard_map/ppermute | solution.py:20
  25.9 1.0 copy-start.3
  28.6 9.2 %copy-start.6 = (bf16[1,3,128,128]{3,2,1,0:T(8,128)(2,1)S(1)}, bf16[1,3,128,128]{3,2,1,0:T(8,128)(2,1)}, u32[]{:S(2)}) copy-start(bf16[1,3,128,128]{3,2,1,0:T(8,128)(2,1)} %get-tuple-element.39) | copy-start | bytes 294916
  28.7 9.5 %copy-start.5 = (bf16[1,3,128,128]{3,2,1,0:T(8,128)(2,1)S(1)}, bf16[1,3,128,128]{3,2,1,0:T(8,128)(2,1)}, u32[]{:S(2)}) copy-start(bf16[1,3,128,128]{3,2,1,0:T(8,128)(2,1)} %get-tuple-element.40) | copy-start | bytes 294916
  28.7 11.4 %collective-permute-start.4 = (f32[1152,128]{1,0:T(8,128)S(1)}, f32[1152,128]{1,0:T(8,128)S(1)}, u32[]{:S(2)}, u32[]{:S(2)}) collective-permute-start(f32[1152,128]{1,0:T(8,128)S(1)} %constant_dynamic-slice_fusion), channel_id=1, source_target_pairs={{0,16},{16,0},{1,17},{17,1},{2,18},{18,2},{3,19},{19,3},{4,20},{20... | collective-permute-start | bytes 1769480 | tf_op jit(solution)/shard_map/ppermute | solution.py:110
  38.1 0.9 copy-start.4
  98.6 7.3 %collective-permute-start.5 = (bf16[1152,128]{1,0:T(8,128)(2,1)S(1)}, bf16[1152,128]{1,0:T(8,128)(2,1)S(1)}, u32[]{:S(2)}, u32[]{:S(2)}) collective-permute-start(bf16[1152,128]{1,0:T(8,128)(2,1)S(1)} %reshape.48), channel_id=1, source_target_pairs={{0,16},{16,0},{1,17},{17,1},{2,18},{18,2},{3,19},{19,3},{4,20},{20... | collective-permute-start | bytes 884744 | tf_op jit(solution)/shard_map/ppermute | solution.py:110

commit v16 on v14

--- a/solution.py
+++ b/solution.py
@@ -75,13 +75,18 @@
     return summed
 
 
-def merged_conv(padded, weights):
+def merged_conv(padded, weights, local=None, edge=0):
     rows_out = padded.shape[0] - 2
     cols_out = padded.shape[1] - 2
     channels, width = weights.shape[2], weights.shape[3]
-    stacked = column_taps(padded, cols_out)
     merged = jnp.transpose(weights, (1, 2, 0, 3)).reshape(3 * channels, 3 * width)
-    spread = jnp.dot(stacked, merged, preferred_element_type=jnp.float32)
+    if local is None:
+        spread = jnp.dot(column_taps(padded, cols_out), merged, preferred_element_type=jnp.float32)
+    else:
+        inner = jnp.dot(column_taps(local, cols_out), merged, preferred_element_type=jnp.float32)
+        rims = jnp.concatenate([padded[:edge], padded[padded.shape[0] - edge :]], axis=0)
+        outer = jnp.dot(column_taps(rims, cols_out), merged, preferred_element_type=jnp.float32)
+        spread = jnp.concatenate([outer[:edge], inner, outer[edge:]], axis=0)
     summed = None
     for row_tap in range(3):
         part = spread[row_tap : row_tap + rows_out, :, row_tap * width : (row_tap + 1) * width]
@@ -135,7 +140,7 @@
     extended = with_halo(widened, ((LAT, 1),), margin, False)
     input_pad = extended[0]
     grad_pad = extended[1][1:-1, 1:-1]
-    preact_wide = merged_conv(input_pad, weights_in)
+    preact_wide = merged_conv(input_pad, weights_in, widened[0], margin)
     hidden_wide = jax.nn.silu(preact_wide).astype(jnp.bfloat16)
     global_row = lax.axis_index(LAT) * tile_rows - 1 + jnp.arange(tile_rows + 2, dtype=jnp.int32)
     inside = (global_row >= 0) & (global_row < tile_rows * lax.axis_size(LAT))
@@ -145,7 +150,7 @@
     decoded = conv_tile(hidden_pad, weights_out).astype(jnp.bfloat16)
     term_out = weight_terms(hidden_pad, cotangent)
     flipped = jnp.transpose(weights_out[::-1, ::-1], (0, 1, 3, 2))
-    grad_hidden = merged_conv(grad_pad, flipped)
+    grad_hidden = merged_conv(grad_pad, flipped, widened[1][:, 1:-1], margin - 1)
     sigmoid_pre = jax.nn.sigmoid(preact)
     grad_pre = (grad_hidden * (sigmoid_pre * (1.0 + preact * (1.0 - sigmoid_pre)))).astype(
         jnp.bfloat16

time: 106 us -> 104 us (0.981)
  waiting for transfers between devices: 4.77 us -> 1 us
  starting transfers between devices: 28.6 us -> 30.6 us
    ppermute x2, waiting for transfers between devices: 3.71 us -> 0.01 us  [with_halo(): lax.ppermute(lax.slice_in_dim(block, 0, width, axis=dim), axis, backward)]
    ppermute x2, starting transfers between devices: 5.79 us -> 8.49 us  [with_halo(): lax.ppermute(lax.slice_in_dim(block, block.shape[dim] - width, None, axis...]
  transfers between devices with their start and end apart: 6 -> 6, of which waited for: 3 -> 1; matrix products, arithmetic and copies ran while one was open for 5% -> 7% of each run, Pallas kernels for 0% -> 0%
where the time goes in v16:
time: 104 us
  blocking collectives  56.7 us (55%)
  starting transfers between devices  30.6 us (29%)
  matrix products  6.18 us (6%)
  local copies, waits for them, and re-layouts  5.48 us (5%)
  other arithmetic  2.93 us (3%)
  between operations  1.1 us (1%)
    all_to_all x2, blocking collectives, sent_to_all(): return lax.all_to_all(copies, axis, split_axis=0, concat_axis=0, tiled=True)  32.6 us
    all_to_all x1, blocking collectives, sent_and_summed(): lax.all_to_all(blocks, axis, split_axis=0, concat_axis=0, tiled=True)  24.1 us
    ppermute x2, starting transfers between devices, with_partner(): return lax.ppermute(x, 'core', [(0, 1), (1, 0)])  14.6 us
    ppermute x2, starting transfers between devices, with_halo(): lax.ppermute(lax.slice_in_dim(block, block.shape[dim] - width, None, axis...  8.49 us
    ppermute x2, starting transfers between devices, with_halo(): lax.ppermute(lax.slice_in_dim(block, 0, width, axis=dim), axis, backward)  7.46 us
    dot_general x6, matrix products, weight_terms(): lax.dot_general(stacked[row_tap:row_tap + rows_out], gradient, (((0, 1),...  2.44 us
  transfers between devices with their start and end apart: 6, of which 1 were waited for; matrix products, arithmetic and copies ran while one was open for 7% of the time, Pallas kernels for 0%

profile of v16, /device:TPU:1, one launch (start us, length us, event | category | flops | bytes accessed | tf_op | source)
XLA Modules:
  0.0 104.0 jit_solution(6495970967870283520)
XLA Ops:
  0.6 0.9 pad_maximum_fusion.17
  1.5 4.5 %collective-permute-start = (bf16[2,16,2,128]{3,2,1,0:T(2,128)(2,1)S(1)}, bf16[2,16,2,128]{3,2,1,0:T(2,128)(2,1)S(1)}, u32[]{:S(2)}, u32[]{:S(2)}) collective-permute-start(bf16[2,16,2,128]{3,2,1,0:T(2,128)(2,1)S(1)} %get-tuple-element.17), channel_id=1, source_target_pairs={{0,16},{16,32},{32,48},{48,64},{64,80},{80,96},{96,112},{112,128},... | collective-permute-start | bytes 49160 | tf_op jit(solution)/shard_map/ppermute | solution.py:17
  6.0 6.2 %collective-permute-start.1 = (bf16[2,16,2,128]{3,2,1,0:T(2,128)(2,1)S(1)}, bf16[2,16,2,128]{3,2,1,0:T(2,128)(2,1)S(1)}, u32[]{:S(2)}, u32[]{:S(2)}) collective-permute-start(bf16[2,16,2,128]{3,2,1,0:T(2,128)(2,1)S(1)} %get-tuple-element.18), channel_id=1, source_target_pairs={{16,0},{32,16},{48,32},{64,48},{80,64},{96,80},{112,96},{128,112},... | collective-permute-start | bytes 49160 | tf_op jit(solution)/shard_map/ppermute | solution.py:20
  12.2 1.0 fusion.51
  13.3 1.0 reverse_bitcast_fusion
  14.3 0.3 copy.12
  15.5 1.3 %collective-permute-start.3 = (bf16[2,2,68,128]{3,2,1,0:T(8,128)(2,1)S(1)}, bf16[2,2,68,128]{3,2,1,0:T(8,128)(2,1)S(1)}, u32[]{:S(2)}, u32[]{:S(2)}) collective-permute-start(bf16[2,2,68,128]{3,2,1,0:T(8,128)(2,1)S(1)} %get-tuple-element.16), channel_id=1, source_target_pairs={{1,0},{2,1},{3,2},{4,3},{5,4},{6,5},{7,6},{8,7},{9,8},{10,9},{11,1... | collective-permute-start | bytes 208904 | tf_op jit(solution)/shard_map/ppermute | solution.py:20
  16.8 4.0 %collective-permute-start.2 = (bf16[2,2,68,128]{3,2,1,0:T(8,128)(2,1)S(1)}, bf16[2,2,68,128]{3,2,1,0:T(8,128)(2,1)S(1)}, u32[]{:S(2)}, u32[]{:S(2)}) collective-permute-start(bf16[2,2,68,128]{3,2,1,0:T(8,128)(2,1)S(1)} %get-tuple-element.15), channel_id=1, source_target_pairs={{0,1},{1,2},{2,3},{3,4},{4,5},{5,6},{6,7},{7,8},{8,9},{9,10},{10,1... | collective-permute-start | bytes 208904 | tf_op jit(solution)/shard_map/ppermute | solution.py:17
  20.8 0.3 pad_maximum_fusion.7
  21.5 0.8 fusion.1
  22.3 0.6 fusion.7
  23.0 0.3 fusion.23
  23.4 0.3 fusion.21
  23.9 0.4 convolution_bitcast_fusion.2
  24.3 0.4 convolution_bitcast_fusion.1
  24.7 0.4 convolution_bitcast_fusion
  25.1 0.3 pad_maximum_fusion.2
  26.2 0.4 convolution_bitcast_fusion.5
  26.6 0.4 convolution_bitcast_fusion.4
  27.0 0.4 convolution_bitcast_fusion.3
  27.5 0.4 fusion.17
  27.9 8.4 %collective-permute-start.4 = (f32[1152,128]{1,0:T(8,128)S(1)}, f32[1152,128]{1,0:T(8,128)S(1)}, u32[]{:S(2)}, u32[]{:S(2)}) collective-permute-start(f32[1152,128]{1,0:T(8,128)S(1)} %fusion.17), channel_id=1, source_target_pairs={{0,16},{16,0},{1,17},{17,1},{2,18},{18,2},{3,19},{19,3},{4,20},{20... | collective-permute-start | bytes 1769480 | tf_op jit(solution)/shard_map/ppermute | solution.py:113
  36.3 0.4 fusion.44
  36.7 0.4 convolution_add_fusion.1
  37.0 1.1 %fusion = bf16[16,64,128]{2,1,0:T(8,128)(2,1)} fusion(f32[16,64,128]{2,1,0:T(8,128)S(1)} %convolution_add_fusion.1, bf16[384,128,1]{1,0,2:T(8,128)(2,1)S(1)} %bitcast.79, bf16[18,64,128]{2,1,0:T(8,128)(2,1)S(1)} %get-tuple-element.27, bf16[18,64,128]{2,1,0:T(8,128)(2,1)S(1)} %get-tuple-element.28, bf16[18,64,128]{2,1,0:T(8,128)(2,1)S(1)} %get-tuple-element.26), kind=kOutput, calls=%fused_computation.6 | convolution fusion | flops 103579648 | bytes 1769472 | tf_op jit(solution)/shard_map/dot_general | solution.py:69
  38.1 0.3 fusion.16
  38.5 24.1 %all_to_all.15 = f32[32,36,128]{2,1,0:T(8,128)S(1)} all-to-all(f32[32,36,128]{2,1,0:T(8,128)S(1)} %reshape.41), channel_id=1, replica_groups=mesh['lon_chip'=16,'core'=2,'lat_z'=8,'lat_pair'=2] {'lon_chip','lat_pair'}, dimensions={0} | all-to-all | bytes 1179648 | tf_op jit(solution)/shard_map/all_to_all | solution.py:33
  62.7 17.1 %all_to_all.16 = f32[8,36,128]{2,1,0:T(8,128)S(1)} all-to-all(f32[8,36,128]{2,1,0:T(8,128)S(1)} %broadcast_in_dim.31), channel_id=1, replica_groups=mesh['lon_chip'=16,'core'=2,'lat_z'=8,'lat_pair'=2] {'lat_z'}, dimensions={0} | all-to-all | bytes 294912 | tf_op jit(solution)/shard_map/all_to_all | solution.py:39
  79.8 15.6 %all_to_all.17 = bf16[32,36,128]{2,1,0:T(8,128)(2,1)S(1)} all-to-all(bf16[32,36,128]{2,1,0:T(8,128)(2,1)S(1)} %broadcast_in_dim.32), channel_id=1, replica_groups=mesh['lon_chip'=16,'core'=2,'lat_z'=8,'lat_pair'=2] {'lon_chip','lat_pair'}, dimensions={0} | all-to-all | bytes 589824 | tf_op jit(solution)/shard_map/all_to_all | solution.py:39
  95.4 6.2 %collective-permute-start.5 = (bf16[1152,128]{1,0:T(8,128)(2,1)S(1)}, bf16[1152,128]{1,0:T(8,128)(2,1)S(1)}, u32[]{:S(2)}, u32[]{:S(2)}) collective-permute-start(bf16[1152,128]{1,0:T(8,128)(2,1)S(1)} %reshape.42), channel_id=1, source_target_pairs={{0,16},{16,0},{1,17},{17,1},{2,18},{18,2},{3,19},{19,3},{4,20},{20... | collective-permute-start | bytes 884744 | tf_op jit(solution)/shard_map/ppermute | solution.py:113
  101.8 1.0 collective-permute-done.5
  102.9 1.1 %fusion.46 = (f32[1,1152,128]{2,1,0:T(8,128)}, f32[1,1152,128]{2,1,0:T(8,128)}) fusion(f32[2,1152,128]{2,1,0:T(8,128)S(1)} %convert_dynamic-update-slice_fusion), kind=kLoop, calls=%fused_computation.93 | loop fusion | bytes 2359296 | tf_op jit(solution)/shard_map/slice | solution.py:131
  (43 shorter events, 2.9 us)
Async XLA Ops:
  0.6 13.7 %copy-start.2 = (bf16[3,3,128,128]{3,2,1,0:T(8,128)(2,1)S(1)}, bf16[3,3,128,128]{3,2,1,0:T(8,128)(2,1)}, u32[]{:S(2)}) copy-start(bf16[3,3,128,128]{3,2,1,0:T(8,128)(2,1)} %param.5) | copy-start | bytes 884740
  1.5 13.8 %collective-permute-start = (bf16[2,16,2,128]{3,2,1,0:T(2,128)(2,1)S(1)}, bf16[2,16,2,128]{3,2,1,0:T(2,128)(2,1)S(1)}, u32[]{:S(2)}, u32[]{:S(2)}) collective-permute-start(bf16[2,16,2,128]{3,2,1,0:T(2,128)(2,1)S(1)} %get-tuple-element.17), channel_id=1, source_target_pairs={{0,16},{16,32},{32,48},{48,64},{64,80},{80,96},{96,112},{112,128},... | collective-permute-start | bytes 49160 | tf_op jit(solution)/shard_map/ppermute | solution.py:17
  6.0 9.4 %collective-permute-start.1 = (bf16[2,16,2,128]{3,2,1,0:T(2,128)(2,1)S(1)}, bf16[2,16,2,128]{3,2,1,0:T(2,128)(2,1)S(1)}, u32[]{:S(2)}, u32[]{:S(2)}) collective-permute-start(bf16[2,16,2,128]{3,2,1,0:T(2,128)(2,1)S(1)} %get-tuple-element.18), channel_id=1, source_target_pairs={{16,0},{32,16},{48,32},{64,48},{80,64},{96,80},{112,96},{128,112},... | collective-permute-start | bytes 49160 | tf_op jit(solution)/shard_map/ppermute | solution.py:20
  13.2 2.2 %copy-start = (bf16[16,64,128]{2,1,0:T(8,128)(2,1)S(1)}, bf16[16,64,128]{2,1,0:T(8,128)(2,1)}, u32[]{:S(2)}) copy-start(bf16[16,64,128]{2,1,0:T(8,128)(2,1)} %param.7) | copy-start | bytes 786436
  13.2 2.2 %copy-start.1 = (bf16[16,64,128]{2,1,0:T(8,128)(2,1)S(1)}, bf16[16,64,128]{2,1,0:T(8,128)(2,1)}, u32[]{:S(2)}) copy-start(bf16[16,64,128]{2,1,0:T(8,128)(2,1)} %param.4) | copy-start | bytes 786436
  15.5 7.5 %collective-permute-start.3 = (bf16[2,2,68,128]{3,2,1,0:T(8,128)(2,1)S(1)}, bf16[2,2,68,128]{3,2,1,0:T(8,128)(2,1)S(1)}, u32[]{:S(2)}, u32[]{:S(2)}) collective-permute-start(bf16[2,2,68,128]{3,2,1,0:T(8,128)(2,1)S(1)} %get-tuple-element.16), channel_id=1, source_target_pairs={{1,0},{2,1},{3,2},{4,3},{5,4},{6,5},{7,6},{8,7},{9,8},{10,9},{11,1... | collective-permute-start | bytes 208904 | tf_op jit(solution)/shard_map/ppermute | solution.py:20
  16.8 6.2 %collective-permute-start.2 = (bf16[2,2,68,128]{3,2,1,0:T(8,128)(2,1)S(1)}, bf16[2,2,68,128]{3,2,1,0:T(8,128)(2,1)S(1)}, u32[]{:S(2)}, u32[]{:S(2)}) collective-permute-start(bf16[2,2,68,128]{3,2,1,0:T(8,128)(2,1)S(1)} %get-tuple-element.15), channel_id=1, source_target_pairs={{0,1},{1,2},{2,3},{3,4},{4,5},{5,6},{6,7},{7,8},{8,9},{9,10},{10,1... | collective-permute-start | bytes 208904 | tf_op jit(solution)/shard_map/ppermute | solution.py:17
  27.9 10.3 %collective-permute-start.4 = (f32[1152,128]{1,0:T(8,128)S(1)}, f32[1152,128]{1,0:T(8,128)S(1)}, u32[]{:S(2)}, u32[]{:S(2)}) collective-permute-start(f32[1152,128]{1,0:T(8,128)S(1)} %fusion.17), channel_id=1, source_target_pairs={{0,16},{16,0},{1,17},{17,1},{2,18},{18,2},{3,19},{19,3},{4,20},{20... | collective-permute-start | bytes 1769480 | tf_op jit(solution)/shard_map/ppermute | solution.py:113
  95.4 7.4 %collective-permute-start.5 = (bf16[1152,128]{1,0:T(8,128)(2,1)S(1)}, bf16[1152,128]{1,0:T(8,128)(2,1)S(1)}, u32[]{:S(2)}, u32[]{:S(2)}) collective-permute-start(bf16[1152,128]{1,0:T(8,128)(2,1)S(1)} %reshape.42), channel_id=1, source_target_pairs={{0,16},{16,0},{1,17},{17,1},{2,18},{18,2},{3,19},{19,3},{4,20},{20... | collective-permute-start | bytes 884744 | tf_op jit(solution)/shard_map/ppermute | solution.py:113
